TPU v7x, 128 devices: a whole 4x4x4 slice. The times are simulated.
128 devices in a mesh: seq: 16 (over x, z), chan: 8 (over y, core).
Axes of the slice: x: 4, y: 4, z: 4, core: 2. Of those that a mesh axis runs over, the one named last changes fastest.
Arguments:
- inputs: bfloat16 [32768, 1024], P('seq'), may hold values from -88 to 88
- gaps: float32 [32768], P('seq'), as said below
- rates: float32 [4096], P('chan'), as said below
- w_in: bfloat16 [1024, 4096], P(None, 'chan'), may hold values from -0.25 to 0.25
- w_out: bfloat16 [4096, 1024], P('chan'), may hold values from -0.09375 to 0.09375
- cotangent: bfloat16 [32768, 1024], P('seq'), may hold values from -48 to 48
Outputs:
- d_inputs: bfloat16 [32768, 1024], P('seq', 'chan')
- d_w_in: float32 [1024, 4096], P('seq', 'chan')
- d_w_out: float32 [4096, 1024], P('chan', 'seq')
Inputs may be any that keep to these rules, and one draw needn't show every extreme that they name: `gaps`: every gap is positive; at a few positions of the whole log drawn from the seed the gap is a sizable fraction of 32768. `rates`: every rate is positive.
All inputs are finite; a program needn't handle non-finite values.
Results may differ from a plain program's by a relative error of at most 0.02.
Values may be sent and summed in bfloat16 or wider, within the bound.
No kernel may reach another device: no remote copies, remote signals or barrier semaphores. Data moves between devices by JAX's collectives and lax.ppermute only.
A program may use at most 128 MiB of HBM per device.

v0:
```python
import math

import jax
import jax.numpy as jnp
from jax import lax
from jax.experimental import pallas as pl
from jax.experimental.pallas import tpu as pltpu
from jax.sharding import PartitionSpec as P

SEGMENTS = 8
LANES = 128
UNROLL = 8


def _summary_kernel(g_ref, gn_ref, r_ref, *refs):
    chunks = (len(refs) - 4) // 2
    drive_refs = refs[:chunks]
    up_refs = refs[chunks:2 * chunks]
    fa_ref, fb_ref, ba_ref, bb_ref = refs[2 * chunks:]
    steps, segs, _ = g_ref.shape
    rs = [r_ref[:, pl.ds(k * LANES, LANES)] for k in range(chunks)]
    ones = tuple(jnp.ones((segs, LANES), jnp.float32) for _ in range(chunks))
    zeros = tuple(jnp.zeros((segs, LANES), jnp.float32) for _ in range(chunks))

    def fwd(i, carry):
        a, b = carry
        g = g_ref[i]
        new_a, new_b = [], []
        for k in range(chunks):
            d = jnp.exp(-(g * rs[k]))
            x = drive_refs[k][pl.ds(i, segs, stride=steps), :]
            new_a.append(a[k] * d)
            new_b.append(d * b[k] + x)
        return (tuple(new_a), tuple(new_b))

    a, b = lax.fori_loop(0, steps, fwd, (ones, zeros), unroll=UNROLL)
    for k in range(chunks):
        fa_ref[:, pl.ds(k * LANES, LANES)] = a[k]
        fb_ref[:, pl.ds(k * LANES, LANES)] = b[k]

    def bwd(j, carry):
        a, b = carry
        i = steps - 1 - j
        g = gn_ref[i]
        new_a, new_b = [], []
        for k in range(chunks):
            e = jnp.exp(-(g * rs[k]))
            u = up_refs[k][pl.ds(i, segs, stride=steps), :]
            new_a.append(a[k] * e)
            new_b.append(e * b[k] + u)
        return (tuple(new_a), tuple(new_b))

    a, b = lax.fori_loop(0, steps, bwd, (ones, zeros), unroll=UNROLL)
    for k in range(chunks):
        ba_ref[:, pl.ds(k * LANES, LANES)] = a[k]
        bb_ref[:, pl.ds(k * LANES, LANES)] = b[k]


def _sweep_kernel(g_ref, gn_ref, r_ref, if_ref, ib_ref, *refs):
    chunks = (len(refs) - 2) // 2
    drive_refs = refs[:chunks]
    up_refs = refs[chunks:2 * chunks]
    st_ref, adj_ref = refs[2 * chunks:]
    steps, segs, _ = g_ref.shape
    rs = [r_ref[:, pl.ds(k * LANES, LANES)] for k in range(chunks)]

    def fwd(i, b):
        g = g_ref[i]
        out = []
        for k in range(chunks):
            d = jnp.exp(-(g * rs[k]))
            v = d * b[k] + drive_refs[k][pl.ds(i, segs, stride=steps), :]
            st_ref[k, pl.ds(i, segs, stride=steps), :] = v
            out.append(v)
        return tuple(out)

    init = tuple(if_ref[:, pl.ds(k * LANES, LANES)] for k in range(chunks))
    lax.fori_loop(0, steps, fwd, init, unroll=UNROLL)

    def bwd(j, b):
        i = steps - 1 - j
        g = gn_ref[i]
        out = []
        for k in range(chunks):
            e = jnp.exp(-(g * rs[k]))
            v = e * b[k] + up_refs[k][pl.ds(i, segs, stride=steps), :]
            adj_ref[k, pl.ds(i, segs, stride=steps), :] = v
            out.append(v)
        return tuple(out)

    init = tuple(ib_ref[:, pl.ds(k * LANES, LANES)] for k in range(chunks))
    lax.fori_loop(0, steps, bwd, init, unroll=UNROLL)


def _column_specs(total, width):
    return [pl.BlockSpec((total, LANES), lambda j, k=k: (0, k)) for k in range(width // LANES)]


def _whole(shape):
    return pl.BlockSpec(shape, lambda j: (0,) * len(shape))


def local_summaries(g3, gn3, rates2, drive, up):
    total, width = drive.shape
    steps, segs, _ = g3.shape
    chunks = width // LANES
    cols = _column_specs(total, width)
    seg_shape = jax.ShapeDtypeStruct((segs, width), jnp.float32)
    return pl.pallas_call(
        _summary_kernel,
        grid=(1,),
        in_specs=[_whole(g3.shape), _whole(gn3.shape), _whole(rates2.shape)] + cols + cols,
        out_specs=[_whole((segs, width))] * 4,
        out_shape=[seg_shape] * 4,
        compiler_params=pltpu.CompilerParams(vmem_limit_bytes=48 * 1024 * 1024),
    )(g3, gn3, rates2, *([drive] * chunks), *([up] * chunks))


def sweeps(g3, gn3, rates2, drive, up, init_f, init_b):
    total, width = drive.shape
    steps, segs, _ = g3.shape
    chunks = width // LANES
    cols = _column_specs(total, width)
    full = jax.ShapeDtypeStruct((chunks, total, LANES), jnp.float32)
    return pl.pallas_call(
        _sweep_kernel,
        grid=(1,),
        in_specs=[_whole(g3.shape), _whole(gn3.shape), _whole(rates2.shape),
                  _whole(init_f.shape), _whole(init_b.shape)] + cols + cols,
        out_specs=[_whole(full.shape)] * 2,
        out_shape=[full, full],
        compiler_params=pltpu.CompilerParams(vmem_limit_bytes=48 * 1024 * 1024),
    )(g3, gn3, rates2, init_f, init_b, *([drive] * chunks), *([up] * chunks))


def local(inputs, gaps, rates, w_in, w_out, cotangent):
    total = inputs.shape[0]
    width = rates.shape[0]
    segs = SEGMENTS
    steps = total // segs
    peers = lax.axis_size("seq")
    place = lax.axis_index("seq")
    factor = 1.0 / math.sqrt(total * peers)

    gain = jnp.sqrt(-jnp.expm1(-2.0 * gaps[:, None] * rates[None, :]))
    drive = gain * jnp.dot(inputs, w_in, preferred_element_type=jnp.float32)
    upstream = lax.dot_general(
        cotangent, w_out, (((1,), (1,)), ((), ())), preferred_element_type=jnp.float32
    )
    gaps_next = jnp.concatenate([gaps[1:], jnp.zeros((1,), jnp.float32)], 0)
    g3 = gaps.reshape(segs, steps).T[:, :, None]
    gn3 = gaps_next.reshape(segs, steps).T[:, :, None]
    rates2 = rates[None, :]

    fa, fb, ba, bb = local_summaries(g3, gn3, rates2, drive, up=upstream)

    end_state = jnp.zeros((width,), jnp.float32)
    block_decay = jnp.ones((width,), jnp.float32)
    for s in range(segs):
        end_state = fb[s] + fa[s] * end_state
        block_decay = block_decay * fa[s]
    first_adj = jnp.zeros((width,), jnp.float32)
    for s in reversed(range(segs)):
        first_adj = bb[s] + ba[s] * first_adj
    start_adj = jnp.exp(-gaps[0] * rates) * first_adj

    gathered = lax.all_gather(jnp.stack([block_decay, end_state, start_adj], 0), "seq")
    carry_in = jnp.zeros((width,), jnp.float32)
    for q in range(peers):
        new = gathered[q, 1] + gathered[q, 0] * carry_in
        carry_in = jnp.where(q < place, new, carry_in)
    right_in = jnp.zeros((width,), jnp.float32)
    for q in reversed(range(peers)):
        new = gathered[q, 2] + gathered[q, 0] * right_in
        right_in = jnp.where(q > place, new, right_in)

    inits_f = []
    e = carry_in
    for s in range(segs):
        inits_f.append(e)
        e = fb[s] + fa[s] * e
    inits_b = [None] * segs
    v = right_in
    for s in reversed(range(segs)):
        inits_b[s] = v
        v = bb[s] + ba[s] * v
    init_f = jnp.stack(inits_f, 0)
    init_b = jnp.stack(inits_b, 0)

    state, adjoint = sweeps(g3, gn3, rates2, drive, upstream, init_f, init_b)
    chunks = width // LANES
    gain3 = gain.reshape(total, chunks, LANES).transpose(1, 0, 2)
    drive_grad = (gain3 * adjoint).astype(jnp.bfloat16)
    state_low = state.astype(jnp.bfloat16)
    d_w_in = lax.psum_scatter(
        (
            lax.dot_general(
                inputs, drive_grad, (((0,), (1,)), ((), ())), preferred_element_type=jnp.float32
            ).reshape(inputs.shape[1], width)
            * factor
        ).astype(jnp.bfloat16),
        "seq",
        scatter_dimension=0,
        tiled=True,
    ).astype(jnp.float32)
    out_term = (
        lax.dot_general(
            state_low, cotangent, (((1,), (0,)), ((), ())), preferred_element_type=jnp.float32
        ).reshape(width, cotangent.shape[1])
        * factor
    )
    d_w_out = lax.psum_scatter(
        out_term.astype(jnp.bfloat16), "seq", scatter_dimension=1, tiled=True
    ).astype(jnp.float32)
    w_in3 = w_in.reshape(w_in.shape[0], chunks, LANES)
    partial_value = lax.dot_general(
        drive_grad, w_in3, (((0, 2), (1, 2)), ((), ())), preferred_element_type=jnp.float32
    )
    d_inputs = lax.psum_scatter(
        partial_value.astype(jnp.bfloat16), "chan", scatter_dimension=1, tiled=True
    )
    return (d_inputs, d_w_in, d_w_out)


def solution(mesh):
    placed = (P("seq", None), P("seq"), P("chan"), P(None, "chan"), P("chan", None), P("seq", None))
    return jax.shard_map(
        local,
        mesh=mesh,
        in_specs=placed,
        out_specs=(P("seq", "chan"), P("seq", "chan"), P("chan", "seq")),
        check_vma=False,
    )
```

profile of v0, /device:TPU:0, one launch (start us, length us, event | category | flops | bytes accessed | tf_op | source)
XLA Modules:
  0.0 290.1 jit_solution(15380794506685541302)
XLA Ops:
  7.2 0.0 copy-start
  7.2 0.0 reduce-scatter.8.cloned.1.call-start
  7.3 1.3 slice.315
  8.6 0.7 broadcast_multiply_fusion
  9.3 0.7 reshape.1227
  10.0 0.8 slice.298
  11.4 0.1 pad_maximum_fusion
  11.5 0.4 copy.26.gn_ref
  11.9 0.4 copy.25.g_ref
  12.3 0.0 copy-start.1
  12.4 0.0 copy-start.3
  12.4 7.0 %fusion.45.refs_4_.refs_5_.refs_6_.refs_7_ = f32[2048,512]{1,0:T(8,128)} fusion(bf16[2048,1024]{1,0:T(8,128)(2,1)} %param.11, bf16[512,1024]{1,0:T(8,128)(2,1)} %param.10), kind=kOutput, calls=%fused_computation.145 | convolution fusion | flops 2147483648 | bytes 9437184 | tf_op jit(solution)/shard_map/dot_general | solution.py:147
  19.4 0.0 copy-done
  19.4 0.0 copy-done.1
  19.4 0.0 copy-done.3
  19.4 6.6 %sqrt_multiply_fusion.refs_0_.refs_1_.refs_2_.refs_3_ = f32[2048,512]{1,0:T(8,128)} fusion(bf16[2048,1024]{1,0:T(8,128)(2,1)S(1)} %copy-done.3, bf16[1024,512]{1,0:T(8,128)(2,1)S(1)} %copy-done, f32[512]{0:T(512)S(1)} %copy-done.1, f32[2048]{0:T(1024)S(1)} %broadcast_multiply_fusion), kind=kOutput, calls=%fused_computation.6 | convolution fusion | flops 2150629376 | bytes 9447424 | tf_op jit(solution)/shard_map/dot_general | solution.py:146
  25.9 12.3 %shard_map.85 = (f32[8,512]{1,0:T(8,128)S(1)}, f32[8,512]{1,0:T(8,128)S(1)}, f32[8,512]{1,0:T(8,128)S(1)}, f32[8,512]{1,0:T(8,128)S(1)}) custom-call(f32[256,8,1]{2,1,0:T(8,128)S(1)} %copy.25.g_ref, f32[256,8,1]{2,1,0:T(8,128)S(1)} %copy.26.gn_ref, f32[1,512]{1,0:T(1,128)S(1)} %bitcast.454, f32[2048,512]{1,0:T(8,128)} %sqrt_multiply_fusion.refs_0_.refs_1_.refs_2_.refs_3_, ...), custom_call_target="tpu_custom_call" | custom-call | tf_op jit(solution)/shard_map/pallas_call | solution.py:109
  38.4 25.2 %all-gather.1 = f32[16,3,512]{2,1,0:T(4,128)S(1)} all-gather(f32[1,3,512]{2,1,0:T(4,128)S(1)} %maximum_bitcast_fusion), channel_id=2, replica_groups=mesh['seq'=16,'chan'=8] {'seq'}, dimensions={0}, use_global_device_ids=true | all-gather | bytes 104448 | tf_op jit(solution)/shard_map/all_gather | solution.py:167
  63.6 0.1 multiply_add_fusion.1
  63.7 0.1 multiply_add_fusion.8
  63.8 0.0 copy-start.2
  63.9 21.7 %shard_map.86 = (f32[4,2048,128]{2,1,0:T(8,128)}, f32[4,2048,128]{2,1,0:T(8,128)}) custom-call(f32[256,8,1]{2,1,0:T(8,128)S(1)} %copy.25.g_ref, f32[256,8,1]{2,1,0:T(8,128)S(1)} %copy.26.gn_ref, f32[1,512]{1,0:T(1,128)S(1)} %bitcast.455, f32[8,512]{1,0:T(8,128)S(1)} %stack.10.if_ref, f32[8,512]{1,0:T(8,128)S(1)} %stack.11.ib_ref, ...), custom_call_target="tpu_custom_call" | custom-call | tf_op jit(solution)/shard_map/pallas_call | solution.py:125
  85.6 0.0 copy-done.2
  85.6 4.5 %multiply_convert_fusion.1 = bf16[4,128,1024]{2,1,0:T(8,128)(2,1)S(1)} fusion(bf16[2048,1024]{1,0:T(8,128)(2,1)S(1)} %copy-done.2, f32[4,2048,128]{2,1,0:T(8,128)} %get-tuple-element.14), kind=kOutput, calls=%fused_computation.7 | convolution fusion | flops 2149580800 | bytes 9437184 | tf_op jit(solution)/shard_map/dot_general | solution.py:207
  90.1 1.3 copy.31
  91.5 0.0 reduce-scatter.8.cloned.1.call-update
  91.5 0.2 reduce-scatter.6.cloned.1.call-start
  91.7 7.5 %multiply_convert_fusion.2 = bf16[4,128,1024]{2,1,0:T(8,128)(2,1)S(1)} fusion(bf16[2048,1024]{1,0:T(8,128)(2,1)} %param.6, f32[4,2048,128]{2,1,0:T(8,128)} %get-tuple-element.13, f32[4,128]{1,0:T(4,128)S(1)} %bitcast.456, f32[2048]{0:T(1024)S(1)} %broadcast_multiply_fusion), kind=kOutput, calls=%fused_computation.9 | convolution fusion | flops 2152726528 | bytes 9447424 | tf_op jit(solution)/shard_map/dot_general | solution.py:197
  99.2 1.4 copy.29
  100.6 0.0 reduce-scatter.6.cloned.1.call-update
  100.6 0.0 reduce-scatter.10.cloned.1.call-start
  100.6 8.2 %bitcast_convert_fusion = bf16[2048,1024]{1,0:T(8,128)(2,1)} fusion(f32[4,2048,128]{2,1,0:T(8,128)} %get-tuple-element.13, f32[4,128]{1,0:T(4,128)S(1)} %bitcast.457, f32[2048]{0:T(1024)S(1)} %broadcast_multiply_fusion, bf16[1024,512]{1,0:T(8,128)(2,1)S(1)} %copy-done), kind=kOutput, calls=%fused_computation | convolution fusion | flops 2153775104 | bytes 9447424 | tf_op jit(solution)/shard_map/dot_general | solution.py:216
  108.9 6.5 %copy.34 = bf16[2048,1024]{0,1:T(8,128)(2,1)} copy(bf16[2048,1024]{1,0:T(8,128)(2,1)} %bitcast_convert_fusion) | data formatting | bytes 8388608
  115.4 0.0 reduce-scatter.10.cloned.1.call-update
  115.4 49.8 %reduce-scatter.8.cloned.1.call-done = bf16[512,64]{0,1:T(8,128)(2,1)} async-done(((bf16[512,1024]{0,1:T(8,128)(2,1)}), bf16[512,64]{0,1:T(8,128)(2,1)}) %reduce-scatter.8.cloned.1.call-update) | async-done | bytes 65552 | tf_op jit(solution)/shard_map/reduce_scatter | solution.py:212
  165.2 1.5 convert_element_type.39
  166.7 75.1 %reduce-scatter.6.cloned.1.call-done = bf16[64,512]{1,0:T(8,128)(2,1)} async-done(((bf16[1024,512]{1,0:T(8,128)(2,1)}), bf16[64,512]{1,0:T(8,128)(2,1)}) %reduce-scatter.6.cloned.1.call-update) | async-done | bytes 65552 | tf_op jit(solution)/shard_map/reduce_scatter | solution.py:195
  241.8 1.5 convert_element_type.35
  243.3 38.2 %reduce-scatter.10.cloned.1.call-done = bf16[128,2048]{1,0:T(8,128)(2,1)} async-done(((bf16[1024,2048]{1,0:T(8,128)(2,1)}), bf16[128,2048]{1,0:T(8,128)(2,1)}) %reduce-scatter.10.cloned.1.call-update) | async-done | bytes 524304
  281.5 2.0 copy.35
  (8 shorter events, 0.2 us)
Async XLA Ops:
  7.2 12.2 %copy-start = (bf16[1024,512]{1,0:T(8,128)(2,1)S(1)}, bf16[1024,512]{1,0:T(8,128)(2,1)}, u32[]{:S(2)}) copy-start(bf16[1024,512]{1,0:T(8,128)(2,1)} %param.9) | copy-start | bytes 3145732
  7.2 158.0 %reduce-scatter.8.cloned.1.call-start = ((), (), s32[]{:S(2)}) async-start(), calls=%async_computation.4 | async-start | bytes 1114112 | tf_op jit(solution)/shard_map/reduce_scatter | solution.py:212
  12.3 7.0 %copy-start.1 = (f32[512]{0:T(512)S(1)}, f32[512]{0:T(512)}, u32[]{:S(2)}) copy-start(f32[512]{0:T(512)} %param.8) | copy-start | bytes 6148
  12.4 7.0 %copy-start.3 = (bf16[2048,1024]{1,0:T(8,128)(2,1)S(1)}, bf16[2048,1024]{1,0:T(8,128)(2,1)}, u32[]{:S(2)}) copy-start(bf16[2048,1024]{1,0:T(8,128)(2,1)} %param.6) | copy-start | bytes 12582916
  63.8 21.8 %copy-start.2 = (bf16[2048,1024]{1,0:T(8,128)(2,1)S(1)}, bf16[2048,1024]{1,0:T(8,128)(2,1)}, u32[]{:S(2)}) copy-start(bf16[2048,1024]{1,0:T(8,128)(2,1)} %param.11) | copy-start | bytes 12582916
  91.5 150.3 %reduce-scatter.6.cloned.1.call-start = ((), (), s32[]{:S(2)}) async-start(), calls=%async_computation.3 | async-start | bytes 1114112 | tf_op jit(solution)/shard_map/reduce_scatter | solution.py:195
  100.6 180.9 %reduce-scatter.10.cloned.1.call-start = ((), (), s32[]{:S(2)}) async-start(), calls=%async_computation.5 | async-start | bytes 4718592
Sparse Core Ops, SparseCore 0:
  91.6 73.5 reduce-scatter.7
  168.4 73.3 reduce-scatter.5
  244.2 37.2 reduce-scatter.9
where the time goes:
time: 291 us; the launch traced here: 290 us
  waiting for transfers between devices  163 us (56%)
  Pallas kernels  34.1 us (12%)
  matrix products  33.8 us (12%)
  blocking collectives  25.2 us (9%)
  local copies, waits for them, and re-layouts  15 us (5%)
  between operations  14.6 us (5%)
  other arithmetic  4.09 us (1%)
    reduce_scatter x1, waiting for transfers between devices, local(): lax.psum_scatter((lax.dot_general(inputs, drive_grad, (((0,), (1,)), ((),...  75.1 us
    reduce_scatter x1, waiting for transfers between devices, local(): lax.psum_scatter(out_term.astype(jnp.bfloat16), 'seq', scatter_dimension=...  49.8 us
    unnamed x4, waiting for transfers between devices  38.2 us
    all_gather x1, blocking collectives, local(): lax.all_gather(jnp.stack([block_decay, end_state, start_adj], 0), 'seq')  25.2 us
    pallas_call x1, Pallas kernels, sweeps(): pl.pallas_call(_sweep_kernel, grid=(1,), in_specs=[_whole(g3.shape), _who...  21.7 us
    pallas_call x1, Pallas kernels, local_summaries(): pl.pallas_call(_summary_kernel, grid=(1,), in_specs=[_whole(g3.shape), _w...  12.3 us
    unnamed x10, local copies, waits for them, and re-layouts  8.61 us
    dot_general x1, matrix products, local(): lax.dot_general(drive_grad, w_in3, (((0, 2), (1, 2)), ((), ())), preferre...  8.24 us
  transfers between devices with their start and end apart: 3, of which 3 were waited for; matrix products, arithmetic and copies ran while one was open for 9% of the time, Pallas kernels for 0%

commit v1 on v0

--- a/solution.py
+++ b/solution.py
@@ -5,7 +5,7 @@
 from jax import lax
 from jax.experimental import pallas as pl
 from jax.experimental.pallas import tpu as pltpu
-from jax.sharding import PartitionSpec as P
+from jax.sharding import Mesh, PartitionSpec as P
 
 SEGMENTS = 8
 LANES = 128
@@ -138,8 +138,8 @@
     width = rates.shape[0]
     segs = SEGMENTS
     steps = total // segs
-    peers = lax.axis_size("seq")
-    place = lax.axis_index("seq")
+    peers = lax.axis_size(SEQ)
+    place = lax.axis_index(SEQ)
     factor = 1.0 / math.sqrt(total * peers)
 
     gain = jnp.sqrt(-jnp.expm1(-2.0 * gaps[:, None] * rates[None, :]))
@@ -164,7 +164,8 @@
         first_adj = bb[s] + ba[s] * first_adj
     start_adj = jnp.exp(-gaps[0] * rates) * first_adj
 
-    gathered = lax.all_gather(jnp.stack([block_decay, end_state, start_adj], 0), "seq")
+    summary = jnp.stack([block_decay, end_state, start_adj], 0)
+    gathered = lax.all_gather(lax.all_gather(summary, "sz"), "sx").reshape(peers, 3, width)
     carry_in = jnp.zeros((width,), jnp.float32)
     for q in range(peers):
         new = gathered[q, 1] + gathered[q, 0] * carry_in
@@ -192,42 +193,45 @@
     gain3 = gain.reshape(total, chunks, LANES).transpose(1, 0, 2)
     drive_grad = (gain3 * adjoint).astype(jnp.bfloat16)
     state_low = state.astype(jnp.bfloat16)
-    d_w_in = lax.psum_scatter(
-        (
-            lax.dot_general(
-                inputs, drive_grad, (((0,), (1,)), ((), ())), preferred_element_type=jnp.float32
-            ).reshape(inputs.shape[1], width)
-            * factor
-        ).astype(jnp.bfloat16),
-        "seq",
-        scatter_dimension=0,
-        tiled=True,
-    ).astype(jnp.float32)
-    out_term = (
-        lax.dot_general(
-            state_low, cotangent, (((1,), (0,)), ((), ())), preferred_element_type=jnp.float32
-        ).reshape(width, cotangent.shape[1])
-        * factor
-    )
-    d_w_out = lax.psum_scatter(
-        out_term.astype(jnp.bfloat16), "seq", scatter_dimension=1, tiled=True
-    ).astype(jnp.float32)
+    in_term = lax.dot_general(
+        inputs, drive_grad, (((0,), (1,)), ((), ())), preferred_element_type=jnp.float32
+    ).reshape(inputs.shape[1], width) * factor
+    out_term = lax.dot_general(
+        cotangent, state_low, (((0,), (1,)), ((), ())), preferred_element_type=jnp.float32
+    ).reshape(cotangent.shape[1], width) * factor
+    joined = jnp.concatenate([in_term, out_term], 1).astype(jnp.bfloat16)
+    joined = lax.psum_scatter(joined, "sx", scatter_dimension=0, tiled=True)
+    joined = lax.psum_scatter(joined, "sz", scatter_dimension=0, tiled=True).astype(jnp.float32)
+    d_w_in = joined[:, :width]
+    d_w_out = joined[:, width:].T
     w_in3 = w_in.reshape(w_in.shape[0], chunks, LANES)
     partial_value = lax.dot_general(
         drive_grad, w_in3, (((0, 2), (1, 2)), ((), ())), preferred_element_type=jnp.float32
     )
     d_inputs = lax.psum_scatter(
-        partial_value.astype(jnp.bfloat16), "chan", scatter_dimension=1, tiled=True
+        partial_value.astype(jnp.bfloat16), CHAN, scatter_dimension=1, tiled=True
     )
     return (d_inputs, d_w_in, d_w_out)
 
 
+SEQ = ("sx", "sz")
+CHAN = ("cy", "cc")
+
+
 def solution(mesh):
-    placed = (P("seq", None), P("seq"), P("chan"), P(None, "chan"), P("chan", None), P("seq", None))
+    grid = mesh.devices
+    seq_size, chan_size = grid.shape
+    z_size = len({d.coords[2] for d in grid[:, 0]})
+    core_size = len({d.core_on_chip for d in grid[0, :]})
+    split = Mesh(
+        grid.reshape(seq_size // z_size, z_size, chan_size // core_size, core_size),
+        ("sx", "sz", "cy", "cc"),
+    )
+    placed = (P(SEQ, None), P(SEQ), P(CHAN), P(None, CHAN), P(CHAN, None), P(SEQ, None))
     return jax.shard_map(
         local,
-        mesh=mesh,
+        mesh=split,
         in_specs=placed,
-        out_specs=(P("seq", "chan"), P("seq", "chan"), P("chan", "seq")),
+        out_specs=(P(SEQ, CHAN), P(SEQ, CHAN), P(CHAN, SEQ)),
         check_vma=False,
     )

time: 291 us -> 206 us (0.71)
  waiting for transfers between devices: 163 us -> 76.4 us
    reduce_scatter x2, waiting for transfers between devices: 125 us -> 39.5 us  [the longest x1 30.4 us: local(): joined = lax.psum_scatter(joined, 'sx', scatter_dimension=0, tiled=True)]
    all_gather x1 -> x2, blocking collectives: 25.2 us -> 25.8 us  [the longest x1 13.2 us: local(): lax.all_gather(summary, 'sz')]
where the time goes in v1:
time: 206 us
  waiting for transfers between devices  76.4 us (37%)
  matrix products  34.8 us (17%)
  Pallas kernels  34.1 us (17%)
  blocking collectives  25.8 us (13%)
  local copies, waits for them, and re-layouts  16.5 us (8%)
  between operations  14.6 us (7%)
  other arithmetic  3.59 us (2%)
    unnamed x4, waiting for transfers between devices  37 us
    reduce_scatter x1, waiting for transfers between devices, local(): joined = lax.psum_scatter(joined, 'sx', scatter_dimension=0, tiled=True)  30.4 us
    pallas_call x1, Pallas kernels, sweeps(): pl.pallas_call(_sweep_kernel, grid=(1,), in_specs=[_whole(g3.shape), _who...  21.7 us
    all_gather x1, blocking collectives, local(): lax.all_gather(summary, 'sz')  13.2 us
    all_gather x1, blocking collectives, local(): lax.all_gather(lax.all_gather(summary, 'sz'), 'sx').reshape(peers, 3, width)  12.5 us
    pallas_call x1, Pallas kernels, local_summaries(): pl.pallas_call(_summary_kernel, grid=(1,), in_specs=[_whole(g3.shape), _w...  12.3 us
    reduce_scatter x1, waiting for transfers between devices, local(): lax.psum_scatter(joined, 'sz', scatter_dimension=0, tiled=True)  9.11 us
    unnamed x10, local copies, waits for them, and re-layouts  8.61 us
  transfers between devices with their start and end apart: 3, of which 3 were waited for; matrix products, arithmetic and copies ran while one was open for 9% of the time, Pallas kernels for 0%

profile of v1, /device:TPU:0, one launch (start us, length us, event | category | flops | bytes accessed | tf_op | source)
XLA Modules:
  0.0 205.8 jit_solution(6290469541367129841)
XLA Ops:
  7.2 0.0 copy-start
  7.2 0.0 reduce-scatter.6.cloned.1.call-start
  7.3 1.3 slice.321
  8.6 0.7 broadcast_multiply_fusion
  9.3 0.7 reshape.1230
  10.0 0.8 slice.304
  11.4 0.1 pad_maximum_fusion.1
  11.5 0.4 copy.26.gn_ref
  11.9 0.4 copy.25.g_ref
  12.4 0.0 copy-start.1
  12.4 0.0 copy-start.3
  12.4 7.0 %fusion.45.refs_4_.refs_5_.refs_6_.refs_7_ = f32[2048,512]{1,0:T(8,128)} fusion(bf16[2048,1024]{1,0:T(8,128)(2,1)} %param.11, bf16[512,1024]{1,0:T(8,128)(2,1)} %param.10), kind=kOutput, calls=%fused_computation.147 | convolution fusion | flops 2147483648 | bytes 9437184 | tf_op jit(solution)/shard_map/dot_general | solution.py:147
  19.4 0.0 copy-done
  19.4 0.0 copy-done.1
  19.4 0.0 copy-done.3
  19.4 6.6 %sqrt_multiply_fusion.refs_0_.refs_1_.refs_2_.refs_3_ = f32[2048,512]{1,0:T(8,128)} fusion(bf16[2048,1024]{1,0:T(8,128)(2,1)S(1)} %copy-done.3, bf16[1024,512]{1,0:T(8,128)(2,1)S(1)} %copy-done, f32[512]{0:T(512)S(1)} %copy-done.1, f32[2048]{0:T(1024)S(1)} %broadcast_multiply_fusion), kind=kOutput, calls=%fused_computation.6 | convolution fusion | flops 2150629376 | bytes 9447424 | tf_op jit(solution)/shard_map/dot_general | solution.py:146
  25.9 12.3 %shard_map.85 = (f32[8,512]{1,0:T(8,128)S(1)}, f32[8,512]{1,0:T(8,128)S(1)}, f32[8,512]{1,0:T(8,128)S(1)}, f32[8,512]{1,0:T(8,128)S(1)}) custom-call(f32[256,8,1]{2,1,0:T(8,128)S(1)} %copy.25.g_ref, f32[256,8,1]{2,1,0:T(8,128)S(1)} %copy.26.gn_ref, f32[1,512]{1,0:T(1,128)S(1)} %bitcast.458, f32[2048,512]{1,0:T(8,128)} %sqrt_multiply_fusion.refs_0_.refs_1_.refs_2_.refs_3_, ...), custom_call_target="tpu_custom_call" | custom-call | tf_op jit(solution)/shard_map/pallas_call | solution.py:109
  38.4 13.2 %all-gather.2 = f32[4,3,512]{2,1,0:T(4,128)S(1)} all-gather(f32[1,3,512]{2,1,0:T(4,128)S(1)} %maximum_bitcast_fusion), channel_id=2, replica_groups=mesh['sx'=4,'sz'=4,'cy'=4,'cc'=2] {'sz'}, dimensions={0}, use_global_device_ids=true | all-gather | bytes 30720 | tf_op jit(solution)/shard_map/all_gather | solution.py:168
  51.6 12.5 %all-gather.1 = f32[16,3,512]{2,1,0:T(4,128)S(1)} all-gather(f32[4,3,512]{2,1,0:T(4,128)S(1)} %all-gather.2), channel_id=3, replica_groups=mesh['sx'=4,'sz'=4,'cy'=4,'cc'=2] {'sx'}, dimensions={0}, use_global_device_ids=true | all-gather | bytes 122880 | tf_op jit(solution)/shard_map/all_gather | solution.py:168
  64.1 0.1 multiply_add_fusion.1
  64.3 0.1 multiply_add_fusion.8
  64.4 0.0 copy-start.2
  64.4 21.7 %shard_map.86 = (f32[4,2048,128]{2,1,0:T(8,128)}, f32[4,2048,128]{2,1,0:T(8,128)}) custom-call(f32[256,8,1]{2,1,0:T(8,128)S(1)} %copy.25.g_ref, f32[256,8,1]{2,1,0:T(8,128)S(1)} %copy.26.gn_ref, f32[1,512]{1,0:T(1,128)S(1)} %bitcast.459, f32[8,512]{1,0:T(8,128)S(1)} %stack.10.if_ref, f32[8,512]{1,0:T(8,128)S(1)} %stack.11.ib_ref, ...), custom_call_target="tpu_custom_call" | custom-call | tf_op jit(solution)/shard_map/pallas_call | solution.py:125
  86.2 0.0 copy-done.2
  86.2 4.5 %multiply_convert_fusion.1 = bf16[4,128,1024]{2,1,0:T(8,128)(2,1)S(1)} fusion(bf16[2048,1024]{1,0:T(8,128)(2,1)S(1)} %copy-done.2, f32[4,2048,128]{2,1,0:T(8,128)} %get-tuple-element.14), kind=kOutput, calls=%fused_computation.8 | convolution fusion | flops 2149580800 | bytes 9437184 | tf_op jit(solution)/shard_map/dot_general | solution.py:199
  90.7 0.5 copy.31
  91.3 8.5 %multiply_convert_fusion.2 = bf16[4,128,1024]{2,1,0:T(8,128)(2,1)} fusion(bf16[2048,1024]{1,0:T(8,128)(2,1)} %param.6, f32[4,2048,128]{2,1,0:T(8,128)} %get-tuple-element.13, f32[4,128]{1,0:T(4,128)S(1)} %bitcast.460, f32[2048]{0:T(1024)S(1)} %broadcast_multiply_fusion), kind=kOutput, calls=%fused_computation.10 | convolution fusion | flops 2152726528 | bytes 9447424 | tf_op jit(solution)/shard_map/dot_general | solution.py:196
  99.7 1.5 copy.30
  101.2 1.6 pad_maximum_fusion
  102.8 0.0 reduce-scatter.6.cloned.1.call-update
  102.8 0.0 reduce-scatter.8.cloned.1.call-start
  102.9 30.4 %reduce-scatter.6.cloned.1.call-done = bf16[256,1024]{1,0:T(8,128)(2,1)} async-done(((bf16[1024,1024]{1,0:T(8,128)(2,1)}), bf16[256,1024]{1,0:T(8,128)(2,1)}) %reduce-scatter.6.cloned.1.call-update) | async-done | bytes 524304 | tf_op jit(solution)/shard_map/reduce_scatter | solution.py:203
  133.2 0.0 reduce-scatter.8.cloned.1.call-update
  133.3 0.0 reduce-scatter.10.cloned.1.call-start
  133.3 8.2 %bitcast_convert_fusion = bf16[2048,1024]{1,0:T(8,128)(2,1)} fusion(f32[4,2048,128]{2,1,0:T(8,128)} %get-tuple-element.13, f32[4,128]{1,0:T(4,128)S(1)} %bitcast.461, f32[2048]{0:T(1024)S(1)} %broadcast_multiply_fusion, bf16[1024,512]{1,0:T(8,128)(2,1)S(1)} %copy-done), kind=kOutput, calls=%fused_computation | convolution fusion | flops 2153775104 | bytes 9447424 | tf_op jit(solution)/shard_map/dot_general | solution.py:208
  141.6 6.5 %copy.34 = bf16[2048,1024]{0,1:T(8,128)(2,1)} copy(bf16[2048,1024]{1,0:T(8,128)(2,1)} %bitcast_convert_fusion) | data formatting | bytes 8388608
  148.1 0.0 reduce-scatter.10.cloned.1.call-update
  148.1 9.1 %reduce-scatter.8.cloned.1.call-done = bf16[64,1024]{1,0:T(8,128)(2,1)} async-done(((bf16[256,1024]{1,0:T(8,128)(2,1)}), bf16[64,1024]{1,0:T(8,128)(2,1)}) %reduce-scatter.8.cloned.1.call-update) | async-done | bytes 131088 | tf_op jit(solution)/shard_map/reduce_scatter | solution.py:204
  157.2 1.5 slice.436
  158.7 0.9 convert_element_type.16
  159.7 0.7 slice_bitcast_fusion
  160.3 36.9 %reduce-scatter.10.cloned.1.call-done = bf16[128,2048]{1,0:T(8,128)(2,1)} async-done(((bf16[1024,2048]{1,0:T(8,128)(2,1)}), bf16[128,2048]{1,0:T(8,128)(2,1)}) %reduce-scatter.10.cloned.1.call-update) | async-done | bytes 524304
  197.2 2.0 copy.35
  (8 shorter events, 0.2 us)
Async XLA Ops:
  7.2 12.2 %copy-start = (bf16[1024,512]{1,0:T(8,128)(2,1)S(1)}, bf16[1024,512]{1,0:T(8,128)(2,1)}, u32[]{:S(2)}) copy-start(bf16[1024,512]{1,0:T(8,128)(2,1)} %param.9) | copy-start | bytes 3145732
  7.2 126.1 %reduce-scatter.6.cloned.1.call-start = ((), (), s32[]{:S(2)}) async-start(), calls=%async_computation.3 | async-start | bytes 2621440 | tf_op jit(solution)/shard_map/reduce_scatter | solution.py:203
  12.4 7.0 %copy-start.1 = (f32[512]{0:T(512)S(1)}, f32[512]{0:T(512)}, u32[]{:S(2)}) copy-start(f32[512]{0:T(512)} %param.8) | copy-start | bytes 6148
  12.4 7.0 %copy-start.3 = (bf16[2048,1024]{1,0:T(8,128)(2,1)S(1)}, bf16[2048,1024]{1,0:T(8,128)(2,1)}, u32[]{:S(2)}) copy-start(bf16[2048,1024]{1,0:T(8,128)(2,1)} %param.6) | copy-start | bytes 12582916
  64.4 21.8 %copy-start.2 = (bf16[2048,1024]{1,0:T(8,128)(2,1)S(1)}, bf16[2048,1024]{1,0:T(8,128)(2,1)}, u32[]{:S(2)}) copy-start(bf16[2048,1024]{1,0:T(8,128)(2,1)} %param.11) | copy-start | bytes 12582916
  102.8 54.4 %reduce-scatter.8.cloned.1.call-start = ((), (), s32[]{:S(2)}) async-start(), calls=%async_computation.4 | async-start | bytes 655360 | tf_op jit(solution)/shard_map/reduce_scatter | solution.py:204
  133.3 64.0 %reduce-scatter.10.cloned.1.call-start = ((), (), s32[]{:S(2)}) async-start(), calls=%async_computation.5 | async-start | bytes 4718592
Sparse Core Ops, SparseCore 0:
  103.0 30.2 reduce-scatter.5
  135.6 21.5 reduce-scatter.7
  159.6 37.5 reduce-scatter.9

commit v2 on v1

--- a/solution.py
+++ b/solution.py
@@ -7,7 +7,7 @@
 from jax.experimental.pallas import tpu as pltpu
 from jax.sharding import Mesh, PartitionSpec as P
 
-SEGMENTS = 8
+SEGMENTS = 16
 LANES = 128
 UNROLL = 8
 
@@ -204,13 +204,19 @@
     joined = lax.psum_scatter(joined, "sz", scatter_dimension=0, tiled=True).astype(jnp.float32)
     d_w_in = joined[:, :width]
     d_w_out = joined[:, width:].T
-    w_in3 = w_in.reshape(w_in.shape[0], chunks, LANES)
-    partial_value = lax.dot_general(
-        drive_grad, w_in3, (((0, 2), (1, 2)), ((), ())), preferred_element_type=jnp.float32
-    )
-    d_inputs = lax.psum_scatter(
-        partial_value.astype(jnp.bfloat16), CHAN, scatter_dimension=1, tiled=True
-    )
+    ys = lax.axis_size("cy")
+    cores = lax.axis_size("cc")
+    dmodel = w_in.shape[0]
+    w_perm = (
+        w_in.reshape(ys, cores, dmodel // (ys * cores), chunks, LANES)
+        .transpose(1, 0, 2, 3, 4)
+        .reshape(dmodel, chunks, LANES)
+    )
+    partial_t = lax.dot_general(
+        w_perm, drive_grad, (((1, 2), (0, 2)), ((), ())), preferred_element_type=jnp.float32
+    ).astype(jnp.bfloat16)
+    partial_t = lax.psum_scatter(partial_t, "cc", scatter_dimension=0, tiled=True)
+    d_inputs = lax.psum_scatter(partial_t, "cy", scatter_dimension=0, tiled=True).T
     return (d_inputs, d_w_in, d_w_out)
 
 

time: 206 us -> 216 us (1.049)
  waiting for transfers between devices: 76.4 us -> 87.4 us
    reduce_scatter x0 -> x1, waiting for transfers between devices: none -> 16.8 us  [local(): lax.psum_scatter(partial_t, 'cc', scatter_dimension=0, tiled=True)]
    reduce_scatter x1, waiting for transfers between devices: 9.11 us -> 21.6 us  [local(): lax.psum_scatter(joined, 'sz', scatter_dimension=0, tiled=True)]
    reduce_scatter x1, waiting for transfers between devices: 30.4 us -> 20.4 us  [local(): joined = lax.psum_scatter(joined, 'sx', scatter_dimension=0, tiled=True)]
    unnamed x4 -> x5, waiting for transfers between devices: 37 us -> 28.6 us
    unnamed x10 -> x12, local copies, waits for them, and re-layouts: 8.61 us -> 6.05 us
    dot_general x1, matrix products: 4.53 us -> 6.88 us  [local(): lax.dot_general(cotangent, state_low, (((0,), (1,)), ((), ())), preferred...]
    dot_general x1, matrix products: 8.46 us -> 6.19 us  [local(): lax.dot_general(inputs, drive_grad, (((0,), (1,)), ((), ())), preferred_e...]
  transfers between devices with their start and end apart: 3 -> 4, of which waited for: 3 -> 4; matrix products, arithmetic and copies ran while one was open for 9% -> 8% of each run, Pallas kernels for 0% -> 0%
where the time goes in v2:
time: 216 us; the launch traced here: 215 us
  waiting for transfers between devices  87.4 us (40%)
  matrix products  34.5 us (16%)
  Pallas kernels  32.6 us (15%)
  blocking collectives  25.7 us (12%)
  local copies, waits for them, and re-layouts  15.7 us (7%)
  between operations  14.6 us (7%)
  other arithmetic  3.87 us (2%)
    unnamed x5, waiting for transfers between devices  28.6 us
    reduce_scatter x1, waiting for transfers between devices, local(): lax.psum_scatter(joined, 'sz', scatter_dimension=0, tiled=True)  21.6 us
    pallas_call x1, Pallas kernels, sweeps(): pl.pallas_call(_sweep_kernel, grid=(1,), in_specs=[_whole(g3.shape), _who...  21.1 us
    reduce_scatter x1, waiting for transfers between devices, local(): joined = lax.psum_scatter(joined, 'sx', scatter_dimension=0, tiled=True)  20.4 us
    reduce_scatter x1, waiting for transfers between devices, local(): lax.psum_scatter(partial_t, 'cc', scatter_dimension=0, tiled=True)  16.8 us
    all_gather x1, blocking collectives, local(): lax.all_gather(summary, 'sz')  13.2 us
    all_gather x1, blocking collectives, local(): lax.all_gather(lax.all_gather(summary, 'sz'), 'sx').reshape(peers, 3, width)  12.5 us
    pallas_call x1, Pallas kernels, local_summaries(): pl.pallas_call(_summary_kernel, grid=(1,), in_specs=[_whole(g3.shape), _w...  11.4 us
  transfers between devices with their start and end apart: 4, of which 4 were waited for; matrix products, arithmetic and copies ran while one was open for 8% of the time, Pallas kernels for 0%

profile of v2, /device:TPU:0, one launch (start us, length us, event | category | flops | bytes accessed | tf_op | source)
XLA Modules:
  0.0 214.5 jit_solution(15311008819739807912)
XLA Ops:
  7.2 0.0 copy-start
  7.2 0.0 reduce-scatter.9.cloned.1.call-start
  7.2 0.8 broadcast_multiply_fusion
  8.0 0.8 slice.440
  8.8 0.1 maximum_bitcast_fusion
  8.9 0.5 copy.26.gn_ref
  9.4 1.2 copy.25.g_ref
  10.6 0.0 copy-start.1
  10.6 0.0 copy-start.2
  10.6 0.0 copy-start.3
  10.6 6.6 %fusion.46.refs_4_.refs_5_.refs_6_.refs_7_ = f32[2048,512]{1,0:T(8,128)} fusion(bf16[2048,1024]{1,0:T(8,128)(2,1)} %param.11, bf16[512,1024]{1,0:T(8,128)(2,1)S(1)} %copy-done), kind=kOutput, calls=%fused_computation.164 | convolution fusion | flops 2147483648 | bytes 9437184 | tf_op jit(solution)/shard_map/dot_general | solution.py:147
  17.3 0.0 copy-done.1
  17.3 6.6 %sqrt_multiply_fusion.refs_0_.refs_1_.refs_2_.refs_3_ = f32[2048,512]{1,0:T(8,128)} fusion(bf16[2048,1024]{1,0:T(8,128)(2,1)S(1)} %copy-done.3, bf16[1024,512]{1,0:T(8,128)(2,1)S(1)} %copy-done.2, f32[512]{0:T(512)S(1)} %copy-done.1, f32[2048]{0:T(1024)S(1)} %broadcast_multiply_fusion), kind=kOutput, calls=%fused_computation.6 | convolution fusion | flops 2150629376 | bytes 9447424 | tf_op jit(solution)/shard_map/dot_general | solution.py:146
  23.8 11.4 %shard_map.85 = (f32[16,512]{1,0:T(8,128)S(1)}, f32[16,512]{1,0:T(8,128)S(1)}, f32[16,512]{1,0:T(8,128)S(1)}, f32[16,512]{1,0:T(8,128)S(1)}) custom-call(f32[128,16,1]{2,1,0:T(8,128)S(1)} %copy.25.g_ref, f32[128,16,1]{2,1,0:T(8,128)S(1)} %copy.26.gn_ref, f32[1,512]{1,0:T(1,128)S(1)} %bitcast.479, ...), custom_call_target="tpu_custom_call" | custom-call | tf_op jit(solution)/shard_map/pallas_call | solution.py:109
  35.4 1.2 slice.473
  37.2 0.1 multiply_add_fusion.31
  37.4 13.2 %all-gather.2 = f32[4,3,512]{2,1,0:T(4,128)S(1)} all-gather(f32[1,3,512]{2,1,0:T(4,128)S(1)} %maximum_bitcast_fusion.1), channel_id=2, replica_groups=mesh['sx'=4,'sz'=4,'cy'=4,'cc'=2] {'sz'}, dimensions={0}, use_global_device_ids=true | all-gather | bytes 30720 | tf_op jit(solution)/shard_map/all_gather | solution.py:168
  50.6 12.5 %all-gather.1 = f32[16,3,512]{2,1,0:T(4,128)S(1)} all-gather(f32[4,3,512]{2,1,0:T(4,128)S(1)} %all-gather.2), channel_id=3, replica_groups=mesh['sx'=4,'sz'=4,'cy'=4,'cc'=2] {'sx'}, dimensions={0}, use_global_device_ids=true | all-gather | bytes 122880 | tf_op jit(solution)/shard_map/all_gather | solution.py:168
  63.1 0.1 multiply_add_fusion.1
  63.2 0.1 stack.11.ib_ref
  63.3 0.2 multiply_add_fusion.16
  63.5 0.1 stack.10.if_ref
  63.6 0.0 copy-start.4
  63.6 21.1 %shard_map.86 = (f32[4,2048,128]{2,1,0:T(8,128)}, f32[4,2048,128]{2,1,0:T(8,128)}) custom-call(f32[128,16,1]{2,1,0:T(8,128)S(1)} %copy.25.g_ref, f32[128,16,1]{2,1,0:T(8,128)S(1)} %copy.26.gn_ref, f32[1,512]{1,0:T(1,128)S(1)} %bitcast.480, f32[16,512]{1,0:T(8,128)S(1)} %stack.10.if_ref, f32[16,512]{1,0:T(8,128)S(1)} %stack.11.ib_ref, ...), custom_call_target="tpu_custom_call" | custom-call | tf_op jit(solution)/shard_map/pallas_call | solution.py:125
  84.7 6.2 %multiply_convert_fusion.2 = bf16[4,128,1024]{2,1,0:T(8,128)(2,1)S(1)} fusion(bf16[2048,1024]{1,0:T(8,128)(2,1)S(1)} %copy-done.4, f32[4,2048,128]{2,1,0:T(8,128)} %get-tuple-element.13, f32[4,128]{1,0:T(4,128)S(1)} %bitcast.481, f32[2048]{0:T(1024)S(1)} %broadcast_multiply_fusion), kind=kOutput, calls=%fused_computation.11 | convolution fusion | flops 2152726528 | bytes 9447424 | tf_op jit(solution)/shard_map/dot_general | solution.py:196
  90.9 0.5 copy.30
  91.4 6.9 %multiply_convert_fusion.1 = bf16[4,128,1024]{2,1,0:T(8,128)(2,1)} fusion(bf16[2048,1024]{1,0:T(8,128)(2,1)} %param.11, f32[4,2048,128]{2,1,0:T(8,128)} %get-tuple-element.14), kind=kOutput, calls=%fused_computation.9 | convolution fusion | flops 2149580800 | bytes 9437184 | tf_op jit(solution)/shard_map/dot_general | solution.py:199
  98.3 1.5 copy.31
  99.8 1.6 pad_maximum_fusion
  101.4 0.0 reduce-scatter.9.cloned.1.call-update
  101.5 0.0 reduce-scatter.7.cloned.1.call-start
  101.5 1.3 reshape.1748
  102.9 0.2 copy.27
  103.1 8.3 %fusion.4 = bf16[1024,2048]{0,1:T(8,128)(2,1)} fusion(bf16[1024,4,128]{2,0,1:T(8,128)(2,1)S(1)} %bitcast.485, f32[4,2048,128]{2,1,0:T(8,128)} %get-tuple-element.13, f32[4,128]{1,0:T(4,128)S(1)} %bitcast.482, f32[2048]{0:T(1024)S(1)} %broadcast_multiply_fusion), kind=kOutput, calls=%fused_computation.7 | convolution fusion | flops 2153775104 | bytes 9447424 | tf_op jit(solution)/shard_map/dot_general | solution.py:215
  111.4 0.0 reduce-scatter.7.cloned.1.call-update
  111.4 0.0 reduce-scatter.11.cloned.1.call-start
  111.5 20.4 %reduce-scatter.9.cloned.1.call-done = bf16[256,1024]{1,0:T(8,128)(2,1)} async-done(((bf16[1024,1024]{1,0:T(8,128)(2,1)}), bf16[256,1024]{1,0:T(8,128)(2,1)}) %reduce-scatter.9.cloned.1.call-update) | async-done | bytes 524304 | tf_op jit(solution)/shard_map/reduce_scatter | solution.py:203
  131.9 0.0 reduce-scatter.11.cloned.1.call-update
  131.9 0.0 reduce-scatter.13.cloned.1.call-start
  131.9 16.8 %reduce-scatter.7.cloned.1.call-done = bf16[512,2048]{0,1:T(8,128)(2,1)} async-done(((bf16[1024,2048]{0,1:T(8,128)(2,1)}), bf16[512,2048]{0,1:T(8,128)(2,1)}) %reduce-scatter.7.cloned.1.call-update) | async-done | bytes 2097168 | tf_op jit(solution)/shard_map/reduce_scatter | solution.py:218
  148.7 4.0 %copy.34 = bf16[512,2048]{1,0:T(8,128)(2,1)} copy(bf16[512,2048]{0,1:T(8,128)(2,1)} %reduce-scatter.7.cloned.1.call-done) | data formatting | bytes 4194304
  152.7 0.0 reduce-scatter.13.cloned.1.call-update
  152.7 21.6 %reduce-scatter.11.cloned.1.call-done = bf16[64,1024]{1,0:T(8,128)(2,1)} async-done(((bf16[256,1024]{1,0:T(8,128)(2,1)}), bf16[64,1024]{1,0:T(8,128)(2,1)}) %reduce-scatter.11.cloned.1.call-update) | async-done | bytes 131088 | tf_op jit(solution)/shard_map/reduce_scatter | solution.py:204
  174.3 0.9 convert_element_type.20
  175.2 1.5 slice.604
  176.7 0.7 slice_bitcast_fusion
  177.4 28.5 %reduce-scatter.13.cloned.1.call-done = bf16[128,2048]{1,0:T(8,128)(2,1)} async-done(((bf16[512,2048]{1,0:T(8,128)(2,1)}), bf16[128,2048]{1,0:T(8,128)(2,1)}) %reduce-scatter.13.cloned.1.call-update) | async-done | bytes 524304
  205.9 2.0 copy.35
  (9 shorter events, 0.1 us)
Async XLA Ops:
  7.2 3.4 %copy-start = (bf16[512,1024]{1,0:T(8,128)(2,1)S(1)}, bf16[512,1024]{1,0:T(8,128)(2,1)}, u32[]{:S(2)}) copy-start(bf16[512,1024]{1,0:T(8,128)(2,1)} %param.10) | copy-start | bytes 3145732
  7.2 124.7 %reduce-scatter.9.cloned.1.call-start = ((), (), s32[]{:S(2)}) async-start(), calls=%async_computation.5 | async-start | bytes 2621440 | tf_op jit(solution)/shard_map/reduce_scatter | solution.py:203
  10.6 6.7 %copy-start.1 = (f32[512]{0:T(512)S(1)}, f32[512]{0:T(512)}, u32[]{:S(2)}) copy-start(f32[512]{0:T(512)} %param.8) | copy-start | bytes 6148
  10.6 6.7 %copy-start.2 = (bf16[1024,512]{1,0:T(8,128)(2,1)S(1)}, bf16[1024,512]{1,0:T(8,128)(2,1)}, u32[]{:S(2)}) copy-start(bf16[1024,512]{1,0:T(8,128)(2,1)} %param.9) | copy-start | bytes 3145732
  10.6 6.7 %copy-start.3 = (bf16[2048,1024]{1,0:T(8,128)(2,1)S(1)}, bf16[2048,1024]{1,0:T(8,128)(2,1)}, u32[]{:S(2)}) copy-start(bf16[2048,1024]{1,0:T(8,128)(2,1)} %param.6) | copy-start | bytes 12582916
  63.6 21.1 %copy-start.4 = (bf16[2048,1024]{1,0:T(8,128)(2,1)S(1)}, bf16[2048,1024]{1,0:T(8,128)(2,1)}, u32[]{:S(2)}) copy-start(bf16[2048,1024]{1,0:T(8,128)(2,1)} %param.6) | copy-start | bytes 12582916
  101.5 47.2 %reduce-scatter.7.cloned.1.call-start = ((), (), s32[]{:S(2)}) async-start(), calls=%async_computation.4 | async-start | bytes 6291456 | tf_op jit(solution)/shard_map/reduce_scatter | solution.py:218
  111.4 62.9 %reduce-scatter.11.cloned.1.call-start = ((), (), s32[]{:S(2)}) async-start(), calls=%async_computation.6 | async-start | bytes 655360 | tf_op jit(solution)/shard_map/reduce_scatter | solution.py:204
  131.9 74.0 %reduce-scatter.13.cloned.1.call-start = ((), (), s32[]{:S(2)}) async-start(), calls=%async_computation.7 | async-start | bytes 2621440
Sparse Core Ops, SparseCore 0:
  101.6 30.2 reduce-scatter.8
  134.3 14.3 reduce-scatter.6
  151.1 23.1 reduce-scatter.10
  176.6 29.3 reduce-scatter.12

commit v3 on v1

--- a/solution.py
+++ b/solution.py
@@ -131,6 +131,37 @@
         out_shape=[full, full],
         compiler_params=pltpu.CompilerParams(vmem_limit_bytes=48 * 1024 * 1024),
     )(g3, gn3, rates2, init_f, init_b, *([drive] * chunks), *([up] * chunks))
+
+
+def _pick(x, index):
+    return lax.dynamic_index_in_dim(x, index, 0, keepdims=False)
+
+
+def chan_reduce(partial_t):
+    ys = lax.axis_size("cy")
+    cores = lax.axis_size("cc")
+    y = lax.axis_index("cy")
+    core = lax.axis_index("cc")
+    dmodel, total = partial_t.shape
+    blk = dmodel // (ys * cores)
+    parts = partial_t.reshape(ys, cores, blk, total).transpose(1, 0, 2, 3)
+    mine = _pick(parts, core).astype(jnp.float32)
+    other = _pick(parts, (core + 1) % cores)
+    swap = [(i, (i + 1) % cores) for i in range(cores)]
+    acc = mine + lax.ppermute(other, "cc", swap).astype(jnp.float32)
+    half = total // 2
+    ahead = acc[:, :, :half]
+    behind = acc[:, :, half:]
+    up_ring = [(i, (i + 1) % ys) for i in range(ys)]
+    down_ring = [(i, (i - 1) % ys) for i in range(ys)]
+    buf_a = _pick(ahead, (y - 1) % ys)
+    buf_b = _pick(behind, (y + 1) % ys)
+    for k in range(ys - 1):
+        got_a = lax.ppermute(buf_a.astype(jnp.bfloat16), "cy", up_ring)
+        got_b = lax.ppermute(buf_b.astype(jnp.bfloat16), "cy", down_ring)
+        buf_a = _pick(ahead, (y - k - 2) % ys) + got_a.astype(jnp.float32)
+        buf_b = _pick(behind, (y + k + 2) % ys) + got_b.astype(jnp.float32)
+    return jnp.concatenate([buf_a, buf_b], 1).astype(jnp.bfloat16)
 
 
 def local(inputs, gaps, rates, w_in, w_out, cotangent):
@@ -205,12 +236,10 @@
     d_w_in = joined[:, :width]
     d_w_out = joined[:, width:].T
     w_in3 = w_in.reshape(w_in.shape[0], chunks, LANES)
-    partial_value = lax.dot_general(
-        drive_grad, w_in3, (((0, 2), (1, 2)), ((), ())), preferred_element_type=jnp.float32
-    )
-    d_inputs = lax.psum_scatter(
-        partial_value.astype(jnp.bfloat16), CHAN, scatter_dimension=1, tiled=True
-    )
+    partial_t = lax.dot_general(
+        w_in3, drive_grad, (((1, 2), (0, 2)), ((), ())), preferred_element_type=jnp.float32
+    ).astype(jnp.bfloat16)
+    d_inputs = chan_reduce(partial_t).T
     return (d_inputs, d_w_in, d_w_out)
 
 

time: 206 us -> 175 us (0.85)
  waiting for transfers between devices: 76.4 us -> 18.1 us
  other arithmetic: 3.59 us -> 15.2 us
  starting transfers between devices: 0.12 us -> 10.4 us
  local copies, waits for them, and re-layouts: 16.5 us -> 21.1 us
    unnamed x4 -> x2, waiting for transfers between devices: 37 us -> 0.03 us
    reduce_scatter x1, waiting for transfers between devices: 30.4 us -> 0.01 us  [local(): joined = lax.psum_scatter(joined, 'sx', scatter_dimension=0, tiled=True)]
    ppermute x0 -> x7, waiting for transfers between devices: none -> 14.7 us  [the longest x3 12.3 us: chan_reduce(): got_a = lax.ppermute(buf_a.astype(jnp.bfloat16), 'cy', up_ring)]
    ppermute x0 -> x7, starting transfers between devices: none -> 10.3 us  [the longest x3 8.2 us: chan_reduce(): got_b = lax.ppermute(buf_b.astype(jnp.bfloat16), 'cy', down_ring)]
    another operation x0 -> x2, local copies, waits for them, and re-layouts: none -> 8.31 us
    convert_element_type x0 -> x4, other arithmetic: none -> 5.77 us  [the longest x2 3.42 us: chan_reduce(): got_b = lax.ppermute(buf_b.astype(jnp.bfloat16), 'cy', down_ring)]
    reduce_scatter x1, waiting for transfers between devices: 9.11 us -> 3.41 us  [local(): lax.psum_scatter(joined, 'sz', scatter_dimension=0, tiled=True)]
    unnamed x10 -> x11, local copies, waits for them, and re-layouts: 8.61 us -> 3.93 us
  transfers between devices with their start and end apart: 3 -> 9, of which waited for: 3 -> 6; matrix products, arithmetic and copies ran while one was open for 9% -> 18% of each run, Pallas kernels for 0% -> 0%
where the time goes in v3:
time: 175 us; the launch traced here: 174 us
  matrix products  34.5 us (20%)
  Pallas kernels  34.1 us (19%)
  blocking collectives  25.7 us (15%)
  local copies, waits for them, and re-layouts  21.1 us (12%)
  waiting for transfers between devices  18.1 us (10%)
  other arithmetic  15.2 us (9%)
  between operations  14.9 us (9%)
  starting transfers between devices  10.4 us (6%)
    pallas_call x1, Pallas kernels, sweeps(): pl.pallas_call(_sweep_kernel, grid=(1,), in_specs=[_whole(g3.shape), _who...  21.8 us
    all_gather x1, blocking collectives, local(): lax.all_gather(summary, 'sz')  13.2 us
    all_gather x1, blocking collectives, local(): lax.all_gather(lax.all_gather(summary, 'sz'), 'sx').reshape(peers, 3, width)  12.5 us
    ppermute x3, waiting for transfers between devices, chan_reduce(): got_a = lax.ppermute(buf_a.astype(jnp.bfloat16), 'cy', up_ring)  12.3 us
    pallas_call x1, Pallas kernels, local_summaries(): pl.pallas_call(_summary_kernel, grid=(1,), in_specs=[_whole(g3.shape), _w...  12.3 us
    another operation x2, local copies, waits for them, and re-layouts  8.31 us
    ppermute x3, starting transfers between devices, chan_reduce(): got_b = lax.ppermute(buf_b.astype(jnp.bfloat16), 'cy', down_ring)  8.2 us
    dot_general x1, matrix products, local(): lax.dot_general(w_in3, drive_grad, (((1, 2), (0, 2)), ((), ())), preferre...  7.95 us
  transfers between devices with their start and end apart: 9, of which 6 were waited for; matrix products, arithmetic and copies ran while one was open for 18% of the time, Pallas kernels for 0%

profile of v3, /device:TPU:0, one launch (start us, length us, event | category | flops | bytes accessed | tf_op | source)
XLA Modules:
  0.0 174.0 jit_solution(15135261832905510924)
XLA Ops:
  7.2 0.8 broadcast_multiply_fusion
  8.0 0.8 slice.310
  8.8 0.7 reshape.1241
  9.5 1.2 slice.327
  10.8 0.4 copy.30.gn_ref
  11.2 0.4 copy.29.g_ref
  11.7 6.9 %fusion.54.refs_4_.refs_5_.refs_6_.refs_7_ = f32[2048,512]{1,0:T(8,128)} fusion(bf16[2048,1024]{1,0:T(8,128)(2,1)} %param.11, bf16[512,1024]{1,0:T(8,128)(2,1)} %param.10), kind=kOutput, calls=%fused_computation.168 | convolution fusion | flops 2147483648 | bytes 9437184 | tf_op jit(solution)/shard_map/dot_general | solution.py:178
  18.6 6.6 %sqrt_multiply_fusion.refs_0_.refs_1_.refs_2_.refs_3_ = f32[2048,512]{1,0:T(8,128)} fusion(bf16[2048,1024]{1,0:T(8,128)(2,1)S(1)} %copy-done.3, bf16[1024,512]{1,0:T(8,128)(2,1)S(1)} %copy-done, f32[512]{0:T(512)S(1)} %copy-done.1, f32[2048]{0:T(1024)S(1)} %broadcast_multiply_fusion), kind=kOutput, calls=%fused_computation.7 | convolution fusion | flops 2150629376 | bytes 9447424 | tf_op jit(solution)/shard_map/dot_general | solution.py:177
  25.2 12.3 %shard_map.85 = (f32[8,512]{1,0:T(8,128)S(1)}, f32[8,512]{1,0:T(8,128)S(1)}, f32[8,512]{1,0:T(8,128)S(1)}, f32[8,512]{1,0:T(8,128)S(1)}) custom-call(f32[256,8,1]{2,1,0:T(8,128)S(1)} %copy.29.g_ref, f32[256,8,1]{2,1,0:T(8,128)S(1)} %copy.30.gn_ref, f32[1,512]{1,0:T(1,128)S(1)} %bitcast.493, f32[2048,512]{1,0:T(8,128)} %sqrt_multiply_fusion.refs_0_.refs_1_.refs_2_.refs_3_, ...), custom_call_target="tpu_custom_call" | custom-call | tf_op jit(solution)/shard_map/pallas_call | solution.py:109
  38.3 13.2 %all-gather.2 = f32[4,3,512]{2,1,0:T(4,128)S(1)} all-gather(f32[1,3,512]{2,1,0:T(4,128)S(1)} %maximum_bitcast_fusion.1), channel_id=2, replica_groups=mesh['sx'=4,'sz'=4,'cy'=4,'cc'=2] {'sz'}, dimensions={0}, use_global_device_ids=true | all-gather | bytes 30720 | tf_op jit(solution)/shard_map/all_gather | solution.py:199
  51.5 12.5 %all-gather.1 = f32[16,3,512]{2,1,0:T(4,128)S(1)} all-gather(f32[4,3,512]{2,1,0:T(4,128)S(1)} %all-gather.2), channel_id=3, replica_groups=mesh['sx'=4,'sz'=4,'cy'=4,'cc'=2] {'sx'}, dimensions={0}, use_global_device_ids=true | all-gather | bytes 122880 | tf_op jit(solution)/shard_map/all_gather | solution.py:199
  64.0 0.1 multiply_add_fusion.1
  64.2 0.1 multiply_add_fusion.8
  64.3 21.8 %shard_map.86 = (f32[4,2048,128]{2,1,0:T(8,128)}, f32[4,2048,128]{2,1,0:T(8,128)}) custom-call(f32[256,8,1]{2,1,0:T(8,128)S(1)} %copy.29.g_ref, f32[256,8,1]{2,1,0:T(8,128)S(1)} %copy.30.gn_ref, f32[1,512]{1,0:T(1,128)S(1)} %bitcast.494, f32[8,512]{1,0:T(8,128)S(1)} %stack.10.if_ref, f32[8,512]{1,0:T(8,128)S(1)} %stack.11.ib_ref, ...), custom_call_target="tpu_custom_call" | custom-call | tf_op jit(solution)/shard_map/pallas_call | solution.py:125
  86.1 6.2 %multiply_convert_fusion.2 = bf16[4,128,1024]{2,1,0:T(8,128)(2,1)S(1)} fusion(bf16[2048,1024]{1,0:T(8,128)(2,1)S(1)} %copy-done.4, f32[4,2048,128]{2,1,0:T(8,128)} %get-tuple-element.13, f32[4,128]{1,0:T(4,128)S(1)} %bitcast.495, f32[2048]{0:T(1024)S(1)} %broadcast_multiply_fusion), kind=kOutput, calls=%fused_computation.11 | convolution fusion | flops 2152726528 | bytes 9447424 | tf_op jit(solution)/shard_map/dot_general | solution.py:227
  92.3 0.5 copy.36
  92.8 6.9 %multiply_convert_fusion.1 = bf16[4,128,1024]{2,1,0:T(8,128)(2,1)} fusion(bf16[2048,1024]{1,0:T(8,128)(2,1)} %param.11, f32[4,2048,128]{2,1,0:T(8,128)} %get-tuple-element.14), kind=kOutput, calls=%fused_computation.9 | convolution fusion | flops 2149580800 | bytes 9437184 | tf_op jit(solution)/shard_map/dot_general | solution.py:230
  99.7 1.5 copy.37
  101.2 1.7 pad_maximum_fusion
  102.9 8.0 %bitcast_convert_fusion = bf16[2048,1024]{0,1:T(8,128)(2,1)} fusion(f32[4,2048,128]{2,1,0:T(8,128)} %get-tuple-element.13, f32[4,128]{1,0:T(4,128)S(1)} %bitcast.496, f32[2048]{0:T(1024)S(1)} %broadcast_multiply_fusion, bf16[1024,512]{1,0:T(8,128)(2,1)S(1)} %copy-done), kind=kOutput, calls=%fused_computation | convolution fusion | flops 2153775104 | bytes 9447424 | tf_op jit(solution)/shard_map/dot_general | solution.py:239
  110.9 4.4 %constant_dynamic-slice_fusion.1 = (bf16[4,1,128,2048]{3,2,1,0:T(8,128)(2,1)S(1)}, bf16[4,1,128,2048]{3,2,1,0:T(8,128)(2,1)}) fusion(bf16[4,2,128,2048]{3,2,1,0:T(8,128)(2,1)} %bitcast.497, s32[]{:T(128)S(6)} %select_n.777, s32[]{:T(128)S(6)} %select_n.779), kind=kLoop, calls=%fused_computation.68 | loop fusion | bytes 8388616 | tf_op jit(solution)/shard_map/dynamic-slice
  115.2 3.9 %copy.33 = bf16[4,1,128,2048]{2,3,0,1:T(8,128)(2,1)} copy(bf16[4,1,128,2048]{3,2,1,0:T(8,128)(2,1)} %get-tuple-element.34) | data formatting | bytes 4194304 | tf_op jit(solution)/shard_map/dynamic-slice.1
  119.2 2.6 %copy.40 = bf16[4,1,128,2048]{2,3,0,1:T(8,128)(2,1)} copy(bf16[4,1,128,2048]{3,2,1,0:T(8,128)(2,1)S(1)} %get-tuple-element.33) | data formatting | bytes 4194304
  121.8 1.9 %collective-permute-done = bf16[4,128,2048]{1,2,0:T(8,128)(2,1)} collective-permute-done((bf16[4,128,2048]{1,2,0:T(8,128)(2,1)}, bf16[4,128,2048]{1,2,0:T(8,128)(2,1)}, u32[]{:S(2)}, u32[]{:S(2)}) %collective-permute-start) | collective-permute-done | bytes 2097184 | tf_op jit(solution)/shard_map/ppermute | solution.py:151
  123.7 2.7 %convert_add_fusion = f32[4,128,2048]{1,2,0:T(8,128)S(1)} fusion(bf16[4,128,2048]{1,2,0:T(8,128)(2,1)} %collective-permute-done, bf16[4,1,128,2048]{2,3,0,1:T(8,128)(2,1)} %copy.40), kind=kLoop, calls=%fused_computation.1 | loop fusion | flops 3145728 | bytes 8388608 | tf_op jit(solution)/shard_map/add | solution.py:151
  126.4 0.3 fusion.53
  126.7 1.3 copy-done.2
  128.0 1.6 collective-permute-start.1
  129.7 0.7 fusion.20
  130.4 1.7 collective-permute-start.4
  132.1 5.8 %collective-permute-done.1 = bf16[128,1024]{0,1:T(8,128)(2,1)} collective-permute-done((bf16[128,1024]{0,1:T(8,128)(2,1)S(1)}, bf16[128,1024]{0,1:T(8,128)(2,1)}, u32[]{:S(2)}, u32[]{:S(2)}) %collective-permute-start.1) | collective-permute-done | bytes 262176 | tf_op jit(solution)/shard_map/ppermute | solution.py:160
  137.8 1.2 fusion.16
  139.0 0.4 collective-permute-start.2
  139.4 1.7 fusion.13
  141.1 2.9 %collective-permute-start.5 = (bf16[128,1024]{0,1:T(8,128)(2,1)}, bf16[128,1024]{0,1:T(8,128)(2,1)}, u32[]{:S(2)}, u32[]{:S(2)}) collective-permute-start(bf16[128,1024]{0,1:T(8,128)(2,1)} %fusion.13), channel_id=1, source_target_pairs={{0,6},{2,0},{4,2},{6,4},{1,7},{3,1},{5,3},{7,5},{8,14},{10,8},{12,... | collective-permute-start | bytes 786440 | tf_op jit(solution)/shard_map/ppermute | solution.py:161
  144.1 3.9 %collective-permute-done.2 = bf16[128,1024]{0,1:T(8,128)(2,1)} collective-permute-done((bf16[128,1024]{0,1:T(8,128)(2,1)S(1)}, bf16[128,1024]{0,1:T(8,128)(2,1)}, u32[]{:S(2)}, u32[]{:S(2)}) %collective-permute-start.2) | collective-permute-done | bytes 262176 | tf_op jit(solution)/shard_map/ppermute | solution.py:160
  148.0 1.2 fusion.17
  149.2 1.7 fusion.14
  150.9 3.6 %collective-permute-start.6 = (bf16[128,1024]{0,1:T(8,128)(2,1)}, bf16[128,1024]{0,1:T(8,128)(2,1)}, u32[]{:S(2)}, u32[]{:S(2)}) collective-permute-start(bf16[128,1024]{0,1:T(8,128)(2,1)} %fusion.14), channel_id=1, source_target_pairs={{0,6},{2,0},{4,2},{6,4},{1,7},{3,1},{5,3},{7,5},{8,14},{10,8},{12,... | collective-permute-start | bytes 786440 | tf_op jit(solution)/shard_map/ppermute | solution.py:161
  154.5 2.7 %collective-permute-done.3 = bf16[128,1024]{0,1:T(8,128)(2,1)} collective-permute-done((bf16[128,1024]{0,1:T(8,128)(2,1)S(1)}, bf16[128,1024]{0,1:T(8,128)(2,1)}, u32[]{:S(2)}, u32[]{:S(2)}) %collective-permute-start.3) | collective-permute-done | bytes 262176 | tf_op jit(solution)/shard_map/ppermute | solution.py:160
  157.2 1.2 fusion.18
  158.4 0.4 collective-permute-done.6
  158.8 1.0 fusion.15
  159.8 0.8 maximum_bitcast_fusion
  160.6 3.4 %reduce-scatter.5.cloned.1.call-done = bf16[64,1024]{1,0:T(8,128)(2,1)} async-done(((bf16[256,1024]{1,0:T(8,128)(2,1)}), bf16[64,1024]{1,0:T(8,128)(2,1)}) %reduce-scatter.5.cloned.1.call-update) | async-done | bytes 131088 | tf_op jit(solution)/shard_map/reduce_scatter | solution.py:235
  164.0 0.9 convert_element_type.89
  165.0 0.7 slice_bitcast_fusion
  165.6 1.5 slice.446
  (28 shorter events, 0.5 us)
Async XLA Ops:
  7.2 11.5 %copy-start = (bf16[1024,512]{1,0:T(8,128)(2,1)S(1)}, bf16[1024,512]{1,0:T(8,128)(2,1)}, u32[]{:S(2)}) copy-start(bf16[1024,512]{1,0:T(8,128)(2,1)} %param.9) | copy-start | bytes 3145732
  7.2 136.8 %reduce-scatter.3.cloned.1.call-start = ((), (), s32[]{:S(2)}) async-start(), calls=%async_computation.2 | async-start | bytes 2621440 | tf_op jit(solution)/shard_map/reduce_scatter | solution.py:234
  11.6 7.0 %copy-start.1 = (f32[512]{0:T(512)S(1)}, f32[512]{0:T(512)}, u32[]{:S(2)}) copy-start(f32[512]{0:T(512)} %param.8) | copy-start | bytes 6148
  11.7 7.0 %copy-start.3 = (bf16[2048,1024]{1,0:T(8,128)(2,1)S(1)}, bf16[2048,1024]{1,0:T(8,128)(2,1)}, u32[]{:S(2)}) copy-start(bf16[2048,1024]{1,0:T(8,128)(2,1)} %param.6) | copy-start | bytes 12582916
  64.3 21.8 %copy-start.4 = (bf16[2048,1024]{1,0:T(8,128)(2,1)S(1)}, bf16[2048,1024]{1,0:T(8,128)(2,1)}, u32[]{:S(2)}) copy-start(bf16[2048,1024]{1,0:T(8,128)(2,1)} %param.6) | copy-start | bytes 12582916
  102.9 61.2 %reduce-scatter.5.cloned.1.call-start = ((), (), s32[]{:S(2)}) async-start(), calls=%async_computation.3 | async-start | bytes 655360 | tf_op jit(solution)/shard_map/reduce_scatter | solution.py:235
  119.2 4.5 %collective-permute-start = (bf16[4,128,2048]{1,2,0:T(8,128)(2,1)}, bf16[4,128,2048]{1,2,0:T(8,128)(2,1)}, u32[]{:S(2)}, u32[]{:S(2)}) collective-permute-start(bf16[4,128,2048]{1,2,0:T(8,128)(2,1)} %bitcast.499), channel_id=1, source_target_pairs={{0,1},{1,0},{2,3},{3,2},{4,5},{5,4},{6,7},{7,6},{8,9},{9,8},{10,11... | collective-permute-start | bytes 6291464 | tf_op jit(solution)/shard_map/ppermute | solution.py:151
  126.7 1.3 copy-start.2
  128.0 9.8 %collective-permute-start.1 = (bf16[128,1024]{0,1:T(8,128)(2,1)S(1)}, bf16[128,1024]{0,1:T(8,128)(2,1)}, u32[]{:S(2)}, u32[]{:S(2)}) collective-permute-start(bf16[128,1024]{0,1:T(8,128)(2,1)S(1)} %fusion.19), channel_id=1, source_target_pairs={{0,2},{2,4},{4,6},{6,0},{1,3},{3,5},{5,7},{7,1},{8,10},{10,12},{12... | collective-permute-start | bytes 786440 | tf_op jit(solution)/shard_map/ppermute | solution.py:160
  130.4 9.0 %collective-permute-start.4 = (bf16[128,1024]{0,1:T(8,128)(2,1)}, bf16[128,1024]{0,1:T(8,128)(2,1)}, u32[]{:S(2)}, u32[]{:S(2)}) collective-permute-start(bf16[128,1024]{0,1:T(8,128)(2,1)} %fusion.20), channel_id=1, source_target_pairs={{0,6},{2,0},{4,2},{6,4},{1,7},{3,1},{5,3},{7,5},{8,14},{10,8},{12,... | collective-permute-start | bytes 786440 | tf_op jit(solution)/shard_map/ppermute | solution.py:161
  139.0 8.9 %collective-permute-start.2 = (bf16[128,1024]{0,1:T(8,128)(2,1)S(1)}, bf16[128,1024]{0,1:T(8,128)(2,1)}, u32[]{:S(2)}, u32[]{:S(2)}) collective-permute-start(bf16[128,1024]{0,1:T(8,128)(2,1)S(1)} %fusion.16), channel_id=1, source_target_pairs={{0,2},{2,4},{4,6},{6,0},{1,3},{3,5},{5,7},{7,1},{8,10},{10,12},{12... | collective-permute-start | bytes 786440 | tf_op jit(solution)/shard_map/ppermute | solution.py:160
  141.1 8.1 %collective-permute-start.5 = (bf16[128,1024]{0,1:T(8,128)(2,1)}, bf16[128,1024]{0,1:T(8,128)(2,1)}, u32[]{:S(2)}, u32[]{:S(2)}) collective-permute-start(bf16[128,1024]{0,1:T(8,128)(2,1)} %fusion.13), channel_id=1, source_target_pairs={{0,6},{2,0},{4,2},{6,4},{1,7},{3,1},{5,3},{7,5},{8,14},{10,8},{12,... | collective-permute-start | bytes 786440 | tf_op jit(solution)/shard_map/ppermute | solution.py:161
  149.1 8.1 %collective-permute-start.3 = (bf16[128,1024]{0,1:T(8,128)(2,1)S(1)}, bf16[128,1024]{0,1:T(8,128)(2,1)}, u32[]{:S(2)}, u32[]{:S(2)}) collective-permute-start(bf16[128,1024]{0,1:T(8,128)(2,1)S(1)} %fusion.17), channel_id=1, source_target_pairs={{0,2},{2,4},{4,6},{6,0},{1,3},{3,5},{5,7},{7,1},{8,10},{10,12},{12... | collective-permute-start | bytes 786440 | tf_op jit(solution)/shard_map/ppermute | solution.py:160
  150.9 7.9 %collective-permute-start.6 = (bf16[128,1024]{0,1:T(8,128)(2,1)}, bf16[128,1024]{0,1:T(8,128)(2,1)}, u32[]{:S(2)}, u32[]{:S(2)}) collective-permute-start(bf16[128,1024]{0,1:T(8,128)(2,1)} %fusion.14), channel_id=1, source_target_pairs={{0,6},{2,0},{4,2},{6,4},{1,7},{3,1},{5,3},{7,5},{8,14},{10,8},{12,... | collective-permute-start | bytes 786440 | tf_op jit(solution)/shard_map/ppermute | solution.py:161
Sparse Core Ops, SparseCore 0:
  103.0 30.2 reduce-scatter.2
  144.2 19.8 reduce-scatter.4

commit v4 on v1

--- a/solution.py
+++ b/solution.py
@@ -131,6 +131,54 @@
         out_shape=[full, full],
         compiler_params=pltpu.CompilerParams(vmem_limit_bytes=48 * 1024 * 1024),
     )(g3, gn3, rates2, init_f, init_b, *([drive] * chunks), *([up] * chunks))
+
+
+def _pick(x, index, axis=0):
+    return lax.dynamic_index_in_dim(x, index, axis, keepdims=False)
+
+
+def chan_reduce(w_in, drive_grad):
+    ys = lax.axis_size("cy")
+    cores = lax.axis_size("cc")
+    y = lax.axis_index("cy")
+    core = lax.axis_index("cc")
+    dmodel, width = w_in.shape
+    chunks, total, lanes = drive_grad.shape
+    blk = dmodel // (ys * cores)
+    w_parts = w_in.reshape(ys, cores, blk, chunks, lanes)
+
+    def product(index):
+        rows = _pick(w_parts, index, 1)
+        return jnp.stack([
+            lax.dot_general(
+                drive_grad, rows[j], (((0, 2), (1, 2)), ((), ())),
+                preferred_element_type=jnp.float32,
+            ).astype(jnp.bfloat16)
+            for j in range(ys)
+        ], 0)
+
+    other = product((core + 1) % cores)
+    swap = [(i, (i + 1) % cores) for i in range(cores)]
+    got = lax.ppermute(other, "cc", swap)
+    kept = product(core)
+    half = total // 2
+
+    def own(index, rows):
+        return (_pick(kept, index)[rows].astype(jnp.float32)
+                + _pick(got, index)[rows].astype(jnp.float32))
+
+    first = slice(0, half)
+    second = slice(half, total)
+    up_ring = [(i, (i + 1) % ys) for i in range(ys)]
+    down_ring = [(i, (i - 1) % ys) for i in range(ys)]
+    buf_a = own((y - 1) % ys, first)
+    buf_b = own((y + 1) % ys, second)
+    for k in range(ys - 1):
+        got_a = lax.ppermute(buf_a.astype(jnp.bfloat16), "cy", up_ring)
+        got_b = lax.ppermute(buf_b.astype(jnp.bfloat16), "cy", down_ring)
+        buf_a = own((y - k - 2) % ys, first) + got_a.astype(jnp.float32)
+        buf_b = own((y + k + 2) % ys, second) + got_b.astype(jnp.float32)
+    return jnp.concatenate([buf_a, buf_b], 0).astype(jnp.bfloat16)
 
 
 def local(inputs, gaps, rates, w_in, w_out, cotangent):
@@ -204,13 +252,7 @@
     joined = lax.psum_scatter(joined, "sz", scatter_dimension=0, tiled=True).astype(jnp.float32)
     d_w_in = joined[:, :width]
     d_w_out = joined[:, width:].T
-    w_in3 = w_in.reshape(w_in.shape[0], chunks, LANES)
-    partial_value = lax.dot_general(
-        drive_grad, w_in3, (((0, 2), (1, 2)), ((), ())), preferred_element_type=jnp.float32
-    )
-    d_inputs = lax.psum_scatter(
-        partial_value.astype(jnp.bfloat16), CHAN, scatter_dimension=1, tiled=True
-    )
+    d_inputs = chan_reduce(w_in, drive_grad)
     return (d_inputs, d_w_in, d_w_out)
 
 

time: 206 us -> 189 us (0.917)
  waiting for transfers between devices: 76.4 us -> 39.2 us
  other arithmetic: 3.59 us -> 23.5 us
  starting transfers between devices: 0.12 us -> 6.11 us
  matrix products: 34.8 us -> 30.1 us
    unnamed x4 -> x2, waiting for transfers between devices: 37 us -> 0.03 us
    ppermute x0 -> x7, waiting for transfers between devices: none -> 35 us  [the longest x3 22.4 us: chan_reduce(): got_a = lax.ppermute(buf_a.astype(jnp.bfloat16), 'cy', up_ring)]
    reduce_scatter x1, waiting for transfers between devices: 30.4 us -> 0.01 us  [local(): joined = lax.psum_scatter(joined, 'sx', scatter_dimension=0, tiled=True)]
    convert_element_type x0 -> x5, other arithmetic: none -> 12.3 us  [the longest x3 5.54 us: chan_reduce(): got_a = lax.ppermute(buf_a.astype(jnp.bfloat16), 'cy', up_ring)]
    unnamed x10, local copies, waits for them, and re-layouts: 8.61 us -> 0.03 us
    ppermute x0 -> x7, starting transfers between devices: none -> 6.04 us  [the longest x3 4.15 us: chan_reduce(): got_b = lax.ppermute(buf_b.astype(jnp.bfloat16), 'cy', down_ring)]
    another operation x0 -> x4, other arithmetic: none -> 5.12 us
    dot_general x1, matrix products: 8.46 us -> 3.36 us  [local(): lax.dot_general(inputs, drive_grad, (((0,), (1,)), ((), ())), preferred_e...]
  transfers between devices with their start and end apart: 3 -> 9, of which waited for: 3 -> 7; matrix products, arithmetic and copies ran while one was open for 9% -> 13% of each run, Pallas kernels for 0% -> 0%
where the time goes in v4:
time: 189 us; the launch traced here: 188 us
  waiting for transfers between devices  39.2 us (21%)
  Pallas kernels  33.9 us (18%)
  matrix products  30.1 us (16%)
  blocking collectives  25.7 us (14%)
  other arithmetic  23.5 us (12%)
  between operations  14.9 us (8%)
  local copies, waits for them, and re-layouts  14.8 us (8%)
  starting transfers between devices  6.11 us (3%)
    ppermute x3, waiting for transfers between devices, chan_reduce(): got_a = lax.ppermute(buf_a.astype(jnp.bfloat16), 'cy', up_ring)  22.4 us
    pallas_call x1, Pallas kernels, sweeps(): pl.pallas_call(_sweep_kernel, grid=(1,), in_specs=[_whole(g3.shape), _who...  21.6 us
    all_gather x1, blocking collectives, local(): lax.all_gather(summary, 'sz')  13.2 us
    all_gather x1, blocking collectives, local(): lax.all_gather(lax.all_gather(summary, 'sz'), 'sx').reshape(peers, 3, width)  12.5 us
    pallas_call x1, Pallas kernels, local_summaries(): pl.pallas_call(_summary_kernel, grid=(1,), in_specs=[_whole(g3.shape), _w...  12.3 us
    ppermute x3, waiting for transfers between devices, chan_reduce(): got_b = lax.ppermute(buf_b.astype(jnp.bfloat16), 'cy', down_ring)  12.1 us
    dot_general x1, matrix products, local(): lax.dot_general(cotangent, state_low, (((0,), (1,)), ((), ())), preferred...  6.83 us
    dot_general x1, matrix products, local(): lax.dot_general(cotangent, w_out, (((1,), (1,)), ((), ())), preferred_ele...  6.7 us
  transfers between devices with their start and end apart: 9, of which 7 were waited for; matrix products, arithmetic and copies ran while one was open for 13% of the time, Pallas kernels for 0%

profile of v4, /device:TPU:0, one launch (start us, length us, event | category | flops | bytes accessed | tf_op | source)
XLA Modules:
  0.0 188.3 jit_solution(15573296101298674319)
XLA Ops:
  7.2 0.8 broadcast_multiply_fusion
  8.0 0.8 slice.400
  8.8 0.7 reshape.1288
  9.5 1.2 slice.417
  10.8 0.4 copy.26.gn_ref
  11.2 0.4 copy.25.g_ref
  11.7 6.7 %fusion.67.refs_4_.refs_5_.refs_6_.refs_7_ = f32[2048,512]{1,0:T(8,128)} fusion(bf16[2048,1024]{1,0:T(8,128)(2,1)} %param.11, bf16[512,1024]{1,0:T(8,128)(2,1)S(1)} %copy-done), kind=kOutput, calls=%fused_computation.203 | convolution fusion | flops 2147483648 | bytes 9437184 | tf_op jit(solution)/shard_map/dot_general | solution.py:195
  18.4 6.6 %sqrt_multiply_fusion.refs_0_.refs_1_.refs_2_.refs_3_ = f32[2048,512]{1,0:T(8,128)} fusion(bf16[2048,1024]{1,0:T(8,128)(2,1)S(1)} %copy-done.3, bf16[1024,512]{1,0:T(8,128)(2,1)S(1)} %copy-done.2, f32[512]{0:T(512)S(1)} %copy-done.1, f32[2048]{0:T(1024)S(1)} %broadcast_multiply_fusion), kind=kOutput, calls=%fused_computation.5 | convolution fusion | flops 2150629376 | bytes 9447424 | tf_op jit(solution)/shard_map/dot_general | solution.py:194
  25.0 12.3 %shard_map.85 = (f32[8,512]{1,0:T(8,128)S(1)}, f32[8,512]{1,0:T(8,128)S(1)}, f32[8,512]{1,0:T(8,128)S(1)}, f32[8,512]{1,0:T(8,128)S(1)}) custom-call(f32[256,8,1]{2,1,0:T(8,128)S(1)} %copy.25.g_ref, f32[256,8,1]{2,1,0:T(8,128)S(1)} %copy.26.gn_ref, f32[1,512]{1,0:T(1,128)S(1)} %bitcast.572, f32[2048,512]{1,0:T(8,128)} %sqrt_multiply_fusion.refs_0_.refs_1_.refs_2_.refs_3_, ...), custom_call_target="tpu_custom_call" | custom-call | tf_op jit(solution)/shard_map/pallas_call | solution.py:109
  38.1 13.2 %all-gather.2 = f32[4,3,512]{2,1,0:T(4,128)S(1)} all-gather(f32[1,3,512]{2,1,0:T(4,128)S(1)} %maximum_bitcast_fusion), channel_id=2, replica_groups=mesh['sx'=4,'sz'=4,'cy'=4,'cc'=2] {'sz'}, dimensions={0}, use_global_device_ids=true | all-gather | bytes 30720 | tf_op jit(solution)/shard_map/all_gather | solution.py:216
  51.3 12.5 %all-gather.1 = f32[16,3,512]{2,1,0:T(4,128)S(1)} all-gather(f32[4,3,512]{2,1,0:T(4,128)S(1)} %all-gather.2), channel_id=3, replica_groups=mesh['sx'=4,'sz'=4,'cy'=4,'cc'=2] {'sx'}, dimensions={0}, use_global_device_ids=true | all-gather | bytes 122880 | tf_op jit(solution)/shard_map/all_gather | solution.py:216
  64.1 21.6 %shard_map.86 = (f32[4,2048,128]{2,1,0:T(8,128)}, f32[4,2048,128]{2,1,0:T(8,128)}) custom-call(f32[256,8,1]{2,1,0:T(8,128)S(1)} %copy.25.g_ref, f32[256,8,1]{2,1,0:T(8,128)S(1)} %copy.26.gn_ref, f32[1,512]{1,0:T(1,128)S(1)} %bitcast.573, f32[8,512]{1,0:T(8,128)S(1)} %stack.30.if_ref, f32[8,512]{1,0:T(8,128)S(1)} %stack.31.ib_ref, ...), custom_call_target="tpu_custom_call" | custom-call | tf_op jit(solution)/shard_map/pallas_call | solution.py:125
  85.7 5.0 %multiply_convert_fusion = bf16[4,2048,128]{2,1,0:T(8,128)(2,1)S(1)} fusion(f32[4,2048,128]{2,1,0:T(8,128)} %get-tuple-element.13, f32[4,128]{1,0:T(4,128)S(1)} %bitcast.574, f32[2048]{0:T(1024)S(1)} %broadcast_multiply_fusion), kind=kLoop, calls=%fused_computation.4 | loop fusion | flops 4194304 | bytes 6301696 | tf_op jit(solution)/shard_map/convert_element_type | solution.py:242
  90.7 3.4 %multiply_convert_fusion.2 = bf16[4,128,1024]{2,1,0:T(8,128)(2,1)} fusion(bf16[4,2048,128]{2,1,0:T(8,128)(2,1)S(1)} %multiply_convert_fusion, bf16[2048,1024]{1,0:T(8,128)(2,1)S(1)} %copy-done.4), kind=kOutput, calls=%fused_computation.35 | convolution fusion | flops 2148532224 | bytes 7340032 | tf_op jit(solution)/shard_map/dot_general | solution.py:244
  94.0 2.3 %copy.31 = bf16[1024,512]{1,0:T(8,128)(2,1)} copy(bf16[1024,512]{0,1:T(8,128)(2,1)} %bitcast.576) | data formatting | bytes 2097152 | tf_op jit(solution)/shard_map/mul | solution.py:244
  96.3 6.8 %multiply_convert_fusion.1 = bf16[4,128,1024]{2,1,0:T(8,128)(2,1)} fusion(bf16[2048,1024]{1,0:T(8,128)(2,1)} %param.11, f32[4,2048,128]{2,1,0:T(8,128)} %get-tuple-element.14), kind=kOutput, calls=%fused_computation.33 | convolution fusion | flops 2149580800 | bytes 9437184 | tf_op jit(solution)/shard_map/dot_general | solution.py:247
  103.1 2.3 %copy.32 = bf16[1024,512]{1,0:T(8,128)(2,1)} copy(bf16[1024,512]{0,1:T(8,128)(2,1)} %bitcast.575) | data formatting | bytes 2097152 | tf_op jit(solution)/shard_map/mul | solution.py:247
  105.4 3.1 %pad_maximum_fusion.2 = bf16[1024,1024]{1,0:T(8,128)(2,1)} fusion(bf16[1024,512]{1,0:T(8,128)(2,1)} %copy.32, bf16[1024,512]{1,0:T(8,128)(2,1)} %copy.31), kind=kLoop, calls=%fused_computation.32 | loop fusion | flops 4194304 | bytes 4194304 | tf_op jit(solution)/shard_map/concatenate | solution.py:250
  108.7 2.1 %reshape.1291 = bf16[4,2,128,4,128]{4,3,2,1,0:T(4,128)(2,1)} reshape(bf16[1024,512]{1,0:T(8,128)(2,1)} %param.9) | data formatting | bytes 2097152 | tf_op jit(solution)/shard_map/reshape | solution.py:148
  110.8 2.3 %constant_dynamic-slice_fusion = (bf16[1,1,128,4,128]{4,3,2,1,0:T(4,128)(2,1)S(1)}, bf16[1,1,128,4,128]{4,3,2,1,0:T(4,128)(2,1)S(1)}, bf16[1,1,128,4,128]{4,3,2,...) fusion(bf16[4,2,128,4,128]{4,3,2,1,0:T(4,128)(2,1)} %reshape.12, ...), kind=kLoop, calls=%fused_computation.64 | loop fusion | bytes 2097172 | tf_op jit(solution)/shard_map/slice | solution.py:154
  113.1 0.7 fusion.13
  113.8 0.7 fusion.14
  114.5 0.7 fusion.15
  115.2 0.7 fusion.12
  115.9 1.6 pad_maximum_fusion.1
  117.6 1.6 fusion.16
  119.2 0.7 fusion.17
  119.9 0.7 fusion.18
  120.6 0.7 fusion.19
  122.1 1.9 fusion.33
  123.9 1.6 collective-permute-start.1
  125.5 8.4 %collective-permute-done.1 = bf16[1024,128]{1,0:T(8,128)(2,1)} collective-permute-done((bf16[1024,128]{1,0:T(8,128)(2,1)}, bf16[1024,128]{1,0:T(8,128)(2,1)}, u32[]{:S(2)}, u32[]{:S(2)}) %collective-permute-start.1) | collective-permute-done | bytes 262176 | tf_op jit(solution)/shard_map/ppermute | solution.py:177
  133.9 1.8 fusion.30
  136.0 2.9 %collective-permute-start.4 = (bf16[1024,128]{1,0:T(8,128)(2,1)S(1)}, bf16[1024,128]{1,0:T(8,128)(2,1)}, u32[]{:S(2)}, u32[]{:S(2)}) collective-permute-start(bf16[1024,128]{1,0:T(8,128)(2,1)S(1)} %get-tuple-element.34), channel_id=1, source_target_pairs={{0,6},{2,0},{4,2},{6,4},{1,7},{3,1},{5,3},{7,5},{8,14},{10,8},{12,... | collective-permute-start | bytes 786440 | tf_op jit(solution)/shard_map/ppermute | solution.py:178
  138.9 5.8 %collective-permute-done.2 = bf16[1024,128]{1,0:T(8,128)(2,1)} collective-permute-done((bf16[1024,128]{1,0:T(8,128)(2,1)}, bf16[1024,128]{1,0:T(8,128)(2,1)}, u32[]{:S(2)}, u32[]{:S(2)}) %collective-permute-start.2) | collective-permute-done | bytes 262176 | tf_op jit(solution)/shard_map/ppermute | solution.py:177
  144.8 1.8 fusion.31
  146.6 8.2 %collective-permute-done.3 = bf16[1024,128]{1,0:T(8,128)(2,1)} collective-permute-done((bf16[1024,128]{1,0:T(8,128)(2,1)}, bf16[1024,128]{1,0:T(8,128)(2,1)}, u32[]{:S(2)}, u32[]{:S(2)}) %collective-permute-start.3) | collective-permute-done | bytes 262176 | tf_op jit(solution)/shard_map/ppermute | solution.py:177
  154.8 2.1 %fusion.32 = (bf16[1024,128]{1,0:T(8,128)(2,1)S(1)}, bf16[1024,128]{1,0:T(8,128)(2,1)}) fusion(bf16[1024,128]{1,0:T(8,128)(2,1)} %collective-permute-done.3, bf16[4,2048,128]{2,1,0:T(8,128)(2,1)} %collective-permute-done, s32[]{:T(128)S(6)} %select_n.787, bf16[4,2048,128]{2,1,0:T(8,128)(2,1)S(1)} %pad_maximum_fusion, ...), kind=kLoop, calls=%fused_computation.48 | loop fusion | flops 1572864 | bytes 2097164 | tf_op jit(solution)/shard_map/convert.6
  157.0 6.6 %collective-permute-done.5 = bf16[1024,128]{1,0:T(8,128)(2,1)} collective-permute-done((bf16[1024,128]{1,0:T(8,128)(2,1)}, bf16[1024,128]{1,0:T(8,128)(2,1)}, u32[]{:S(2)}, u32[]{:S(2)}) %collective-permute-start.5) | collective-permute-done | bytes 262176 | tf_op jit(solution)/shard_map/ppermute | solution.py:178
  163.6 1.8 fusion.28
  165.5 1.2 collective-permute-start.6
  166.7 5.5 %collective-permute-done.6 = bf16[1024,128]{1,0:T(8,128)(2,1)} collective-permute-done((bf16[1024,128]{1,0:T(8,128)(2,1)}, bf16[1024,128]{1,0:T(8,128)(2,1)}, u32[]{:S(2)}, u32[]{:S(2)}) %collective-permute-start.6) | collective-permute-done | bytes 262176 | tf_op jit(solution)/shard_map/ppermute | solution.py:178
  172.1 1.1 fusion.29
  173.3 0.8 pad_maximum_fusion.3
  174.1 4.2 %reduce-scatter.5.cloned.1.call-done = bf16[64,1024]{1,0:T(8,128)(2,1)} async-done(((bf16[256,1024]{1,0:T(8,128)(2,1)}), bf16[64,1024]{1,0:T(8,128)(2,1)}) %reduce-scatter.5.cloned.1.call-update) | async-done | bytes 131088 | tf_op jit(solution)/shard_map/reduce_scatter | solution.py:252
  178.4 0.9 convert_element_type.181
  179.3 0.7 slice_bitcast_fusion
  179.9 1.5 slice.556
  (33 shorter events, 1.6 us)
Async XLA Ops:
  7.2 4.5 %copy-start = (bf16[512,1024]{1,0:T(8,128)(2,1)S(1)}, bf16[512,1024]{1,0:T(8,128)(2,1)}, u32[]{:S(2)}) copy-start(bf16[512,1024]{1,0:T(8,128)(2,1)} %param.10) | copy-start | bytes 3145732
  7.2 149.8 %reduce-scatter.3.cloned.1.call-start = ((), (), s32[]{:S(2)}) async-start(), calls=%async_computation.2 | async-start | bytes 2621440 | tf_op jit(solution)/shard_map/reduce_scatter | solution.py:251
  11.7 6.7 %copy-start.1 = (f32[512]{0:T(512)S(1)}, f32[512]{0:T(512)}, u32[]{:S(2)}) copy-start(f32[512]{0:T(512)} %param.8) | copy-start | bytes 6148
  11.7 6.7 %copy-start.2 = (bf16[1024,512]{1,0:T(8,128)(2,1)S(1)}, bf16[1024,512]{1,0:T(8,128)(2,1)}, u32[]{:S(2)}) copy-start(bf16[1024,512]{1,0:T(8,128)(2,1)} %param.9) | copy-start | bytes 3145732
  11.7 6.7 %copy-start.3 = (bf16[2048,1024]{1,0:T(8,128)(2,1)S(1)}, bf16[2048,1024]{1,0:T(8,128)(2,1)}, u32[]{:S(2)}) copy-start(bf16[2048,1024]{1,0:T(8,128)(2,1)} %param.6) | copy-start | bytes 12582916
  85.7 5.0 %copy-start.4 = (bf16[2048,1024]{1,0:T(8,128)(2,1)S(1)}, bf16[2048,1024]{1,0:T(8,128)(2,1)}, u32[]{:S(2)}) copy-start(bf16[2048,1024]{1,0:T(8,128)(2,1)} %param.6) | copy-start | bytes 12582916
  108.6 69.8 %reduce-scatter.5.cloned.1.call-start = ((), (), s32[]{:S(2)}) async-start(), calls=%async_computation.3 | async-start | bytes 655360 | tf_op jit(solution)/shard_map/reduce_scatter | solution.py:252
  117.6 4.5 %collective-permute-start = (bf16[4,2048,128]{2,1,0:T(8,128)(2,1)}, bf16[4,2048,128]{2,1,0:T(8,128)(2,1)}, u32[]{:S(2)}, u32[]{:S(2)}) collective-permute-start(bf16[4,2048,128]{2,1,0:T(8,128)(2,1)} %pad_maximum_fusion.1), channel_id=1, source_target_pairs={{0,1},{1,0},{2,3},{3,2},{4,5},{5,4},{6,7},{7,6},{8,9},{9,8},{10,11... | collective-permute-start | bytes 6291464 | tf_op jit(solution)/shard_map/ppermute | solution.py:162
  123.9 9.9 %collective-permute-start.1 = (bf16[1024,128]{1,0:T(8,128)(2,1)}, bf16[1024,128]{1,0:T(8,128)(2,1)}, u32[]{:S(2)}, u32[]{:S(2)}) collective-permute-start(bf16[1024,128]{1,0:T(8,128)(2,1)} %get-tuple-element.33), channel_id=1, source_target_pairs={{0,2},{2,4},{4,6},{6,0},{1,3},{3,5},{5,7},{7,1},{8,10},{10,12},{12... | collective-permute-start | bytes 786440 | tf_op jit(solution)/shard_map/ppermute | solution.py:177
  135.7 9.1 %collective-permute-start.2 = (bf16[1024,128]{1,0:T(8,128)(2,1)}, bf16[1024,128]{1,0:T(8,128)(2,1)}, u32[]{:S(2)}, u32[]{:S(2)}) collective-permute-start(bf16[1024,128]{1,0:T(8,128)(2,1)} %fusion.30), channel_id=1, source_target_pairs={{0,2},{2,4},{4,6},{6,0},{1,3},{3,5},{5,7},{7,1},{8,10},{10,12},{12... | collective-permute-start | bytes 786440 | tf_op jit(solution)/shard_map/ppermute | solution.py:177
  136.0 10.6 %collective-permute-start.4 = (bf16[1024,128]{1,0:T(8,128)(2,1)S(1)}, bf16[1024,128]{1,0:T(8,128)(2,1)}, u32[]{:S(2)}, u32[]{:S(2)}) collective-permute-start(bf16[1024,128]{1,0:T(8,128)(2,1)S(1)} %get-tuple-element.34), channel_id=1, source_target_pairs={{0,6},{2,0},{4,2},{6,4},{1,7},{3,1},{5,3},{7,5},{8,14},{10,8},{12,... | collective-permute-start | bytes 786440 | tf_op jit(solution)/shard_map/ppermute | solution.py:178
  146.6 8.2 %collective-permute-start.3 = (bf16[1024,128]{1,0:T(8,128)(2,1)}, bf16[1024,128]{1,0:T(8,128)(2,1)}, u32[]{:S(2)}, u32[]{:S(2)}) collective-permute-start(bf16[1024,128]{1,0:T(8,128)(2,1)} %fusion.31), channel_id=1, source_target_pairs={{0,2},{2,4},{4,6},{6,0},{1,3},{3,5},{5,7},{7,1},{8,10},{10,12},{12... | collective-permute-start | bytes 786440 | tf_op jit(solution)/shard_map/ppermute | solution.py:177
  156.9 6.7 %collective-permute-start.5 = (bf16[1024,128]{1,0:T(8,128)(2,1)}, bf16[1024,128]{1,0:T(8,128)(2,1)}, u32[]{:S(2)}, u32[]{:S(2)}) collective-permute-start(bf16[1024,128]{1,0:T(8,128)(2,1)} %get-tuple-element.32), channel_id=1, source_target_pairs={{0,6},{2,0},{4,2},{6,4},{1,7},{3,1},{5,3},{7,5},{8,14},{10,8},{12,... | collective-permute-start | bytes 786440 | tf_op jit(solution)/shard_map/ppermute | solution.py:178
  165.5 6.7 %collective-permute-start.6 = (bf16[1024,128]{1,0:T(8,128)(2,1)}, bf16[1024,128]{1,0:T(8,128)(2,1)}, u32[]{:S(2)}, u32[]{:S(2)}) collective-permute-start(bf16[1024,128]{1,0:T(8,128)(2,1)} %fusion.28), channel_id=1, source_target_pairs={{0,6},{2,0},{4,2},{6,4},{1,7},{3,1},{5,3},{7,5},{8,14},{10,8},{12,... | collective-permute-start | bytes 786440 | tf_op jit(solution)/shard_map/ppermute | solution.py:178
Sparse Core Ops, SparseCore 0:
  108.7 30.2 reduce-scatter.2
  157.1 21.2 reduce-scatter.4

commit v5 on v3

--- a/solution.py
+++ b/solution.py
@@ -7,130 +7,101 @@
 from jax.experimental.pallas import tpu as pltpu
 from jax.sharding import Mesh, PartitionSpec as P
 
-SEGMENTS = 8
+SEGMENTS = 16
 LANES = 128
 UNROLL = 8
 
 
-def _summary_kernel(g_ref, gn_ref, r_ref, *refs):
-    chunks = (len(refs) - 4) // 2
-    drive_refs = refs[:chunks]
-    up_refs = refs[chunks:2 * chunks]
-    fa_ref, fb_ref, ba_ref, bb_ref = refs[2 * chunks:]
+def _summary_kernel(g_ref, gn_ref, r_ref, drive_ref, up_ref, fa_ref, fb_ref, ba_ref, bb_ref):
     steps, segs, _ = g_ref.shape
-    rs = [r_ref[:, pl.ds(k * LANES, LANES)] for k in range(chunks)]
-    ones = tuple(jnp.ones((segs, LANES), jnp.float32) for _ in range(chunks))
-    zeros = tuple(jnp.zeros((segs, LANES), jnp.float32) for _ in range(chunks))
+    r = r_ref[...]
+    ones = jnp.ones((segs, LANES), jnp.float32)
+    zeros = jnp.zeros((segs, LANES), jnp.float32)
 
     def fwd(i, carry):
         a, b = carry
-        g = g_ref[i]
-        new_a, new_b = [], []
-        for k in range(chunks):
-            d = jnp.exp(-(g * rs[k]))
-            x = drive_refs[k][pl.ds(i, segs, stride=steps), :]
-            new_a.append(a[k] * d)
-            new_b.append(d * b[k] + x)
-        return (tuple(new_a), tuple(new_b))
+        d = jnp.exp(-(g_ref[i] * r))
+        x = drive_ref[pl.ds(i, segs, stride=steps), :]
+        return (a * d, d * b + x)
 
     a, b = lax.fori_loop(0, steps, fwd, (ones, zeros), unroll=UNROLL)
-    for k in range(chunks):
-        fa_ref[:, pl.ds(k * LANES, LANES)] = a[k]
-        fb_ref[:, pl.ds(k * LANES, LANES)] = b[k]
+    fa_ref[...] = a
+    fb_ref[...] = b
 
     def bwd(j, carry):
         a, b = carry
         i = steps - 1 - j
-        g = gn_ref[i]
-        new_a, new_b = [], []
-        for k in range(chunks):
-            e = jnp.exp(-(g * rs[k]))
-            u = up_refs[k][pl.ds(i, segs, stride=steps), :]
-            new_a.append(a[k] * e)
-            new_b.append(e * b[k] + u)
-        return (tuple(new_a), tuple(new_b))
+        e = jnp.exp(-(gn_ref[i] * r))
+        u = up_ref[pl.ds(i, segs, stride=steps), :]
+        return (a * e, e * b + u)
 
     a, b = lax.fori_loop(0, steps, bwd, (ones, zeros), unroll=UNROLL)
-    for k in range(chunks):
-        ba_ref[:, pl.ds(k * LANES, LANES)] = a[k]
-        bb_ref[:, pl.ds(k * LANES, LANES)] = b[k]
-
-
-def _sweep_kernel(g_ref, gn_ref, r_ref, if_ref, ib_ref, *refs):
-    chunks = (len(refs) - 2) // 2
-    drive_refs = refs[:chunks]
-    up_refs = refs[chunks:2 * chunks]
-    st_ref, adj_ref = refs[2 * chunks:]
+    ba_ref[...] = a
+    bb_ref[...] = b
+
+
+def _sweep_kernel(g_ref, gn_ref, r_ref, if_ref, ib_ref, drive_ref, up_ref, st_ref, adj_ref):
     steps, segs, _ = g_ref.shape
-    rs = [r_ref[:, pl.ds(k * LANES, LANES)] for k in range(chunks)]
+    r = r_ref[...]
 
     def fwd(i, b):
-        g = g_ref[i]
-        out = []
-        for k in range(chunks):
-            d = jnp.exp(-(g * rs[k]))
-            v = d * b[k] + drive_refs[k][pl.ds(i, segs, stride=steps), :]
-            st_ref[k, pl.ds(i, segs, stride=steps), :] = v
-            out.append(v)
-        return tuple(out)
-
-    init = tuple(if_ref[:, pl.ds(k * LANES, LANES)] for k in range(chunks))
-    lax.fori_loop(0, steps, fwd, init, unroll=UNROLL)
+        d = jnp.exp(-(g_ref[i] * r))
+        b = d * b + drive_ref[pl.ds(i, segs, stride=steps), :]
+        st_ref[0, pl.ds(i, segs, stride=steps), :] = b
+        return b
+
+    lax.fori_loop(0, steps, fwd, if_ref[...], unroll=UNROLL)
 
     def bwd(j, b):
         i = steps - 1 - j
-        g = gn_ref[i]
-        out = []
-        for k in range(chunks):
-            e = jnp.exp(-(g * rs[k]))
-            v = e * b[k] + up_refs[k][pl.ds(i, segs, stride=steps), :]
-            adj_ref[k, pl.ds(i, segs, stride=steps), :] = v
-            out.append(v)
-        return tuple(out)
-
-    init = tuple(ib_ref[:, pl.ds(k * LANES, LANES)] for k in range(chunks))
-    lax.fori_loop(0, steps, bwd, init, unroll=UNROLL)
-
-
-def _column_specs(total, width):
-    return [pl.BlockSpec((total, LANES), lambda j, k=k: (0, k)) for k in range(width // LANES)]
+        e = jnp.exp(-(gn_ref[i] * r))
+        b = e * b + up_ref[pl.ds(i, segs, stride=steps), :]
+        adj_ref[0, pl.ds(i, segs, stride=steps), :] = b
+        return b
+
+    lax.fori_loop(0, steps, bwd, ib_ref[...], unroll=UNROLL)
 
 
 def _whole(shape):
     return pl.BlockSpec(shape, lambda j: (0,) * len(shape))
+
+
+def _lane_specs(total, segs):
+    return (
+        pl.BlockSpec((1, LANES), lambda j: (0, j)),
+        pl.BlockSpec((total, LANES), lambda j: (0, j)),
+        pl.BlockSpec((segs, LANES), lambda j: (0, j)),
+    )
 
 
 def local_summaries(g3, gn3, rates2, drive, up):
     total, width = drive.shape
     steps, segs, _ = g3.shape
-    chunks = width // LANES
-    cols = _column_specs(total, width)
+    r_spec, col, small = _lane_specs(total, segs)
     seg_shape = jax.ShapeDtypeStruct((segs, width), jnp.float32)
     return pl.pallas_call(
         _summary_kernel,
-        grid=(1,),
-        in_specs=[_whole(g3.shape), _whole(gn3.shape), _whole(rates2.shape)] + cols + cols,
-        out_specs=[_whole((segs, width))] * 4,
+        grid=(width // LANES,),
+        in_specs=[_whole(g3.shape), _whole(gn3.shape), r_spec, col, col],
+        out_specs=[small] * 4,
         out_shape=[seg_shape] * 4,
-        compiler_params=pltpu.CompilerParams(vmem_limit_bytes=48 * 1024 * 1024),
-    )(g3, gn3, rates2, *([drive] * chunks), *([up] * chunks))
+    )(g3, gn3, rates2, drive, up)
 
 
 def sweeps(g3, gn3, rates2, drive, up, init_f, init_b):
     total, width = drive.shape
     steps, segs, _ = g3.shape
     chunks = width // LANES
-    cols = _column_specs(total, width)
+    r_spec, col, small = _lane_specs(total, segs)
     full = jax.ShapeDtypeStruct((chunks, total, LANES), jnp.float32)
+    out = pl.BlockSpec((1, total, LANES), lambda j: (j, 0, 0))
     return pl.pallas_call(
         _sweep_kernel,
-        grid=(1,),
-        in_specs=[_whole(g3.shape), _whole(gn3.shape), _whole(rates2.shape),
-                  _whole(init_f.shape), _whole(init_b.shape)] + cols + cols,
-        out_specs=[_whole(full.shape)] * 2,
+        grid=(chunks,),
+        in_specs=[_whole(g3.shape), _whole(gn3.shape), r_spec, small, small, col, col],
+        out_specs=[out, out],
         out_shape=[full, full],
-        compiler_params=pltpu.CompilerParams(vmem_limit_bytes=48 * 1024 * 1024),
-    )(g3, gn3, rates2, init_f, init_b, *([drive] * chunks), *([up] * chunks))
+    )(g3, gn3, rates2, init_f, init_b, drive, up)
 
 
 def _pick(x, index):

time: 175 us -> 191 us (1.091)
  other arithmetic: 15.2 us -> 21.4 us
  local copies, waits for them, and re-layouts: 21.1 us -> 26.7 us
  Pallas kernels: 34.1 us -> 37.5 us
    pallas_call x2, Pallas kernels: 34.1 us -> 37.5 us  [the longest x1 21.7 us: sweeps(): pl.pallas_call(_sweep_kernel, grid=(chunks,), in_specs=[_whole(g3.shape),...]
    unnamed x11 -> x13, local copies, waits for them, and re-layouts: 3.93 us -> 3.87 us
  transfers between devices with their start and end apart: 9 -> 9, of which waited for: 6 -> 6; matrix products, arithmetic and copies ran while one was open for 18% -> 16% of each run, Pallas kernels for 0% -> 0%
where the time goes in v5:
time: 191 us; the launch traced here: 190 us
  Pallas kernels  37.5 us (20%)
  matrix products  35.7 us (19%)
  local copies, waits for them, and re-layouts  26.7 us (14%)
  blocking collectives  25.8 us (14%)
  other arithmetic  21.4 us (11%)
  waiting for transfers between devices  18.1 us (9%)
  between operations  14.8 us (8%)
  starting transfers between devices  10.4 us (5%)
    pallas_call x1, Pallas kernels, sweeps(): pl.pallas_call(_sweep_kernel, grid=(chunks,), in_specs=[_whole(g3.shape),...  21.7 us
    pallas_call x1, Pallas kernels, local_summaries(): pl.pallas_call(_summary_kernel, grid=(width // LANES,), in_specs=[_whole(...  15.8 us
    all_gather x1, blocking collectives, local(): lax.all_gather(summary, 'sz')  13.2 us
    all_gather x1, blocking collectives, local(): lax.all_gather(lax.all_gather(summary, 'sz'), 'sx').reshape(peers, 3, width)  12.5 us
    ppermute x3, waiting for transfers between devices, chan_reduce(): got_a = lax.ppermute(buf_a.astype(jnp.bfloat16), 'cy', up_ring)  12.3 us
    another operation x2, local copies, waits for them, and re-layouts  8.35 us
    ppermute x3, starting transfers between devices, chan_reduce(): got_b = lax.ppermute(buf_b.astype(jnp.bfloat16), 'cy', down_ring)  8.18 us
    dot_general x1, matrix products, local(): lax.dot_general(w_in3, drive_grad, (((1, 2), (0, 2)), ((), ())), preferre...  7.91 us
  transfers between devices with their start and end apart: 9, of which 6 were waited for; matrix products, arithmetic and copies ran while one was open for 16% of the time, Pallas kernels for 0%

profile of v5, /device:TPU:0, one launch (start us, length us, event | category | flops | bytes accessed | tf_op | source)
XLA Modules:
  0.0 190.3 jit_solution(7334230930905588114)
XLA Ops:
  7.2 0.8 broadcast_multiply_fusion
  8.0 0.8 slice.446
  8.9 1.4 copy.30.gn_ref
  10.3 2.1 %copy.29.g_ref = f32[128,16,1]{2,1,0:T(8,128)} copy(f32[128,16,1]{0,1,2:T(8,128)} %bitcast.518) | data formatting | bytes 16384 | tf_op jit(solution)/shard_map/broadcast_in_dim | solution.py:153
  12.4 7.0 %fusion.56.up_ref = f32[2048,512]{1,0:T(8,128)} fusion(bf16[2048,1024]{1,0:T(8,128)(2,1)} %param.11, bf16[512,1024]{1,0:T(8,128)(2,1)} %param.10), kind=kOutput, calls=%fused_computation.186 | convolution fusion | flops 2147483648 | bytes 9437184 | tf_op jit(solution)/shard_map/dot_general | solution.py:149
  19.4 6.5 %sqrt_multiply_fusion.drive_ref = f32[2048,512]{1,0:T(8,128)} fusion(bf16[2048,1024]{1,0:T(8,128)(2,1)S(1)} %copy-done.5, bf16[1024,512]{1,0:T(8,128)(2,1)S(1)} %copy-done, f32[512]{0:T(512)S(1)} %copy-done.2, f32[2048]{0:T(1024)S(1)} %broadcast_multiply_fusion), kind=kOutput, calls=%fused_computation.7 | convolution fusion | flops 2150629376 | bytes 9447424 | tf_op jit(solution)/shard_map/dot_general | solution.py:148
  25.9 15.8 %shard_map.85 = (f32[16,512]{1,0:T(8,128)}, f32[16,512]{1,0:T(8,128)}, f32[16,512]{1,0:T(8,128)}, f32[16,512]{1,0:T(8,128)}) custom-call(f32[128,16,1]{2,1,0:T(8,128)} %copy.29.g_ref, f32[128,16,1]{2,1,0:T(8,128)} %copy.30.gn_ref, f32[1,512]{1,0:T(1,128)} %bitcast.519, f32[2048,512]{1,0:T(8,128)} %sqrt_multiply_fusion.drive_ref, f32[2048,512]{1,0:T(8,128)} %fusion.56.up_ref), custom_call_target="tpu_custom_call" | custom-call | tf_op jit(solution)/shard_map/pallas_call | solution.py:82
  41.7 1.2 fusion.54
  42.9 1.3 multiply_add_fusion
  44.2 1.2 slice.479
  46.0 1.1 multiply_multiply_fusion
  47.1 1.4 multiply_add_fusion.31
  48.5 13.2 %all-gather.2 = f32[4,3,512]{2,1,0:T(4,128)S(1)} all-gather(f32[1,3,512]{2,1,0:T(4,128)S(1)} %maximum_bitcast_fusion.2), channel_id=2, replica_groups=mesh['sx'=4,'sz'=4,'cy'=4,'cc'=2] {'sz'}, dimensions={0}, use_global_device_ids=true | all-gather | bytes 30720 | tf_op jit(solution)/shard_map/all_gather | solution.py:170
  61.7 12.5 %all-gather.1 = f32[16,3,512]{2,1,0:T(4,128)S(1)} all-gather(f32[4,3,512]{2,1,0:T(4,128)S(1)} %all-gather.2), channel_id=3, replica_groups=mesh['sx'=4,'sz'=4,'cy'=4,'cc'=2] {'sx'}, dimensions={0}, use_global_device_ids=true | all-gather | bytes 122880 | tf_op jit(solution)/shard_map/all_gather | solution.py:170
  74.3 1.4 multiply_add_fusion.1
  75.7 1.3 stack.11.ib_ref
  76.9 1.4 multiply_add_fusion.16
  78.3 1.3 stack.10.if_ref
  79.6 21.7 %shard_map.86 = (f32[4,2048,128]{2,1,0:T(8,128)}, f32[4,2048,128]{2,1,0:T(8,128)}) custom-call(f32[128,16,1]{2,1,0:T(8,128)} %copy.29.g_ref, f32[128,16,1]{2,1,0:T(8,128)} %copy.30.gn_ref, f32[1,512]{1,0:T(1,128)} %bitcast.520, f32[16,512]{1,0:T(8,128)} %stack.10.if_ref, f32[16,512]{1,0:T(8,128)} %stack.11.ib_ref, f32[2048,512]{1,0:T(8,128)} %sqrt_multiply_fusion.drive_ref, ...), custom_call_target="tpu_custom_call" | custom-call | tf_op jit(solution)/shard_map/pallas_call | solution.py:98
  101.3 7.5 %multiply_convert_fusion.2 = bf16[4,128,1024]{2,1,0:T(8,128)(2,1)S(1)} fusion(bf16[2048,1024]{1,0:T(8,128)(2,1)} %param.6, f32[4,2048,128]{2,1,0:T(8,128)} %get-tuple-element.13, f32[4,128]{1,0:T(4,128)S(1)} %bitcast.521, f32[2048]{0:T(1024)S(1)} %broadcast_multiply_fusion), kind=kOutput, calls=%fused_computation.11 | convolution fusion | flops 2152726528 | bytes 9447424 | tf_op jit(solution)/shard_map/dot_general | solution.py:198
  109.3 6.8 %multiply_convert_fusion.1 = bf16[4,128,1024]{2,1,0:T(8,128)(2,1)} fusion(bf16[2048,1024]{1,0:T(8,128)(2,1)} %param.11, f32[4,2048,128]{2,1,0:T(8,128)} %get-tuple-element.14), kind=kOutput, calls=%fused_computation.9 | convolution fusion | flops 2149580800 | bytes 9437184 | tf_op jit(solution)/shard_map/dot_general | solution.py:201
  116.1 1.5 copy.37
  117.6 1.7 pad_maximum_fusion
  119.4 7.9 %bitcast_convert_fusion = bf16[2048,1024]{0,1:T(8,128)(2,1)} fusion(f32[4,2048,128]{2,1,0:T(8,128)} %get-tuple-element.13, f32[4,128]{1,0:T(4,128)S(1)} %bitcast.522, f32[2048]{0:T(1024)S(1)} %broadcast_multiply_fusion, bf16[1024,512]{1,0:T(8,128)(2,1)S(1)} %copy-done), kind=kOutput, calls=%fused_computation | convolution fusion | flops 2153775104 | bytes 9447424 | tf_op jit(solution)/shard_map/dot_general | solution.py:210
  127.3 4.4 %constant_dynamic-slice_fusion.1 = (bf16[4,1,128,2048]{3,2,1,0:T(8,128)(2,1)S(1)}, bf16[4,1,128,2048]{3,2,1,0:T(8,128)(2,1)}) fusion(bf16[4,2,128,2048]{3,2,1,0:T(8,128)(2,1)} %bitcast.514, s32[]{:T(128)S(6)} %select_n.1033, s32[]{:T(128)S(6)} %select_n.1035), kind=kLoop, calls=%fused_computation.68 | loop fusion | bytes 8388616 | tf_op jit(solution)/shard_map/dynamic-slice
  131.7 3.9 %copy.33 = bf16[4,1,128,2048]{2,3,0,1:T(8,128)(2,1)} copy(bf16[4,1,128,2048]{3,2,1,0:T(8,128)(2,1)} %get-tuple-element.50) | data formatting | bytes 4194304 | tf_op jit(solution)/shard_map/dynamic-slice.1
  135.6 2.5 %copy.40 = bf16[4,1,128,2048]{2,3,0,1:T(8,128)(2,1)} copy(bf16[4,1,128,2048]{3,2,1,0:T(8,128)(2,1)S(1)} %get-tuple-element.49) | data formatting | bytes 4194304
  138.2 2.0 %collective-permute-done = bf16[4,128,2048]{1,2,0:T(8,128)(2,1)} collective-permute-done((bf16[4,128,2048]{1,2,0:T(8,128)(2,1)}, bf16[4,128,2048]{1,2,0:T(8,128)(2,1)}, u32[]{:S(2)}, u32[]{:S(2)}) %collective-permute-start) | collective-permute-done | bytes 2097184 | tf_op jit(solution)/shard_map/ppermute | solution.py:122
  140.1 2.7 %convert_add_fusion = f32[4,128,2048]{1,2,0:T(8,128)S(1)} fusion(bf16[4,128,2048]{1,2,0:T(8,128)(2,1)} %collective-permute-done, bf16[4,1,128,2048]{2,3,0,1:T(8,128)(2,1)} %copy.40), kind=kLoop, calls=%fused_computation.1 | loop fusion | flops 3145728 | bytes 8388608 | tf_op jit(solution)/shard_map/add | solution.py:122
  143.1 1.3 copy-done.1
  144.5 1.7 collective-permute-start.1
  146.1 0.7 fusion.20
  146.8 1.7 collective-permute-start.4
  148.5 5.8 %collective-permute-done.1 = bf16[128,1024]{0,1:T(8,128)(2,1)} collective-permute-done((bf16[128,1024]{0,1:T(8,128)(2,1)S(1)}, bf16[128,1024]{0,1:T(8,128)(2,1)}, u32[]{:S(2)}, u32[]{:S(2)}) %collective-permute-start.1) | collective-permute-done | bytes 262176 | tf_op jit(solution)/shard_map/ppermute | solution.py:131
  154.3 1.2 fusion.16
  155.8 1.7 fusion.13
  157.5 2.9 %collective-permute-start.5 = (bf16[128,1024]{0,1:T(8,128)(2,1)}, bf16[128,1024]{0,1:T(8,128)(2,1)}, u32[]{:S(2)}, u32[]{:S(2)}) collective-permute-start(bf16[128,1024]{0,1:T(8,128)(2,1)} %fusion.13), channel_id=1, source_target_pairs={{0,6},{2,0},{4,2},{6,4},{1,7},{3,1},{5,3},{7,5},{8,14},{10,8},{12,... | collective-permute-start | bytes 786440 | tf_op jit(solution)/shard_map/ppermute | solution.py:132
  160.5 3.9 %collective-permute-done.2 = bf16[128,1024]{0,1:T(8,128)(2,1)} collective-permute-done((bf16[128,1024]{0,1:T(8,128)(2,1)S(1)}, bf16[128,1024]{0,1:T(8,128)(2,1)}, u32[]{:S(2)}, u32[]{:S(2)}) %collective-permute-start.2) | collective-permute-done | bytes 262176 | tf_op jit(solution)/shard_map/ppermute | solution.py:131
  164.4 1.2 fusion.17
  165.7 1.7 fusion.14
  167.4 3.6 %collective-permute-start.6 = (bf16[128,1024]{0,1:T(8,128)(2,1)}, bf16[128,1024]{0,1:T(8,128)(2,1)}, u32[]{:S(2)}, u32[]{:S(2)}) collective-permute-start(bf16[128,1024]{0,1:T(8,128)(2,1)} %fusion.14), channel_id=1, source_target_pairs={{0,6},{2,0},{4,2},{6,4},{1,7},{3,1},{5,3},{7,5},{8,14},{10,8},{12,... | collective-permute-start | bytes 786440 | tf_op jit(solution)/shard_map/ppermute | solution.py:132
  171.0 2.7 %collective-permute-done.3 = bf16[128,1024]{0,1:T(8,128)(2,1)} collective-permute-done((bf16[128,1024]{0,1:T(8,128)(2,1)S(1)}, bf16[128,1024]{0,1:T(8,128)(2,1)}, u32[]{:S(2)}, u32[]{:S(2)}) %collective-permute-start.3) | collective-permute-done | bytes 262176 | tf_op jit(solution)/shard_map/ppermute | solution.py:131
  173.6 1.2 fusion.18
  175.2 1.0 fusion.15
  176.2 0.8 maximum_bitcast_fusion
  177.1 3.4 %reduce-scatter.5.cloned.1.call-done = bf16[64,1024]{1,0:T(8,128)(2,1)} async-done(((bf16[256,1024]{1,0:T(8,128)(2,1)}), bf16[64,1024]{1,0:T(8,128)(2,1)}) %reduce-scatter.5.cloned.1.call-update) | async-done | bytes 131088 | tf_op jit(solution)/shard_map/reduce_scatter | solution.py:206
  180.4 0.9 convert_element_type.89
  182.0 1.5 slice.614
  (29 shorter events, 2.6 us)
Async XLA Ops:
  7.2 12.2 %copy-start = (bf16[1024,512]{1,0:T(8,128)(2,1)S(1)}, bf16[1024,512]{1,0:T(8,128)(2,1)}, u32[]{:S(2)}) copy-start(bf16[1024,512]{1,0:T(8,128)(2,1)} %param.9) | copy-start | bytes 3145732
  7.2 153.3 %reduce-scatter.3.cloned.1.call-start = ((), (), s32[]{:S(2)}) async-start(), calls=%async_computation.2 | async-start | bytes 2621440 | tf_op jit(solution)/shard_map/reduce_scatter | solution.py:205
  12.4 7.0 %copy-start.2 = (f32[512]{0:T(512)S(1)}, f32[512]{0:T(512)}, u32[]{:S(2)}) copy-start(f32[512]{0:T(512)} %param.8) | copy-start | bytes 6148
  12.4 7.0 %copy-start.5 = (bf16[2048,1024]{1,0:T(8,128)(2,1)S(1)}, bf16[2048,1024]{1,0:T(8,128)(2,1)}, u32[]{:S(2)}) copy-start(bf16[2048,1024]{1,0:T(8,128)(2,1)} %param.6) | copy-start | bytes 12582916
  25.9 22.5 %copy-start.3 = (f32[512]{0:T(512)S(1)}, f32[512]{0:T(512)}, u32[]{:S(2)}) copy-start(f32[512]{0:T(512)} %param.8) | copy-start | bytes 6148
  79.6 21.7 %copy-start.4 = (f32[512]{0:T(512)S(1)}, f32[512]{0:T(512)}, u32[]{:S(2)}) copy-start(f32[512]{0:T(512)} %param.8) | copy-start | bytes 6148
  119.3 61.1 %reduce-scatter.5.cloned.1.call-start = ((), (), s32[]{:S(2)}) async-start(), calls=%async_computation.3 | async-start | bytes 655360 | tf_op jit(solution)/shard_map/reduce_scatter | solution.py:206
  135.6 4.5 %collective-permute-start = (bf16[4,128,2048]{1,2,0:T(8,128)(2,1)}, bf16[4,128,2048]{1,2,0:T(8,128)(2,1)}, u32[]{:S(2)}, u32[]{:S(2)}) collective-permute-start(bf16[4,128,2048]{1,2,0:T(8,128)(2,1)} %bitcast.516), channel_id=1, source_target_pairs={{0,1},{1,0},{2,3},{3,2},{4,5},{5,4},{6,7},{7,6},{8,9},{9,8},{10,11... | collective-permute-start | bytes 6291464 | tf_op jit(solution)/shard_map/ppermute | solution.py:122
  143.1 1.3 copy-start.1
  144.5 9.8 %collective-permute-start.1 = (bf16[128,1024]{0,1:T(8,128)(2,1)S(1)}, bf16[128,1024]{0,1:T(8,128)(2,1)}, u32[]{:S(2)}, u32[]{:S(2)}) collective-permute-start(bf16[128,1024]{0,1:T(8,128)(2,1)S(1)} %fusion.19), channel_id=1, source_target_pairs={{0,2},{2,4},{4,6},{6,0},{1,3},{3,5},{5,7},{7,1},{8,10},{10,12},{12... | collective-permute-start | bytes 786440 | tf_op jit(solution)/shard_map/ppermute | solution.py:131
  146.8 9.0 %collective-permute-start.4 = (bf16[128,1024]{0,1:T(8,128)(2,1)}, bf16[128,1024]{0,1:T(8,128)(2,1)}, u32[]{:S(2)}, u32[]{:S(2)}) collective-permute-start(bf16[128,1024]{0,1:T(8,128)(2,1)} %fusion.20), channel_id=1, source_target_pairs={{0,6},{2,0},{4,2},{6,4},{1,7},{3,1},{5,3},{7,5},{8,14},{10,8},{12,... | collective-permute-start | bytes 786440 | tf_op jit(solution)/shard_map/ppermute | solution.py:132
  155.4 8.9 %collective-permute-start.2 = (bf16[128,1024]{0,1:T(8,128)(2,1)S(1)}, bf16[128,1024]{0,1:T(8,128)(2,1)}, u32[]{:S(2)}, u32[]{:S(2)}) collective-permute-start(bf16[128,1024]{0,1:T(8,128)(2,1)S(1)} %fusion.16), channel_id=1, source_target_pairs={{0,2},{2,4},{4,6},{6,0},{1,3},{3,5},{5,7},{7,1},{8,10},{10,12},{12... | collective-permute-start | bytes 786440 | tf_op jit(solution)/shard_map/ppermute | solution.py:131
  157.5 8.1 %collective-permute-start.5 = (bf16[128,1024]{0,1:T(8,128)(2,1)}, bf16[128,1024]{0,1:T(8,128)(2,1)}, u32[]{:S(2)}, u32[]{:S(2)}) collective-permute-start(bf16[128,1024]{0,1:T(8,128)(2,1)} %fusion.13), channel_id=1, source_target_pairs={{0,6},{2,0},{4,2},{6,4},{1,7},{3,1},{5,3},{7,5},{8,14},{10,8},{12,... | collective-permute-start | bytes 786440 | tf_op jit(solution)/shard_map/ppermute | solution.py:132
  165.6 8.1 %collective-permute-start.3 = (bf16[128,1024]{0,1:T(8,128)(2,1)S(1)}, bf16[128,1024]{0,1:T(8,128)(2,1)}, u32[]{:S(2)}, u32[]{:S(2)}) collective-permute-start(bf16[128,1024]{0,1:T(8,128)(2,1)S(1)} %fusion.17), channel_id=1, source_target_pairs={{0,2},{2,4},{4,6},{6,0},{1,3},{3,5},{5,7},{7,1},{8,10},{10,12},{12... | collective-permute-start | bytes 786440 | tf_op jit(solution)/shard_map/ppermute | solution.py:131
  167.4 7.9 %collective-permute-start.6 = (bf16[128,1024]{0,1:T(8,128)(2,1)}, bf16[128,1024]{0,1:T(8,128)(2,1)}, u32[]{:S(2)}, u32[]{:S(2)}) collective-permute-start(bf16[128,1024]{0,1:T(8,128)(2,1)} %fusion.14), channel_id=1, source_target_pairs={{0,6},{2,0},{4,2},{6,4},{1,7},{3,1},{5,3},{7,5},{8,14},{10,8},{12,... | collective-permute-start | bytes 786440 | tf_op jit(solution)/shard_map/ppermute | solution.py:132
Sparse Core Ops, SparseCore 0:
  119.4 30.2 reduce-scatter.2
  160.6 19.7 reduce-scatter.4

commit v6 on v3

--- a/solution.py
+++ b/solution.py
@@ -144,7 +144,7 @@
     core = lax.axis_index("cc")
     dmodel, total = partial_t.shape
     blk = dmodel // (ys * cores)
-    parts = partial_t.reshape(ys, cores, blk, total).transpose(1, 0, 2, 3)
+    parts = partial_t.reshape(cores, ys, blk, total)
     mine = _pick(parts, core).astype(jnp.float32)
     other = _pick(parts, (core + 1) % cores)
     swap = [(i, (i + 1) % cores) for i in range(cores)]
@@ -235,9 +235,16 @@
     joined = lax.psum_scatter(joined, "sz", scatter_dimension=0, tiled=True).astype(jnp.float32)
     d_w_in = joined[:, :width]
     d_w_out = joined[:, width:].T
-    w_in3 = w_in.reshape(w_in.shape[0], chunks, LANES)
+    ys = lax.axis_size("cy")
+    cores = lax.axis_size("cc")
+    dmodel = w_in.shape[0]
+    w_rows = (
+        w_in.reshape(ys, cores, dmodel // (ys * cores), width)
+        .transpose(1, 0, 2, 3)
+        .reshape(dmodel, chunks, LANES)
+    )
     partial_t = lax.dot_general(
-        w_in3, drive_grad, (((1, 2), (0, 2)), ((), ())), preferred_element_type=jnp.float32
+        w_rows, drive_grad, (((1, 2), (0, 2)), ((), ())), preferred_element_type=jnp.float32
     ).astype(jnp.bfloat16)
     d_inputs = chan_reduce(partial_t).T
     return (d_inputs, d_w_in, d_w_out)

time: 175 us -> 177 us (1.011)
  local copies, waits for them, and re-layouts: 21.1 us -> 23.4 us
    another operation x2 -> x0, local copies, waits for them, and re-layouts: 8.31 us -> none
    dynamic_slice x0 -> x2, local copies, waits for them, and re-layouts: none -> 7.98 us  [_pick(): return lax.dynamic_index_in_dim(x, index, 0, keepdims=False)]
  transfers between devices with their start and end apart: 9 -> 9, of which waited for: 6 -> 6; matrix products, arithmetic and copies ran while one was open for 18% -> 20% of each run, Pallas kernels for 0% -> 0%
where the time goes in v6:
time: 177 us; the launch traced here: 176 us
  matrix products  34.3 us (19%)
  Pallas kernels  34.1 us (19%)
  blocking collectives  25.8 us (15%)
  local copies, waits for them, and re-layouts  23.4 us (13%)
  waiting for transfers between devices  18.2 us (10%)
  other arithmetic  15.2 us (9%)
  between operations  14.9 us (8%)
  starting transfers between devices  10.4 us (6%)
    pallas_call x1, Pallas kernels, sweeps(): pl.pallas_call(_sweep_kernel, grid=(1,), in_specs=[_whole(g3.shape), _who...  21.8 us
    all_gather x1, blocking collectives, local(): lax.all_gather(summary, 'sz')  13.2 us
    all_gather x1, blocking collectives, local(): lax.all_gather(lax.all_gather(summary, 'sz'), 'sx').reshape(peers, 3, width)  12.5 us
    pallas_call x1, Pallas kernels, local_summaries(): pl.pallas_call(_summary_kernel, grid=(1,), in_specs=[_whole(g3.shape), _w...  12.3 us
    ppermute x3, waiting for transfers between devices, chan_reduce(): got_a = lax.ppermute(buf_a.astype(jnp.bfloat16), 'cy', up_ring)  12.3 us
    ppermute x3, starting transfers between devices, chan_reduce(): got_b = lax.ppermute(buf_b.astype(jnp.bfloat16), 'cy', down_ring)  8.17 us
    dot_general x1, matrix products, local(): lax.dot_general(w_rows, drive_grad, (((1, 2), (0, 2)), ((), ())), preferr...  8.02 us
    dynamic_slice x2, local copies, waits for them, and re-layouts, _pick(): return lax.dynamic_index_in_dim(x, index, 0, keepdims=False)  7.98 us
  transfers between devices with their start and end apart: 9, of which 6 were waited for; matrix products, arithmetic and copies ran while one was open for 20% of the time, Pallas kernels for 0%

profile of v6, /device:TPU:0, one launch (start us, length us, event | category | flops | bytes accessed | tf_op | source)
XLA Modules:
  0.0 176.1 jit_solution(7458425371957875849)
XLA Ops:
  7.2 0.8 broadcast_multiply_fusion
  8.0 0.8 slice.310
  8.8 0.7 reshape.1240
  9.5 1.2 slice.327
  10.8 0.4 copy.30.gn_ref
  11.2 0.4 copy.29.g_ref
  11.7 6.7 %fusion.53.refs_4_.refs_5_.refs_6_.refs_7_ = f32[2048,512]{1,0:T(8,128)} fusion(bf16[2048,1024]{1,0:T(8,128)(2,1)} %param.11, bf16[512,1024]{1,0:T(8,128)(2,1)S(1)} %copy-done), kind=kOutput, calls=%fused_computation.168 | convolution fusion | flops 2147483648 | bytes 9437184 | tf_op jit(solution)/shard_map/dot_general | solution.py:178
  18.4 6.6 %sqrt_multiply_fusion.refs_0_.refs_1_.refs_2_.refs_3_ = f32[2048,512]{1,0:T(8,128)} fusion(bf16[2048,1024]{1,0:T(8,128)(2,1)S(1)} %copy-done.3, bf16[1024,512]{1,0:T(8,128)(2,1)S(1)} %copy-done.2, f32[512]{0:T(512)S(1)} %copy-done.1, f32[2048]{0:T(1024)S(1)} %broadcast_multiply_fusion), kind=kOutput, calls=%fused_computation.7 | convolution fusion | flops 2150629376 | bytes 9447424 | tf_op jit(solution)/shard_map/dot_general | solution.py:177
  24.9 12.3 %shard_map.85 = (f32[8,512]{1,0:T(8,128)S(1)}, f32[8,512]{1,0:T(8,128)S(1)}, f32[8,512]{1,0:T(8,128)S(1)}, f32[8,512]{1,0:T(8,128)S(1)}) custom-call(f32[256,8,1]{2,1,0:T(8,128)S(1)} %copy.29.g_ref, f32[256,8,1]{2,1,0:T(8,128)S(1)} %copy.30.gn_ref, f32[1,512]{1,0:T(1,128)S(1)} %bitcast.492, f32[2048,512]{1,0:T(8,128)} %sqrt_multiply_fusion.refs_0_.refs_1_.refs_2_.refs_3_, ...), custom_call_target="tpu_custom_call" | custom-call | tf_op jit(solution)/shard_map/pallas_call | solution.py:109
  38.0 13.2 %all-gather.2 = f32[4,3,512]{2,1,0:T(4,128)S(1)} all-gather(f32[1,3,512]{2,1,0:T(4,128)S(1)} %maximum_bitcast_fusion.1), channel_id=2, replica_groups=mesh['sx'=4,'sz'=4,'cy'=4,'cc'=2] {'sz'}, dimensions={0}, use_global_device_ids=true | all-gather | bytes 30720 | tf_op jit(solution)/shard_map/all_gather | solution.py:199
  51.2 12.5 %all-gather.1 = f32[16,3,512]{2,1,0:T(4,128)S(1)} all-gather(f32[4,3,512]{2,1,0:T(4,128)S(1)} %all-gather.2), channel_id=3, replica_groups=mesh['sx'=4,'sz'=4,'cy'=4,'cc'=2] {'sx'}, dimensions={0}, use_global_device_ids=true | all-gather | bytes 122880 | tf_op jit(solution)/shard_map/all_gather | solution.py:199
  64.1 21.8 %shard_map.86 = (f32[4,2048,128]{2,1,0:T(8,128)}, f32[4,2048,128]{2,1,0:T(8,128)}) custom-call(f32[256,8,1]{2,1,0:T(8,128)S(1)} %copy.29.g_ref, f32[256,8,1]{2,1,0:T(8,128)S(1)} %copy.30.gn_ref, f32[1,512]{1,0:T(1,128)S(1)} %bitcast.493, f32[8,512]{1,0:T(8,128)S(1)} %stack.10.if_ref, f32[8,512]{1,0:T(8,128)S(1)} %stack.11.ib_ref, ...), custom_call_target="tpu_custom_call" | custom-call | tf_op jit(solution)/shard_map/pallas_call | solution.py:125
  85.8 6.2 %multiply_convert_fusion.2 = bf16[4,128,1024]{2,1,0:T(8,128)(2,1)S(1)} fusion(bf16[2048,1024]{1,0:T(8,128)(2,1)S(1)} %copy-done.4, f32[4,2048,128]{2,1,0:T(8,128)} %get-tuple-element.13, f32[4,128]{1,0:T(4,128)S(1)} %bitcast.494, f32[2048]{0:T(1024)S(1)} %broadcast_multiply_fusion), kind=kOutput, calls=%fused_computation.11 | convolution fusion | flops 2152726528 | bytes 9447424 | tf_op jit(solution)/shard_map/dot_general | solution.py:227
  92.0 0.5 copy.37
  92.6 6.9 %multiply_convert_fusion.1 = bf16[4,128,1024]{2,1,0:T(8,128)(2,1)} fusion(bf16[2048,1024]{1,0:T(8,128)(2,1)} %param.11, f32[4,2048,128]{2,1,0:T(8,128)} %get-tuple-element.14), kind=kOutput, calls=%fused_computation.9 | convolution fusion | flops 2149580800 | bytes 9437184 | tf_op jit(solution)/shard_map/dot_general | solution.py:230
  99.4 1.5 copy.38
  100.9 1.7 pad_maximum_fusion
  102.7 1.3 copy.45
  104.0 0.3 reshape.1244
  104.3 8.0 %bitcast_convert_fusion = bf16[2048,1024]{0,1:T(8,128)(2,1)} fusion(bf16[1024,4,128]{2,1,0:T(4,128)(2,1)S(1)} %reshape.1244, f32[4,2048,128]{2,1,0:T(8,128)} %get-tuple-element.13, f32[4,128]{1,0:T(4,128)S(1)} %bitcast.495, f32[2048]{0:T(1024)S(1)} %broadcast_multiply_fusion), kind=kOutput, calls=%fused_computation | convolution fusion | flops 2153775104 | bytes 9447424 | tf_op jit(solution)/shard_map/dot_general | solution.py:246
  112.3 4.0 %constant_dynamic-slice_fusion.1 = (bf16[1,4,128,2048]{3,2,1,0:T(8,128)(2,1)S(1)}, bf16[1,4,128,2048]{3,2,1,0:T(8,128)(2,1)}) fusion(bf16[2,4,128,2048]{3,2,1,0:T(8,128)(2,1)} %bitcast.496, s32[]{:T(128)S(6)} %select_n.777, s32[]{:T(128)S(6)} %select_n.779), kind=kLoop, calls=%fused_computation.68 | loop fusion | bytes 8388616 | tf_op jit(solution)/shard_map/jit(dynamic_index_in_dim)/dynamic_slice | solution.py:137
  116.3 4.0 %copy.34 = bf16[1,4,128,2048]{2,3,1,0:T(8,128)(2,1)} copy(bf16[1,4,128,2048]{3,2,1,0:T(8,128)(2,1)} %get-tuple-element.34) | data formatting | bytes 4194304 | tf_op jit(solution)/shard_map/jit(dynamic_index_in_dim)/dynamic_slice | solution.py:137
  120.3 2.6 %copy.41 = bf16[1,4,128,2048]{2,3,1,0:T(8,128)(2,1)} copy(bf16[1,4,128,2048]{3,2,1,0:T(8,128)(2,1)S(1)} %get-tuple-element.33) | data formatting | bytes 4194304
  122.8 1.9 %collective-permute-done = bf16[4,128,2048]{1,2,0:T(8,128)(2,1)} collective-permute-done((bf16[4,128,2048]{1,2,0:T(8,128)(2,1)}, bf16[4,128,2048]{1,2,0:T(8,128)(2,1)}, u32[]{:S(2)}, u32[]{:S(2)}) %collective-permute-start) | collective-permute-done | bytes 2097184 | tf_op jit(solution)/shard_map/ppermute | solution.py:151
  124.8 2.7 %convert_add_fusion = f32[4,128,2048]{1,2,0:T(8,128)S(1)} fusion(bf16[4,128,2048]{1,2,0:T(8,128)(2,1)} %collective-permute-done, bf16[1,4,128,2048]{2,3,1,0:T(8,128)(2,1)} %copy.41), kind=kLoop, calls=%fused_computation.1 | loop fusion | flops 3145728 | bytes 8388608 | tf_op jit(solution)/shard_map/add | solution.py:151
  127.4 1.6 fusion.52
  129.1 1.1 fusion.18
  130.1 1.6 collective-permute-start.1
  131.8 0.7 fusion.19
  132.5 1.7 collective-permute-start.4
  134.2 5.7 %collective-permute-done.1 = bf16[128,1024]{0,1:T(8,128)(2,1)} collective-permute-done((bf16[128,1024]{0,1:T(8,128)(2,1)S(1)}, bf16[128,1024]{0,1:T(8,128)(2,1)}, u32[]{:S(2)}, u32[]{:S(2)}) %collective-permute-start.1) | collective-permute-done | bytes 262176 | tf_op jit(solution)/shard_map/ppermute | solution.py:160
  139.9 1.2 fusion.15
  141.1 0.4 collective-permute-start.2
  141.5 1.7 fusion.12
  143.2 2.9 %collective-permute-start.5 = (bf16[128,1024]{0,1:T(8,128)(2,1)}, bf16[128,1024]{0,1:T(8,128)(2,1)}, u32[]{:S(2)}, u32[]{:S(2)}) collective-permute-start(bf16[128,1024]{0,1:T(8,128)(2,1)} %fusion.12), channel_id=1, source_target_pairs={{0,6},{2,0},{4,2},{6,4},{1,7},{3,1},{5,3},{7,5},{8,14},{10,8},{12,... | collective-permute-start | bytes 786440 | tf_op jit(solution)/shard_map/ppermute | solution.py:161
  146.1 3.9 %collective-permute-done.2 = bf16[128,1024]{0,1:T(8,128)(2,1)} collective-permute-done((bf16[128,1024]{0,1:T(8,128)(2,1)S(1)}, bf16[128,1024]{0,1:T(8,128)(2,1)}, u32[]{:S(2)}, u32[]{:S(2)}) %collective-permute-start.2) | collective-permute-done | bytes 262176 | tf_op jit(solution)/shard_map/ppermute | solution.py:160
  150.0 1.2 fusion.16
  151.3 1.7 fusion.13
  153.0 3.6 %collective-permute-start.6 = (bf16[128,1024]{0,1:T(8,128)(2,1)}, bf16[128,1024]{0,1:T(8,128)(2,1)}, u32[]{:S(2)}, u32[]{:S(2)}) collective-permute-start(bf16[128,1024]{0,1:T(8,128)(2,1)} %fusion.13), channel_id=1, source_target_pairs={{0,6},{2,0},{4,2},{6,4},{1,7},{3,1},{5,3},{7,5},{8,14},{10,8},{12,... | collective-permute-start | bytes 786440 | tf_op jit(solution)/shard_map/ppermute | solution.py:161
  156.6 2.7 %collective-permute-done.3 = bf16[128,1024]{0,1:T(8,128)(2,1)} collective-permute-done((bf16[128,1024]{0,1:T(8,128)(2,1)S(1)}, bf16[128,1024]{0,1:T(8,128)(2,1)}, u32[]{:S(2)}, u32[]{:S(2)}) %collective-permute-start.3) | collective-permute-done | bytes 262176 | tf_op jit(solution)/shard_map/ppermute | solution.py:160
  159.3 1.2 fusion.17
  160.4 0.4 collective-permute-done.6
  160.8 1.0 fusion.14
  161.8 0.8 maximum_bitcast_fusion
  162.7 3.5 %reduce-scatter.5.cloned.1.call-done = bf16[64,1024]{1,0:T(8,128)(2,1)} async-done(((bf16[256,1024]{1,0:T(8,128)(2,1)}), bf16[64,1024]{1,0:T(8,128)(2,1)}) %reduce-scatter.5.cloned.1.call-update) | async-done | bytes 131088 | tf_op jit(solution)/shard_map/reduce_scatter | solution.py:235
  166.2 0.9 convert_element_type.89
  167.1 0.7 slice_bitcast_fusion
  167.8 1.5 slice.446
  (30 shorter events, 0.7 us)
Async XLA Ops:
  7.2 4.5 %copy-start = (bf16[512,1024]{1,0:T(8,128)(2,1)S(1)}, bf16[512,1024]{1,0:T(8,128)(2,1)}, u32[]{:S(2)}) copy-start(bf16[512,1024]{1,0:T(8,128)(2,1)} %param.10) | copy-start | bytes 3145732
  7.2 138.9 %reduce-scatter.3.cloned.1.call-start = ((), (), s32[]{:S(2)}) async-start(), calls=%async_computation.2 | async-start | bytes 2621440 | tf_op jit(solution)/shard_map/reduce_scatter | solution.py:234
  11.7 6.7 %copy-start.1 = (f32[512]{0:T(512)S(1)}, f32[512]{0:T(512)}, u32[]{:S(2)}) copy-start(f32[512]{0:T(512)} %param.8) | copy-start | bytes 6148
  11.7 6.7 %copy-start.2 = (bf16[1024,512]{1,0:T(8,128)(2,1)S(1)}, bf16[1024,512]{1,0:T(8,128)(2,1)}, u32[]{:S(2)}) copy-start(bf16[1024,512]{1,0:T(8,128)(2,1)} %param.9) | copy-start | bytes 3145732
  11.7 6.7 %copy-start.3 = (bf16[2048,1024]{1,0:T(8,128)(2,1)S(1)}, bf16[2048,1024]{1,0:T(8,128)(2,1)}, u32[]{:S(2)}) copy-start(bf16[2048,1024]{1,0:T(8,128)(2,1)} %param.6) | copy-start | bytes 12582916
  64.0 21.8 %copy-start.4 = (bf16[2048,1024]{1,0:T(8,128)(2,1)S(1)}, bf16[2048,1024]{1,0:T(8,128)(2,1)}, u32[]{:S(2)}) copy-start(bf16[2048,1024]{1,0:T(8,128)(2,1)} %param.6) | copy-start | bytes 12582916
  102.6 63.6 %reduce-scatter.5.cloned.1.call-start = ((), (), s32[]{:S(2)}) async-start(), calls=%async_computation.3 | async-start | bytes 655360 | tf_op jit(solution)/shard_map/reduce_scatter | solution.py:235
  120.3 4.5 %collective-permute-start = (bf16[4,128,2048]{1,2,0:T(8,128)(2,1)}, bf16[4,128,2048]{1,2,0:T(8,128)(2,1)}, u32[]{:S(2)}, u32[]{:S(2)}) collective-permute-start(bf16[4,128,2048]{1,2,0:T(8,128)(2,1)} %bitcast.499), channel_id=1, source_target_pairs={{0,1},{1,0},{2,3},{3,2},{4,5},{5,4},{6,7},{7,6},{8,9},{9,8},{10,11... | collective-permute-start | bytes 6291464 | tf_op jit(solution)/shard_map/ppermute | solution.py:151
  130.1 9.8 %collective-permute-start.1 = (bf16[128,1024]{0,1:T(8,128)(2,1)S(1)}, bf16[128,1024]{0,1:T(8,128)(2,1)}, u32[]{:S(2)}, u32[]{:S(2)}) collective-permute-start(bf16[128,1024]{0,1:T(8,128)(2,1)S(1)} %fusion.18), channel_id=1, source_target_pairs={{0,2},{2,4},{4,6},{6,0},{1,3},{3,5},{5,7},{7,1},{8,10},{10,12},{12... | collective-permute-start | bytes 786440 | tf_op jit(solution)/shard_map/ppermute | solution.py:160
  132.5 9.0 %collective-permute-start.4 = (bf16[128,1024]{0,1:T(8,128)(2,1)}, bf16[128,1024]{0,1:T(8,128)(2,1)}, u32[]{:S(2)}, u32[]{:S(2)}) collective-permute-start(bf16[128,1024]{0,1:T(8,128)(2,1)} %fusion.19), channel_id=1, source_target_pairs={{0,6},{2,0},{4,2},{6,4},{1,7},{3,1},{5,3},{7,5},{8,14},{10,8},{12,... | collective-permute-start | bytes 786440 | tf_op jit(solution)/shard_map/ppermute | solution.py:161
  141.1 8.9 %collective-permute-start.2 = (bf16[128,1024]{0,1:T(8,128)(2,1)S(1)}, bf16[128,1024]{0,1:T(8,128)(2,1)}, u32[]{:S(2)}, u32[]{:S(2)}) collective-permute-start(bf16[128,1024]{0,1:T(8,128)(2,1)S(1)} %fusion.15), channel_id=1, source_target_pairs={{0,2},{2,4},{4,6},{6,0},{1,3},{3,5},{5,7},{7,1},{8,10},{10,12},{12... | collective-permute-start | bytes 786440 | tf_op jit(solution)/shard_map/ppermute | solution.py:160
  143.2 8.1 %collective-permute-start.5 = (bf16[128,1024]{0,1:T(8,128)(2,1)}, bf16[128,1024]{0,1:T(8,128)(2,1)}, u32[]{:S(2)}, u32[]{:S(2)}) collective-permute-start(bf16[128,1024]{0,1:T(8,128)(2,1)} %fusion.12), channel_id=1, source_target_pairs={{0,6},{2,0},{4,2},{6,4},{1,7},{3,1},{5,3},{7,5},{8,14},{10,8},{12,... | collective-permute-start | bytes 786440 | tf_op jit(solution)/shard_map/ppermute | solution.py:161
  151.2 8.1 %collective-permute-start.3 = (bf16[128,1024]{0,1:T(8,128)(2,1)S(1)}, bf16[128,1024]{0,1:T(8,128)(2,1)}, u32[]{:S(2)}, u32[]{:S(2)}) collective-permute-start(bf16[128,1024]{0,1:T(8,128)(2,1)S(1)} %fusion.16), channel_id=1, source_target_pairs={{0,2},{2,4},{4,6},{6,0},{1,3},{3,5},{5,7},{7,1},{8,10},{10,12},{12... | collective-permute-start | bytes 786440 | tf_op jit(solution)/shard_map/ppermute | solution.py:160
  153.0 7.8 %collective-permute-start.6 = (bf16[128,1024]{0,1:T(8,128)(2,1)}, bf16[128,1024]{0,1:T(8,128)(2,1)}, u32[]{:S(2)}, u32[]{:S(2)}) collective-permute-start(bf16[128,1024]{0,1:T(8,128)(2,1)} %fusion.13), channel_id=1, source_target_pairs={{0,6},{2,0},{4,2},{6,4},{1,7},{3,1},{5,3},{7,5},{8,14},{10,8},{12,... | collective-permute-start | bytes 786440 | tf_op jit(solution)/shard_map/ppermute | solution.py:161
Sparse Core Ops, SparseCore 0:
  102.7 30.2 reduce-scatter.2
  146.3 19.9 reduce-scatter.4

commit v7 on v3

--- a/solution.py
+++ b/solution.py
@@ -12,11 +12,8 @@
 UNROLL = 8
 
 
-def _summary_kernel(g_ref, gn_ref, r_ref, *refs):
-    chunks = (len(refs) - 4) // 2
-    drive_refs = refs[:chunks]
-    up_refs = refs[chunks:2 * chunks]
-    fa_ref, fb_ref, ba_ref, bb_ref = refs[2 * chunks:]
+def _summary_kernel(g_ref, gn_ref, r_ref, drive_refs, up_refs, fa_ref, fb_ref, ba_ref, bb_ref):
+    chunks = drive_refs.shape[0]
     steps, segs, _ = g_ref.shape
     rs = [r_ref[:, pl.ds(k * LANES, LANES)] for k in range(chunks)]
     ones = tuple(jnp.ones((segs, LANES), jnp.float32) for _ in range(chunks))
@@ -28,7 +25,7 @@
         new_a, new_b = [], []
         for k in range(chunks):
             d = jnp.exp(-(g * rs[k]))
-            x = drive_refs[k][pl.ds(i, segs, stride=steps), :]
+            x = drive_refs[k, pl.ds(i, segs, stride=steps), :]
             new_a.append(a[k] * d)
             new_b.append(d * b[k] + x)
         return (tuple(new_a), tuple(new_b))
@@ -45,7 +42,7 @@
         new_a, new_b = [], []
         for k in range(chunks):
             e = jnp.exp(-(g * rs[k]))
-            u = up_refs[k][pl.ds(i, segs, stride=steps), :]
+            u = up_refs[k, pl.ds(i, segs, stride=steps), :]
             new_a.append(a[k] * e)
             new_b.append(e * b[k] + u)
         return (tuple(new_a), tuple(new_b))
@@ -56,11 +53,8 @@
         bb_ref[:, pl.ds(k * LANES, LANES)] = b[k]
 
 
-def _sweep_kernel(g_ref, gn_ref, r_ref, if_ref, ib_ref, *refs):
-    chunks = (len(refs) - 2) // 2
-    drive_refs = refs[:chunks]
-    up_refs = refs[chunks:2 * chunks]
-    st_ref, adj_ref = refs[2 * chunks:]
+def _sweep_kernel(g_ref, gn_ref, r_ref, if_ref, ib_ref, drive_refs, up_refs, st_ref, adj_ref):
+    chunks = drive_refs.shape[0]
     steps, segs, _ = g_ref.shape
     rs = [r_ref[:, pl.ds(k * LANES, LANES)] for k in range(chunks)]
 
@@ -69,7 +63,7 @@
         out = []
         for k in range(chunks):
             d = jnp.exp(-(g * rs[k]))
-            v = d * b[k] + drive_refs[k][pl.ds(i, segs, stride=steps), :]
+            v = d * b[k] + drive_refs[k, pl.ds(i, segs, stride=steps), :]
             st_ref[k, pl.ds(i, segs, stride=steps), :] = v
             out.append(v)
         return tuple(out)
@@ -83,7 +77,7 @@
         out = []
         for k in range(chunks):
             e = jnp.exp(-(g * rs[k]))
-            v = e * b[k] + up_refs[k][pl.ds(i, segs, stride=steps), :]
+            v = e * b[k] + up_refs[k, pl.ds(i, segs, stride=steps), :]
             adj_ref[k, pl.ds(i, segs, stride=steps), :] = v
             out.append(v)
         return tuple(out)
@@ -101,10 +95,10 @@
 
 
 def local_summaries(g3, gn3, rates2, drive, up):
-    total, width = drive.shape
+    chunks, total, lanes = drive.shape
+    width = chunks * lanes
     steps, segs, _ = g3.shape
-    chunks = width // LANES
-    cols = _column_specs(total, width)
+    cols = [_whole(drive.shape)]
     seg_shape = jax.ShapeDtypeStruct((segs, width), jnp.float32)
     return pl.pallas_call(
         _summary_kernel,
@@ -113,14 +107,13 @@
         out_specs=[_whole((segs, width))] * 4,
         out_shape=[seg_shape] * 4,
         compiler_params=pltpu.CompilerParams(vmem_limit_bytes=48 * 1024 * 1024),
-    )(g3, gn3, rates2, *([drive] * chunks), *([up] * chunks))
+    )(g3, gn3, rates2, drive, up)
 
 
 def sweeps(g3, gn3, rates2, drive, up, init_f, init_b):
-    total, width = drive.shape
+    chunks, total, lanes = drive.shape
     steps, segs, _ = g3.shape
-    chunks = width // LANES
-    cols = _column_specs(total, width)
+    cols = [_whole(drive.shape)]
     full = jax.ShapeDtypeStruct((chunks, total, LANES), jnp.float32)
     return pl.pallas_call(
         _sweep_kernel,
@@ -130,7 +123,7 @@
         out_specs=[_whole(full.shape)] * 2,
         out_shape=[full, full],
         compiler_params=pltpu.CompilerParams(vmem_limit_bytes=48 * 1024 * 1024),
-    )(g3, gn3, rates2, init_f, init_b, *([drive] * chunks), *([up] * chunks))
+    )(g3, gn3, rates2, init_f, init_b, drive, up)
 
 
 def _pick(x, index):
@@ -178,6 +171,9 @@
     upstream = lax.dot_general(
         cotangent, w_out, (((1,), (1,)), ((), ())), preferred_element_type=jnp.float32
     )
+    chunks = width // LANES
+    drive = drive.reshape(total, chunks, LANES).transpose(1, 0, 2)
+    upstream = upstream.reshape(total, chunks, LANES).transpose(1, 0, 2)
     gaps_next = jnp.concatenate([gaps[1:], jnp.zeros((1,), jnp.float32)], 0)
     g3 = gaps.reshape(segs, steps).T[:, :, None]
     gn3 = gaps_next.reshape(segs, steps).T[:, :, None]

time: 175 us -> 187 us (1.069)
  local copies, waits for them, and re-layouts: 21.1 us -> 31.9 us
    reshape x0 -> x2, local copies, waits for them, and re-layouts: none -> 10.8 us  [the longest x1 5.46 us: local(): drive = drive.reshape(total, chunks, LANES).transpose(1, 0, 2)]
    dot_general x1, matrix products: 6.56 us -> 8.65 us  [local(): drive = gain * jnp.dot(inputs, w_in, preferred_element_type=jnp.float32)]
  transfers between devices with their start and end apart: 9 -> 9, of which waited for: 6 -> 6; matrix products, arithmetic and copies ran while one was open for 18% -> 17% of each run, Pallas kernels for 0% -> 0%
where the time goes in v7:
time: 187 us; the launch traced here: 186 us
  matrix products  36.1 us (19%)
  Pallas kernels  34.1 us (18%)
  local copies, waits for them, and re-layouts  31.9 us (17%)
  blocking collectives  25.8 us (14%)
  waiting for transfers between devices  18.1 us (10%)
  other arithmetic  15.2 us (8%)
  between operations  14.9 us (8%)
  starting transfers between devices  10.4 us (6%)
    pallas_call x1, Pallas kernels, sweeps(): pl.pallas_call(_sweep_kernel, grid=(1,), in_specs=[_whole(g3.shape), _who...  21.9 us
    all_gather x1, blocking collectives, local(): lax.all_gather(summary, 'sz')  13.2 us
    all_gather x1, blocking collectives, local(): lax.all_gather(lax.all_gather(summary, 'sz'), 'sx').reshape(peers, 3, width)  12.5 us
    ppermute x3, waiting for transfers between devices, chan_reduce(): got_a = lax.ppermute(buf_a.astype(jnp.bfloat16), 'cy', up_ring)  12.4 us
    pallas_call x1, Pallas kernels, local_summaries(): pl.pallas_call(_summary_kernel, grid=(1,), in_specs=[_whole(g3.shape), _w...  12.2 us
    dot_general x1, matrix products, local(): drive = gain * jnp.dot(inputs, w_in, preferred_element_type=jnp.float32)  8.65 us
    another operation x2, local copies, waits for them, and re-layouts  8.31 us
    ppermute x3, starting transfers between devices, chan_reduce(): got_b = lax.ppermute(buf_b.astype(jnp.bfloat16), 'cy', down_ring)  8.22 us
  transfers between devices with their start and end apart: 9, of which 6 were waited for; matrix products, arithmetic and copies ran while one was open for 17% of the time, Pallas kernels for 0%

profile of v7, /device:TPU:0, one launch (start us, length us, event | category | flops | bytes accessed | tf_op | source)
XLA Modules:
  0.0 186.3 jit_solution(2517850511542462287)
XLA Ops:
  7.2 0.8 broadcast_multiply_fusion
  8.0 0.8 slice.310
  8.8 0.7 reshape.1247
  9.5 1.2 slice.327
  10.7 8.6 %sqrt_multiply_fusion = f32[2048,512]{0,1:T(8,128)} fusion(bf16[2048,1024]{1,0:T(8,128)(2,1)} %param.6, bf16[1024,512]{1,0:T(8,128)(2,1)S(1)} %copy-done, f32[512]{0:T(512)} %param.8, f32[2048]{0:T(1024)S(1)} %broadcast_multiply_fusion), kind=kOutput, calls=%fused_computation.7 | convolution fusion | flops 2150629376 | bytes 9447424 | tf_op jit(solution)/shard_map/dot_general | solution.py:170
  19.3 5.5 %copy.29 = f32[2048,4,128]{2,0,1:T(8,128)} copy(f32[2048,4,128]{0,2,1:T(8,128)} %bitcast.506) | data formatting | bytes 8388608 | tf_op jit(solution)/shard_map/reshape | solution.py:175
  24.8 6.5 %fusion.54 = f32[2048,512]{0,1:T(8,128)} fusion(bf16[2048,1024]{1,0:T(8,128)(2,1)} %param.11, bf16[512,1024]{1,0:T(8,128)(2,1)S(1)} %copy-done.4), kind=kOutput, calls=%fused_computation.168 | convolution fusion | flops 2147483648 | bytes 9437184 | tf_op jit(solution)/shard_map/dot_general | solution.py:171
  31.3 5.4 %copy.30 = f32[2048,4,128]{2,0,1:T(8,128)} copy(f32[2048,4,128]{0,2,1:T(8,128)} %bitcast.507) | data formatting | bytes 8388608 | tf_op jit(solution)/shard_map/reshape | solution.py:176
  36.7 0.4 copy.34.gn_ref
  37.2 0.4 copy.33.g_ref
  37.6 12.2 %shard_map.85 = (f32[8,512]{1,0:T(8,128)S(1)}, f32[8,512]{1,0:T(8,128)S(1)}, f32[8,512]{1,0:T(8,128)S(1)}, f32[8,512]{1,0:T(8,128)S(1)}) custom-call(f32[256,8,1]{2,1,0:T(8,128)S(1)} %copy.33.g_ref, f32[256,8,1]{2,1,0:T(8,128)S(1)} %copy.34.gn_ref, f32[1,512]{1,0:T(1,128)S(1)} %bitcast.497, f32[4,2048,128]{2,1,0:T(8,128)} %bitcast.501, f32[4,2048,128]{2,1,0:T(8,128)} %bitcast.503), custom_call_target="tpu_custom_call" | custom-call | tf_op jit(solution)/shard_map/pallas_call | solution.py:103
  50.6 13.2 %all-gather.2 = f32[4,3,512]{2,1,0:T(4,128)S(1)} all-gather(f32[1,3,512]{2,1,0:T(4,128)S(1)} %maximum_bitcast_fusion.1), channel_id=2, replica_groups=mesh['sx'=4,'sz'=4,'cy'=4,'cc'=2] {'sz'}, dimensions={0}, use_global_device_ids=true | all-gather | bytes 30720 | tf_op jit(solution)/shard_map/all_gather | solution.py:195
  63.9 12.5 %all-gather.1 = f32[16,3,512]{2,1,0:T(4,128)S(1)} all-gather(f32[4,3,512]{2,1,0:T(4,128)S(1)} %all-gather.2), channel_id=3, replica_groups=mesh['sx'=4,'sz'=4,'cy'=4,'cc'=2] {'sx'}, dimensions={0}, use_global_device_ids=true | all-gather | bytes 122880 | tf_op jit(solution)/shard_map/all_gather | solution.py:195
  76.7 21.9 %shard_map.86 = (f32[4,2048,128]{2,1,0:T(8,128)}, f32[4,2048,128]{2,1,0:T(8,128)}) custom-call(f32[256,8,1]{2,1,0:T(8,128)S(1)} %copy.33.g_ref, f32[256,8,1]{2,1,0:T(8,128)S(1)} %copy.34.gn_ref, f32[1,512]{1,0:T(1,128)S(1)} %bitcast.498, f32[8,512]{1,0:T(8,128)S(1)} %stack.10.if_ref, f32[8,512]{1,0:T(8,128)S(1)} %stack.11.ib_ref, f32[4,2048,128]{2,1,0:T(8,128)} %bitcast.502, ...), custom_call_target="tpu_custom_call" | custom-call | tf_op jit(solution)/shard_map/pallas_call | solution.py:118
  98.6 6.2 %multiply_convert_fusion.2 = bf16[4,128,1024]{2,1,0:T(8,128)(2,1)S(1)} fusion(bf16[2048,1024]{1,0:T(8,128)(2,1)S(1)} %copy-done.3, f32[4,2048,128]{2,1,0:T(8,128)} %get-tuple-element.13, f32[4,128]{1,0:T(4,128)S(1)} %bitcast.499, f32[2048]{0:T(1024)S(1)} %broadcast_multiply_fusion), kind=kOutput, calls=%fused_computation.11 | convolution fusion | flops 2152726528 | bytes 9447424 | tf_op jit(solution)/shard_map/dot_general | solution.py:223
  104.8 0.5 copy.40
  105.3 6.8 %multiply_convert_fusion.1 = bf16[4,128,1024]{2,1,0:T(8,128)(2,1)} fusion(bf16[2048,1024]{1,0:T(8,128)(2,1)} %param.11, f32[4,2048,128]{2,1,0:T(8,128)} %get-tuple-element.14), kind=kOutput, calls=%fused_computation.9 | convolution fusion | flops 2149580800 | bytes 9437184 | tf_op jit(solution)/shard_map/dot_general | solution.py:226
  112.1 1.5 copy.41
  113.6 1.7 pad_maximum_fusion
  115.3 7.9 %bitcast_convert_fusion = bf16[2048,1024]{0,1:T(8,128)(2,1)} fusion(f32[4,2048,128]{2,1,0:T(8,128)} %get-tuple-element.13, f32[4,128]{1,0:T(4,128)S(1)} %bitcast.500, f32[2048]{0:T(1024)S(1)} %broadcast_multiply_fusion, bf16[1024,512]{1,0:T(8,128)(2,1)S(1)} %copy-done), kind=kOutput, calls=%fused_computation | convolution fusion | flops 2153775104 | bytes 9447424 | tf_op jit(solution)/shard_map/dot_general | solution.py:235
  123.3 4.4 %constant_dynamic-slice_fusion.1 = (bf16[4,1,128,2048]{3,2,1,0:T(8,128)(2,1)S(1)}, bf16[4,1,128,2048]{3,2,1,0:T(8,128)(2,1)}) fusion(bf16[4,2,128,2048]{3,2,1,0:T(8,128)(2,1)} %bitcast.505, s32[]{:T(128)S(6)} %select_n.777, s32[]{:T(128)S(6)} %select_n.779), kind=kLoop, calls=%fused_computation.68 | loop fusion | bytes 8388616 | tf_op jit(solution)/shard_map/dynamic-slice
  127.6 3.9 %copy.37 = bf16[4,1,128,2048]{2,3,0,1:T(8,128)(2,1)} copy(bf16[4,1,128,2048]{3,2,1,0:T(8,128)(2,1)} %get-tuple-element.34) | data formatting | bytes 4194304 | tf_op jit(solution)/shard_map/dynamic-slice.1
  131.6 2.6 %copy.44 = bf16[4,1,128,2048]{2,3,0,1:T(8,128)(2,1)} copy(bf16[4,1,128,2048]{3,2,1,0:T(8,128)(2,1)S(1)} %get-tuple-element.33) | data formatting | bytes 4194304
  134.2 1.9 %collective-permute-done = bf16[4,128,2048]{1,2,0:T(8,128)(2,1)} collective-permute-done((bf16[4,128,2048]{1,2,0:T(8,128)(2,1)}, bf16[4,128,2048]{1,2,0:T(8,128)(2,1)}, u32[]{:S(2)}, u32[]{:S(2)}) %collective-permute-start) | collective-permute-done | bytes 2097184 | tf_op jit(solution)/shard_map/ppermute | solution.py:144
  136.1 2.7 %convert_add_fusion = f32[4,128,2048]{1,2,0:T(8,128)S(1)} fusion(bf16[4,128,2048]{1,2,0:T(8,128)(2,1)} %collective-permute-done, bf16[4,1,128,2048]{2,3,0,1:T(8,128)(2,1)} %copy.44), kind=kLoop, calls=%fused_computation.1 | loop fusion | flops 3145728 | bytes 8388608 | tf_op jit(solution)/shard_map/add | solution.py:144
  138.8 0.3 fusion.53
  139.1 1.3 copy-done.2
  140.4 1.6 collective-permute-start.1
  142.1 0.7 fusion.20
  142.8 1.7 collective-permute-start.4
  144.5 5.8 %collective-permute-done.1 = bf16[128,1024]{0,1:T(8,128)(2,1)} collective-permute-done((bf16[128,1024]{0,1:T(8,128)(2,1)S(1)}, bf16[128,1024]{0,1:T(8,128)(2,1)}, u32[]{:S(2)}, u32[]{:S(2)}) %collective-permute-start.1) | collective-permute-done | bytes 262176 | tf_op jit(solution)/shard_map/ppermute | solution.py:153
  150.2 1.2 fusion.16
  151.4 0.4 collective-permute-start.2
  151.8 1.7 fusion.13
  153.5 3.0 %collective-permute-start.5 = (bf16[128,1024]{0,1:T(8,128)(2,1)}, bf16[128,1024]{0,1:T(8,128)(2,1)}, u32[]{:S(2)}, u32[]{:S(2)}) collective-permute-start(bf16[128,1024]{0,1:T(8,128)(2,1)} %fusion.13), channel_id=1, source_target_pairs={{0,6},{2,0},{4,2},{6,4},{1,7},{3,1},{5,3},{7,5},{8,14},{10,8},{12,... | collective-permute-start | bytes 786440 | tf_op jit(solution)/shard_map/ppermute | solution.py:154
  156.4 3.9 %collective-permute-done.2 = bf16[128,1024]{0,1:T(8,128)(2,1)} collective-permute-done((bf16[128,1024]{0,1:T(8,128)(2,1)S(1)}, bf16[128,1024]{0,1:T(8,128)(2,1)}, u32[]{:S(2)}, u32[]{:S(2)}) %collective-permute-start.2) | collective-permute-done | bytes 262176 | tf_op jit(solution)/shard_map/ppermute | solution.py:153
  160.4 1.2 fusion.17
  161.6 1.7 fusion.14
  163.3 3.6 %collective-permute-start.6 = (bf16[128,1024]{0,1:T(8,128)(2,1)}, bf16[128,1024]{0,1:T(8,128)(2,1)}, u32[]{:S(2)}, u32[]{:S(2)}) collective-permute-start(bf16[128,1024]{0,1:T(8,128)(2,1)} %fusion.14), channel_id=1, source_target_pairs={{0,6},{2,0},{4,2},{6,4},{1,7},{3,1},{5,3},{7,5},{8,14},{10,8},{12,... | collective-permute-start | bytes 786440 | tf_op jit(solution)/shard_map/ppermute | solution.py:154
  166.9 2.7 %collective-permute-done.3 = bf16[128,1024]{0,1:T(8,128)(2,1)} collective-permute-done((bf16[128,1024]{0,1:T(8,128)(2,1)S(1)}, bf16[128,1024]{0,1:T(8,128)(2,1)}, u32[]{:S(2)}, u32[]{:S(2)}) %collective-permute-start.3) | collective-permute-done | bytes 262176 | tf_op jit(solution)/shard_map/ppermute | solution.py:153
  169.6 1.2 fusion.18
  170.8 0.4 collective-permute-done.6
  171.2 1.0 fusion.15
  172.2 0.8 maximum_bitcast_fusion
  173.0 3.3 %reduce-scatter.5.cloned.1.call-done = bf16[64,1024]{1,0:T(8,128)(2,1)} async-done(((bf16[256,1024]{1,0:T(8,128)(2,1)}), bf16[64,1024]{1,0:T(8,128)(2,1)}) %reduce-scatter.5.cloned.1.call-update) | async-done | bytes 131088 | tf_op jit(solution)/shard_map/reduce_scatter | solution.py:231
  176.4 0.9 convert_element_type.89
  177.3 0.7 slice_bitcast_fusion
  178.0 1.5 slice.446
  (30 shorter events, 0.7 us)
Async XLA Ops:
  7.2 3.5 %copy-start = (bf16[1024,512]{1,0:T(8,128)(2,1)S(1)}, bf16[1024,512]{1,0:T(8,128)(2,1)}, u32[]{:S(2)}) copy-start(bf16[1024,512]{1,0:T(8,128)(2,1)} %param.9) | copy-start | bytes 3145732
  7.2 149.2 %reduce-scatter.3.cloned.1.call-start = ((), (), s32[]{:S(2)}) async-start(), calls=%async_computation.2 | async-start | bytes 2621440 | tf_op jit(solution)/shard_map/reduce_scatter | solution.py:230
  19.3 5.5 %copy-start.4 = (bf16[512,1024]{1,0:T(8,128)(2,1)S(1)}, bf16[512,1024]{1,0:T(8,128)(2,1)}, u32[]{:S(2)}) copy-start(bf16[512,1024]{1,0:T(8,128)(2,1)} %param.10) | copy-start | bytes 3145732
  31.3 6.3 %copy-start.1 = (f32[512]{0:T(512)S(1)}, f32[512]{0:T(512)}, u32[]{:S(2)}) copy-start(f32[512]{0:T(512)} %param.8) | copy-start | bytes 6148
  76.7 21.9 %copy-start.3 = (bf16[2048,1024]{1,0:T(8,128)(2,1)S(1)}, bf16[2048,1024]{1,0:T(8,128)(2,1)}, u32[]{:S(2)}) copy-start(bf16[2048,1024]{1,0:T(8,128)(2,1)} %param.6) | copy-start | bytes 12582916
  115.3 61.1 %reduce-scatter.5.cloned.1.call-start = ((), (), s32[]{:S(2)}) async-start(), calls=%async_computation.3 | async-start | bytes 655360 | tf_op jit(solution)/shard_map/reduce_scatter | solution.py:231
  131.6 4.5 %collective-permute-start = (bf16[4,128,2048]{1,2,0:T(8,128)(2,1)}, bf16[4,128,2048]{1,2,0:T(8,128)(2,1)}, u32[]{:S(2)}, u32[]{:S(2)}) collective-permute-start(bf16[4,128,2048]{1,2,0:T(8,128)(2,1)} %bitcast.509), channel_id=1, source_target_pairs={{0,1},{1,0},{2,3},{3,2},{4,5},{5,4},{6,7},{7,6},{8,9},{9,8},{10,11... | collective-permute-start | bytes 6291464 | tf_op jit(solution)/shard_map/ppermute | solution.py:144
  139.0 1.3 copy-start.2
  140.4 9.8 %collective-permute-start.1 = (bf16[128,1024]{0,1:T(8,128)(2,1)S(1)}, bf16[128,1024]{0,1:T(8,128)(2,1)}, u32[]{:S(2)}, u32[]{:S(2)}) collective-permute-start(bf16[128,1024]{0,1:T(8,128)(2,1)S(1)} %fusion.19), channel_id=1, source_target_pairs={{0,2},{2,4},{4,6},{6,0},{1,3},{3,5},{5,7},{7,1},{8,10},{10,12},{12... | collective-permute-start | bytes 786440 | tf_op jit(solution)/shard_map/ppermute | solution.py:153
  142.8 9.0 %collective-permute-start.4 = (bf16[128,1024]{0,1:T(8,128)(2,1)}, bf16[128,1024]{0,1:T(8,128)(2,1)}, u32[]{:S(2)}, u32[]{:S(2)}) collective-permute-start(bf16[128,1024]{0,1:T(8,128)(2,1)} %fusion.20), channel_id=1, source_target_pairs={{0,6},{2,0},{4,2},{6,4},{1,7},{3,1},{5,3},{7,5},{8,14},{10,8},{12,... | collective-permute-start | bytes 786440 | tf_op jit(solution)/shard_map/ppermute | solution.py:154
  151.4 8.9 %collective-permute-start.2 = (bf16[128,1024]{0,1:T(8,128)(2,1)S(1)}, bf16[128,1024]{0,1:T(8,128)(2,1)}, u32[]{:S(2)}, u32[]{:S(2)}) collective-permute-start(bf16[128,1024]{0,1:T(8,128)(2,1)S(1)} %fusion.16), channel_id=1, source_target_pairs={{0,2},{2,4},{4,6},{6,0},{1,3},{3,5},{5,7},{7,1},{8,10},{10,12},{12... | collective-permute-start | bytes 786440 | tf_op jit(solution)/shard_map/ppermute | solution.py:153
  153.5 8.2 %collective-permute-start.5 = (bf16[128,1024]{0,1:T(8,128)(2,1)}, bf16[128,1024]{0,1:T(8,128)(2,1)}, u32[]{:S(2)}, u32[]{:S(2)}) collective-permute-start(bf16[128,1024]{0,1:T(8,128)(2,1)} %fusion.13), channel_id=1, source_target_pairs={{0,6},{2,0},{4,2},{6,4},{1,7},{3,1},{5,3},{7,5},{8,14},{10,8},{12,... | collective-permute-start | bytes 786440 | tf_op jit(solution)/shard_map/ppermute | solution.py:154
  161.5 8.1 %collective-permute-start.3 = (bf16[128,1024]{0,1:T(8,128)(2,1)S(1)}, bf16[128,1024]{0,1:T(8,128)(2,1)}, u32[]{:S(2)}, u32[]{:S(2)}) collective-permute-start(bf16[128,1024]{0,1:T(8,128)(2,1)S(1)} %fusion.17), channel_id=1, source_target_pairs={{0,2},{2,4},{4,6},{6,0},{1,3},{3,5},{5,7},{7,1},{8,10},{10,12},{12... | collective-permute-start | bytes 786440 | tf_op jit(solution)/shard_map/ppermute | solution.py:153
  163.3 7.9 %collective-permute-start.6 = (bf16[128,1024]{0,1:T(8,128)(2,1)}, bf16[128,1024]{0,1:T(8,128)(2,1)}, u32[]{:S(2)}, u32[]{:S(2)}) collective-permute-start(bf16[128,1024]{0,1:T(8,128)(2,1)} %fusion.14), channel_id=1, source_target_pairs={{0,6},{2,0},{4,2},{6,4},{1,7},{3,1},{5,3},{7,5},{8,14},{10,8},{12,... | collective-permute-start | bytes 786440 | tf_op jit(solution)/shard_map/ppermute | solution.py:154
Sparse Core Ops, SparseCore 0:
  115.4 30.2 reduce-scatter.2
  156.6 19.7 reduce-scatter.4

commit v8 on v5

--- a/solution.py
+++ b/solution.py
@@ -7,7 +7,7 @@
 from jax.experimental.pallas import tpu as pltpu
 from jax.sharding import Mesh, PartitionSpec as P
 
-SEGMENTS = 16
+SEGMENTS = 8
 LANES = 128
 UNROLL = 8
 
@@ -15,13 +15,13 @@
 def _summary_kernel(g_ref, gn_ref, r_ref, drive_ref, up_ref, fa_ref, fb_ref, ba_ref, bb_ref):
     steps, segs, _ = g_ref.shape
     r = r_ref[...]
-    ones = jnp.ones((segs, LANES), jnp.float32)
-    zeros = jnp.zeros((segs, LANES), jnp.float32)
+    ones = jnp.ones(fa_ref.shape, jnp.float32)
+    zeros = jnp.zeros(fb_ref.shape, jnp.float32)
 
     def fwd(i, carry):
         a, b = carry
         d = jnp.exp(-(g_ref[i] * r))
-        x = drive_ref[pl.ds(i, segs, stride=steps), :]
+        x = drive_ref[pl.ds(pl.multiple_of(i * segs, segs), segs), :]
         return (a * d, d * b + x)
 
     a, b = lax.fori_loop(0, steps, fwd, (ones, zeros), unroll=UNROLL)
@@ -32,7 +32,7 @@
         a, b = carry
         i = steps - 1 - j
         e = jnp.exp(-(gn_ref[i] * r))
-        u = up_ref[pl.ds(i, segs, stride=steps), :]
+        u = up_ref[pl.ds(pl.multiple_of(i * segs, segs), segs), :]
         return (a * e, e * b + u)
 
     a, b = lax.fori_loop(0, steps, bwd, (ones, zeros), unroll=UNROLL)
@@ -45,18 +45,20 @@
     r = r_ref[...]
 
     def fwd(i, b):
+        rows = pl.ds(pl.multiple_of(i * segs, segs), segs)
         d = jnp.exp(-(g_ref[i] * r))
-        b = d * b + drive_ref[pl.ds(i, segs, stride=steps), :]
-        st_ref[0, pl.ds(i, segs, stride=steps), :] = b
+        b = d * b + drive_ref[rows, :]
+        st_ref[rows, :] = b
         return b
 
     lax.fori_loop(0, steps, fwd, if_ref[...], unroll=UNROLL)
 
     def bwd(j, b):
         i = steps - 1 - j
+        rows = pl.ds(pl.multiple_of(i * segs, segs), segs)
         e = jnp.exp(-(gn_ref[i] * r))
-        b = e * b + up_ref[pl.ds(i, segs, stride=steps), :]
-        adj_ref[0, pl.ds(i, segs, stride=steps), :] = b
+        b = e * b + up_ref[rows, :]
+        adj_ref[rows, :] = b
         return b
 
     lax.fori_loop(0, steps, bwd, ib_ref[...], unroll=UNROLL)
@@ -64,43 +66,35 @@
 
 def _whole(shape):
     return pl.BlockSpec(shape, lambda j: (0,) * len(shape))
-
-
-def _lane_specs(total, segs):
-    return (
-        pl.BlockSpec((1, LANES), lambda j: (0, j)),
-        pl.BlockSpec((total, LANES), lambda j: (0, j)),
-        pl.BlockSpec((segs, LANES), lambda j: (0, j)),
-    )
 
 
 def local_summaries(g3, gn3, rates2, drive, up):
     total, width = drive.shape
     steps, segs, _ = g3.shape
-    r_spec, col, small = _lane_specs(total, segs)
     seg_shape = jax.ShapeDtypeStruct((segs, width), jnp.float32)
     return pl.pallas_call(
         _summary_kernel,
-        grid=(width // LANES,),
-        in_specs=[_whole(g3.shape), _whole(gn3.shape), r_spec, col, col],
-        out_specs=[small] * 4,
+        grid=(1,),
+        in_specs=[_whole(g3.shape), _whole(gn3.shape), _whole(rates2.shape),
+                  _whole(drive.shape), _whole(up.shape)],
+        out_specs=[_whole((segs, width))] * 4,
         out_shape=[seg_shape] * 4,
+        compiler_params=pltpu.CompilerParams(vmem_limit_bytes=48 * 1024 * 1024),
     )(g3, gn3, rates2, drive, up)
 
 
 def sweeps(g3, gn3, rates2, drive, up, init_f, init_b):
     total, width = drive.shape
-    steps, segs, _ = g3.shape
-    chunks = width // LANES
-    r_spec, col, small = _lane_specs(total, segs)
-    full = jax.ShapeDtypeStruct((chunks, total, LANES), jnp.float32)
-    out = pl.BlockSpec((1, total, LANES), lambda j: (j, 0, 0))
+    full = jax.ShapeDtypeStruct((total, width), jnp.float32)
     return pl.pallas_call(
         _sweep_kernel,
-        grid=(chunks,),
-        in_specs=[_whole(g3.shape), _whole(gn3.shape), r_spec, small, small, col, col],
-        out_specs=[out, out],
+        grid=(1,),
+        in_specs=[_whole(g3.shape), _whole(gn3.shape), _whole(rates2.shape),
+                  _whole(init_f.shape), _whole(init_b.shape),
+                  _whole(drive.shape), _whole(up.shape)],
+        out_specs=[_whole(full.shape)] * 2,
         out_shape=[full, full],
+        compiler_params=pltpu.CompilerParams(vmem_limit_bytes=48 * 1024 * 1024),
     )(g3, gn3, rates2, init_f, init_b, drive, up)
 
 
@@ -144,14 +138,20 @@
     place = lax.axis_index(SEQ)
     factor = 1.0 / math.sqrt(total * peers)
 
-    gain = jnp.sqrt(-jnp.expm1(-2.0 * gaps[:, None] * rates[None, :]))
-    drive = gain * jnp.dot(inputs, w_in, preferred_element_type=jnp.float32)
+    def interleave(x):
+        return x.reshape((segs, steps) + x.shape[1:]).swapaxes(0, 1).reshape(x.shape)
+
+    x_rows = interleave(inputs)
+    c_rows = interleave(cotangent)
+    g_rows = interleave(gaps)
+    gain = jnp.sqrt(-jnp.expm1(-2.0 * g_rows[:, None] * rates[None, :]))
+    drive = gain * jnp.dot(x_rows, w_in, preferred_element_type=jnp.float32)
     upstream = lax.dot_general(
-        cotangent, w_out, (((1,), (1,)), ((), ())), preferred_element_type=jnp.float32
+        c_rows, w_out, (((1,), (1,)), ((), ())), preferred_element_type=jnp.float32
     )
     gaps_next = jnp.concatenate([gaps[1:], jnp.zeros((1,), jnp.float32)], 0)
-    g3 = gaps.reshape(segs, steps).T[:, :, None]
-    gn3 = gaps_next.reshape(segs, steps).T[:, :, None]
+    g3 = g_rows.reshape(steps, segs)[:, :, None]
+    gn3 = interleave(gaps_next).reshape(steps, segs)[:, :, None]
     rates2 = rates[None, :]
 
     fa, fb, ba, bb = local_summaries(g3, gn3, rates2, drive, up=upstream)
@@ -191,26 +191,24 @@
     init_b = jnp.stack(inits_b, 0)
 
     state, adjoint = sweeps(g3, gn3, rates2, drive, upstream, init_f, init_b)
-    chunks = width // LANES
-    gain3 = gain.reshape(total, chunks, LANES).transpose(1, 0, 2)
-    drive_grad = (gain3 * adjoint).astype(jnp.bfloat16)
+    drive_grad = (gain * adjoint).astype(jnp.bfloat16)
     state_low = state.astype(jnp.bfloat16)
     in_term = lax.dot_general(
-        inputs, drive_grad, (((0,), (1,)), ((), ())), preferred_element_type=jnp.float32
-    ).reshape(inputs.shape[1], width) * factor
+        x_rows, drive_grad, (((0,), (0,)), ((), ())), preferred_element_type=jnp.float32
+    ) * factor
     out_term = lax.dot_general(
-        cotangent, state_low, (((0,), (1,)), ((), ())), preferred_element_type=jnp.float32
-    ).reshape(cotangent.shape[1], width) * factor
+        c_rows, state_low, (((0,), (0,)), ((), ())), preferred_element_type=jnp.float32
+    ) * factor
     joined = jnp.concatenate([in_term, out_term], 1).astype(jnp.bfloat16)
     joined = lax.psum_scatter(joined, "sx", scatter_dimension=0, tiled=True)
     joined = lax.psum_scatter(joined, "sz", scatter_dimension=0, tiled=True).astype(jnp.float32)
     d_w_in = joined[:, :width]
     d_w_out = joined[:, width:].T
-    w_in3 = w_in.reshape(w_in.shape[0], chunks, LANES)
     partial_t = lax.dot_general(
-        w_in3, drive_grad, (((1, 2), (0, 2)), ((), ())), preferred_element_type=jnp.float32
+        w_in, drive_grad, (((1,), (1,)), ((), ())), preferred_element_type=jnp.float32
     ).astype(jnp.bfloat16)
-    d_inputs = chan_reduce(partial_t).T
+    d_rows = chan_reduce(partial_t).T
+    d_inputs = d_rows.reshape((steps, segs) + d_rows.shape[1:]).swapaxes(0, 1).reshape(d_rows.shape)
     return (d_inputs, d_w_in, d_w_out)
 
 

time: 191 us -> 162 us (0.85)
  Pallas kernels: 37.5 us -> 23.2 us
  other arithmetic: 21.4 us -> 12.7 us
  local copies, waits for them, and re-layouts: 26.7 us -> 22.8 us
  matrix products: 35.7 us -> 33.4 us
    pallas_call x2, Pallas kernels: 37.5 us -> 23.2 us  [the longest x1 13.1 us: sweeps(): pl.pallas_call(_sweep_kernel, grid=(1,), in_specs=[_whole(g3.shape), _who...]
    unnamed x2 -> x3, waiting for transfers between devices: 0.03 us -> 5.34 us
    unnamed x13 -> x19, local copies, waits for them, and re-layouts: 3.87 us -> 8.59 us
    broadcast_in_dim x2 -> x0, local copies, waits for them, and re-layouts: 3.51 us -> none  [the longest x1 2.11 us: local(): g3 = gaps.reshape(segs, steps).T[:, :, None]]
    reduce_scatter x1 -> x0, waiting for transfers between devices: 3.35 us -> none  [local(): lax.psum_scatter(joined, 'sz', scatter_dimension=0, tiled=True)]
    dot_general x5, matrix products: 35.7 us -> 33.4 us  [the longest x1 7.92 us: local(): lax.dot_general(w_in, drive_grad, (((1,), (1,)), ((), ())), preferred_ele...]
    ppermute x3, waiting for transfers between devices: 12.3 us -> 10.4 us  [chan_reduce(): got_a = lax.ppermute(buf_a.astype(jnp.bfloat16), 'cy', up_ring)]
    another operation x2 -> x4, local copies, waits for them, and re-layouts: 8.35 us -> 9.22 us
  transfers between devices with their start and end apart: 9 -> 9, of which waited for: 6 -> 6; matrix products, arithmetic and copies ran while one was open for 16% -> 21% of each run, Pallas kernels for 0% -> 0%
where the time goes in v8:
time: 162 us; the launch traced here: 161 us
  matrix products  33.4 us (21%)
  blocking collectives  25.7 us (16%)
  Pallas kernels  23.2 us (14%)
  local copies, waits for them, and re-layouts  22.8 us (14%)
  waiting for transfers between devices  18.1 us (11%)
  between operations  14.9 us (9%)
  other arithmetic  12.7 us (8%)
  starting transfers between devices  10.6 us (7%)
    all_gather x1, blocking collectives, local(): lax.all_gather(summary, 'sz')  13.2 us
    pallas_call x1, Pallas kernels, sweeps(): pl.pallas_call(_sweep_kernel, grid=(1,), in_specs=[_whole(g3.shape), _who...  13.1 us
    all_gather x1, blocking collectives, local(): lax.all_gather(lax.all_gather(summary, 'sz'), 'sx').reshape(peers, 3, width)  12.5 us
    ppermute x3, waiting for transfers between devices, chan_reduce(): got_a = lax.ppermute(buf_a.astype(jnp.bfloat16), 'cy', up_ring)  10.4 us
    pallas_call x1, Pallas kernels, local_summaries(): pl.pallas_call(_summary_kernel, grid=(1,), in_specs=[_whole(g3.shape), _w...  10.1 us
    unnamed x19, local copies, waits for them, and re-layouts  8.59 us
    another operation x2, local copies, waits for them, and re-layouts  8.34 us
    ppermute x3, starting transfers between devices, chan_reduce(): got_b = lax.ppermute(buf_b.astype(jnp.bfloat16), 'cy', down_ring)  8.17 us
  transfers between devices with their start and end apart: 9, of which 6 were waited for; matrix products, arithmetic and copies ran while one was open for 21% of the time, Pallas kernels for 0%

profile of v8, /device:TPU:0, one launch (start us, length us, event | category | flops | bytes accessed | tf_op | source)
XLA Modules:
  0.0 161.4 jit_solution(11381776146445678491)
XLA Ops:
  7.2 0.8 reshape.1244
  8.0 0.8 slice.310
  8.8 1.2 slice.327
  10.0 0.1 copy.33
  10.1 0.1 mul.787
  10.2 0.4 copy.38.g_ref
  10.8 0.4 copy.39.gn_ref
  11.2 7.6 %fusion.2.up_ref = f32[2048,512]{1,0:T(8,128)} fusion(bf16[512,1024]{1,0:T(8,128)(2,1)} %param.10, bf16[256,8,1024]{2,0,1:T(8,128)(2,1)} %bitcast.514), kind=kOutput, calls=%fused_computation.3 | convolution fusion | flops 2147483648 | bytes 9437184 | tf_op jit(solution)/shard_map/dot_general | solution.py:149
  18.8 7.3 %fusion.8.drive_ref = f32[2048,512]{1,0:T(8,128)} fusion(bf16[1024,512]{1,0:T(8,128)(2,1)S(1)} %copy-done, bf16[256,8,1024]{2,0,1:T(8,128)(2,1)S(1)} %bitcast.512, f32[512]{0:T(512)S(1)} %copy-done.1, f32[2048]{0:T(1024)S(1)} %mul.787), kind=kOutput, calls=%fused_computation.11 | convolution fusion | flops 2150629376 | bytes 9447424 | tf_op jit(solution)/shard_map/dot_general | solution.py:148
  26.1 10.1 %shard_map.85 = (f32[8,512]{1,0:T(8,128)S(1)}, f32[8,512]{1,0:T(8,128)S(1)}, f32[8,512]{1,0:T(8,128)S(1)}, f32[8,512]{1,0:T(8,128)S(1)}) custom-call(f32[256,8,1]{2,1,0:T(8,128)S(1)} %copy.38.g_ref, f32[256,8,1]{2,1,0:T(8,128)S(1)} %copy.39.gn_ref, f32[1,512]{1,0:T(1,128)S(1)} %bitcast.503, f32[2048,512]{1,0:T(8,128)} %fusion.8.drive_ref, ...), custom_call_target="tpu_custom_call" | custom-call | tf_op jit(solution)/shard_map/pallas_call | solution.py:75
  37.0 13.2 %all-gather.2 = f32[4,3,512]{2,1,0:T(4,128)S(1)} all-gather(f32[1,3,512]{2,1,0:T(4,128)S(1)} %maximum_bitcast_fusion.1), channel_id=2, replica_groups=mesh['sx'=4,'sz'=4,'cy'=4,'cc'=2] {'sz'}, dimensions={0}, use_global_device_ids=true | all-gather | bytes 30720 | tf_op jit(solution)/shard_map/all_gather | solution.py:170
  50.2 12.5 %all-gather.1 = f32[16,3,512]{2,1,0:T(4,128)S(1)} all-gather(f32[4,3,512]{2,1,0:T(4,128)S(1)} %all-gather.2), channel_id=3, replica_groups=mesh['sx'=4,'sz'=4,'cy'=4,'cc'=2] {'sx'}, dimensions={0}, use_global_device_ids=true | all-gather | bytes 122880 | tf_op jit(solution)/shard_map/all_gather | solution.py:170
  62.9 0.1 multiply_add_fusion.8
  63.0 13.1 %shard_map.86 = (f32[2048,512]{1,0:T(8,128)}, f32[2048,512]{1,0:T(8,128)}) custom-call(f32[256,8,1]{2,1,0:T(8,128)S(1)} %copy.38.g_ref, f32[256,8,1]{2,1,0:T(8,128)S(1)} %copy.39.gn_ref, f32[1,512]{1,0:T(1,128)S(1)} %bitcast.504, f32[8,512]{1,0:T(8,128)S(1)} %stack.10.if_ref, f32[8,512]{1,0:T(8,128)S(1)} %stack.11.ib_ref, f32[2048,512]{1,0:T(8,128)} %fusion.8.drive_ref, ...), custom_call_target="tpu_custom_call" | custom-call | tf_op jit(solution)/shard_map/pallas_call | solution.py:89
  76.2 7.6 %fusion.22 = bf16[1024,512]{0,1:T(8,128)(2,1)S(1)} fusion(bf16[256,8,1024]{2,0,1:T(8,128)(2,1)S(1)} %bitcast.513, f32[2048,512]{1,0:T(8,128)} %get-tuple-element.13, f32[512]{0:T(512)S(1)} %copy-done.1, f32[2048]{0:T(1024)S(1)} %mul.787), kind=kOutput, calls=%fused_computation.21 | convolution fusion | flops 2152726528 | bytes 9447424 | tf_op jit(solution)/shard_map/dot_general | solution.py:196
  83.8 3.0 %fusion.25 = bf16[1024,512]{0,1:T(8,128)(2,1)S(1)} fusion(bf16[256,8,1024]{2,0,1:T(8,128)(2,1)S(1)} %bitcast.515, f32[2048,512]{1,0:T(8,128)S(1)} %copy-done.6), kind=kOutput, calls=%fused_computation.22 | convolution fusion | flops 2149580800 | bytes 9437184 | tf_op jit(solution)/shard_map/dot_general | solution.py:199
  86.8 1.6 pad_maximum_fusion
  88.4 0.3 reduce-scatter.7.cloned.1.call-start
  88.7 7.9 %convolution_convert_fusion = bf16[2048,1024]{0,1:T(8,128)(2,1)} fusion(bf16[1024,512]{1,0:T(8,128)(2,1)S(1)} %copy-done, f32[2048,512]{1,0:T(8,128)} %get-tuple-element.13, f32[512]{0:T(512)S(1)} %copy-done.1, f32[2048]{0:T(1024)S(1)} %mul.787), kind=kOutput, calls=%fused_computation.12 | convolution fusion | flops 2153775104 | bytes 9447424 | tf_op jit(solution)/shard_map/dot_general | solution.py:207
  96.6 4.4 %constant_dynamic-slice_fusion.1 = (bf16[4,1,128,2048]{3,2,1,0:T(8,128)(2,1)S(1)}, bf16[4,1,128,2048]{3,2,1,0:T(8,128)(2,1)}) fusion(bf16[4,2,128,2048]{3,2,1,0:T(8,128)(2,1)} %bitcast.505, s32[]{:T(128)S(6)} %select_n.777, s32[]{:T(128)S(6)} %select_n.779), kind=kLoop, calls=%fused_computation.77 | loop fusion | bytes 8388616 | tf_op jit(solution)/shard_map/dynamic-slice
  101.0 4.0 %copy.41 = bf16[4,1,128,2048]{2,3,0,1:T(8,128)(2,1)} copy(bf16[4,1,128,2048]{3,2,1,0:T(8,128)(2,1)} %get-tuple-element.46) | data formatting | bytes 4194304 | tf_op jit(solution)/shard_map/dynamic-slice.1
  104.9 2.6 %copy.47 = bf16[4,1,128,2048]{2,3,0,1:T(8,128)(2,1)} copy(bf16[4,1,128,2048]{3,2,1,0:T(8,128)(2,1)S(1)} %get-tuple-element.45) | data formatting | bytes 4194304
  107.5 1.9 %collective-permute-done = bf16[4,128,2048]{1,2,0:T(8,128)(2,1)} collective-permute-done((bf16[4,128,2048]{1,2,0:T(8,128)(2,1)}, bf16[4,128,2048]{1,2,0:T(8,128)(2,1)}, u32[]{:S(2)}, u32[]{:S(2)}) %collective-permute-start) | collective-permute-done | bytes 2097184 | tf_op jit(solution)/shard_map/ppermute | solution.py:116
  109.4 2.7 %convert_add_fusion = f32[4,128,2048]{1,2,0:T(8,128)S(1)} fusion(bf16[4,128,2048]{1,2,0:T(8,128)(2,1)} %collective-permute-done, bf16[4,1,128,2048]{2,3,0,1:T(8,128)(2,1)} %copy.47), kind=kLoop, calls=%fused_computation | loop fusion | flops 3145728 | bytes 8388608 | tf_op jit(solution)/shard_map/add | solution.py:116
  112.1 0.3 fusion.70
  112.4 1.3 copy-done.2
  113.8 1.7 %collective-permute-start.1 = (bf16[128,1024]{0,1:T(8,128)(2,1)S(1)}, bf16[128,1024]{0,1:T(8,128)(2,1)}, u32[]{:S(2)}, u32[]{:S(2)}) collective-permute-start(bf16[128,1024]{0,1:T(8,128)(2,1)S(1)} %fusion.36), channel_id=1, source_target_pairs={{0,2},{2,4},{4,6},{6,0},{1,3},{3,5},{5,7},{7,1},{8,10},{10,12},{12... | collective-permute-start | bytes 786440 | tf_op jit(solution)/shard_map/ppermute | solution.py:125
  115.4 0.7 fusion.37
  116.2 1.6 %collective-permute-start.4 = (bf16[128,1024]{0,1:T(8,128)(2,1)}, bf16[128,1024]{0,1:T(8,128)(2,1)}, u32[]{:S(2)}, u32[]{:S(2)}) collective-permute-start(bf16[128,1024]{0,1:T(8,128)(2,1)} %fusion.37), channel_id=1, source_target_pairs={{0,6},{2,0},{4,2},{6,4},{1,7},{3,1},{5,3},{7,5},{8,14},{10,8},{12,... | collective-permute-start | bytes 786440 | tf_op jit(solution)/shard_map/ppermute | solution.py:126
  117.8 5.8 %collective-permute-done.1 = bf16[128,1024]{0,1:T(8,128)(2,1)} collective-permute-done((bf16[128,1024]{0,1:T(8,128)(2,1)S(1)}, bf16[128,1024]{0,1:T(8,128)(2,1)}, u32[]{:S(2)}, u32[]{:S(2)}) %collective-permute-start.1) | collective-permute-done | bytes 262176 | tf_op jit(solution)/shard_map/ppermute | solution.py:125
  123.6 1.2 fusion.33
  124.8 0.4 collective-permute-start.2
  125.1 1.7 %fusion.30 = bf16[128,1024]{0,1:T(8,128)(2,1)} fusion(bf16[128,1024]{0,1:T(8,128)(2,1)} %collective-permute-done.4, f32[4,128,1024]{1,2,0:T(8,128)S(1)} %get-tuple-element.44, s32[]{:T(128)S(6)} %select_n.793), kind=kLoop, calls=%fused_computation.25 | loop fusion | flops 393216 | bytes 1048580 | tf_op jit(solution)/shard_map/convert_element_type | solution.py:126
  126.8 3.0 %collective-permute-start.5 = (bf16[128,1024]{0,1:T(8,128)(2,1)}, bf16[128,1024]{0,1:T(8,128)(2,1)}, u32[]{:S(2)}, u32[]{:S(2)}) collective-permute-start(bf16[128,1024]{0,1:T(8,128)(2,1)} %fusion.30), channel_id=1, source_target_pairs={{0,6},{2,0},{4,2},{6,4},{1,7},{3,1},{5,3},{7,5},{8,14},{10,8},{12,... | collective-permute-start | bytes 786440 | tf_op jit(solution)/shard_map/ppermute | solution.py:126
  129.8 2.0 %copy.45 = bf16[256,1024]{1,0:T(8,128)(2,1)} copy(bf16[256,1024]{0,1:T(8,128)(2,1)} %reduce-scatter.5.cloned.1.call-done) | data formatting | bytes 1048576
  131.9 1.9 %collective-permute-done.2 = bf16[128,1024]{0,1:T(8,128)(2,1)} collective-permute-done((bf16[128,1024]{0,1:T(8,128)(2,1)S(1)}, bf16[128,1024]{0,1:T(8,128)(2,1)}, u32[]{:S(2)}, u32[]{:S(2)}) %collective-permute-start.2) | collective-permute-done | bytes 262176 | tf_op jit(solution)/shard_map/ppermute | solution.py:125
  133.8 1.2 fusion.34
  135.0 1.7 %fusion.31 = bf16[128,1024]{0,1:T(8,128)(2,1)} fusion(bf16[128,1024]{0,1:T(8,128)(2,1)} %collective-permute-done.5, f32[4,128,1024]{1,2,0:T(8,128)S(1)} %get-tuple-element.44, s32[]{:T(128)S(6)} %select_n.791), kind=kLoop, calls=%fused_computation.27 | loop fusion | flops 393216 | bytes 1048580 | tf_op jit(solution)/shard_map/convert_element_type | solution.py:126
  136.8 3.6 %collective-permute-start.6 = (bf16[128,1024]{0,1:T(8,128)(2,1)}, bf16[128,1024]{0,1:T(8,128)(2,1)}, u32[]{:S(2)}, u32[]{:S(2)}) collective-permute-start(bf16[128,1024]{0,1:T(8,128)(2,1)} %fusion.31), channel_id=1, source_target_pairs={{0,6},{2,0},{4,2},{6,4},{1,7},{3,1},{5,3},{7,5},{8,14},{10,8},{12,... | collective-permute-start | bytes 786440 | tf_op jit(solution)/shard_map/ppermute | solution.py:126
  140.3 2.7 %collective-permute-done.3 = bf16[128,1024]{0,1:T(8,128)(2,1)} collective-permute-done((bf16[128,1024]{0,1:T(8,128)(2,1)S(1)}, bf16[128,1024]{0,1:T(8,128)(2,1)}, u32[]{:S(2)}, u32[]{:S(2)}) %collective-permute-start.3) | collective-permute-done | bytes 262176 | tf_op jit(solution)/shard_map/ppermute | solution.py:125
  143.1 1.2 fusion.35
  144.3 0.4 collective-permute-done.6
  144.6 1.0 fusion.32
  145.7 0.9 copy.42
  146.6 5.3 %reduce-scatter.7.cloned.1.call-done = bf16[64,1024]{1,0:T(8,128)(2,1)} async-done(((bf16[256,1024]{1,0:T(8,128)(2,1)}), bf16[64,1024]{1,0:T(8,128)(2,1)}) %reduce-scatter.7.cloned.1.call-update) | async-done | bytes 131088
  151.9 1.1 copy.46
  153.1 0.8 copy.44
  153.8 0.8 copy.43
  (37 shorter events, 0.7 us)
Async XLA Ops:
  7.2 11.7 %copy-start = (bf16[1024,512]{1,0:T(8,128)(2,1)S(1)}, bf16[1024,512]{1,0:T(8,128)(2,1)}, u32[]{:S(2)}) copy-start(bf16[1024,512]{1,0:T(8,128)(2,1)} %param.9) | copy-start | bytes 3145732
  7.2 122.6 %reduce-scatter.5.cloned.1.call-start = ((), (), s32[]{:S(2)}) async-start(), calls=%async_computation.2 | async-start | bytes 2621440 | tf_op jit(solution)/shard_map/reduce_scatter | solution.py:203
  11.2 7.6 %copy-start.1 = (f32[512]{0:T(512)S(1)}, f32[512]{0:T(512)}, u32[]{:S(2)}) copy-start(f32[512]{0:T(512)} %param.8) | copy-start | bytes 6148
  11.2 7.6 %copy-start.3 = (bf16[2048,1024]{1,0:T(8,128)(2,1)S(1)}, bf16[2048,1024]{1,0:T(8,128)(2,1)}, u32[]{:S(2)}) copy-start(bf16[2048,1024]{1,0:T(8,128)(2,1)} %param.6) | copy-start | bytes 12582916
  63.0 13.1 %copy-start.4 = (bf16[2048,1024]{1,0:T(8,128)(2,1)S(1)}, bf16[2048,1024]{1,0:T(8,128)(2,1)}, u32[]{:S(2)}) copy-start(bf16[2048,1024]{1,0:T(8,128)(2,1)} %param.6) | copy-start | bytes 12582916
  76.2 7.6 %copy-start.5 = (bf16[2048,1024]{1,0:T(8,128)(2,1)S(1)}, bf16[2048,1024]{1,0:T(8,128)(2,1)}, u32[]{:S(2)}) copy-start(bf16[2048,1024]{1,0:T(8,128)(2,1)} %param.11) | copy-start | bytes 12582916
  76.2 7.6 %copy-start.6 = (f32[2048,512]{1,0:T(8,128)S(1)}, f32[2048,512]{1,0:T(8,128)}, u32[]{:S(2)}) copy-start(f32[2048,512]{1,0:T(8,128)} %get-tuple-element.14) | copy-start | bytes 12582916
  88.4 63.5 %reduce-scatter.7.cloned.1.call-start = ((), (), s32[]{:S(2)}) async-start(), calls=%async_computation.3 | async-start | bytes 655360
  104.9 4.5 %collective-permute-start = (bf16[4,128,2048]{1,2,0:T(8,128)(2,1)}, bf16[4,128,2048]{1,2,0:T(8,128)(2,1)}, u32[]{:S(2)}, u32[]{:S(2)}) collective-permute-start(bf16[4,128,2048]{1,2,0:T(8,128)(2,1)} %bitcast.506), channel_id=1, source_target_pairs={{0,1},{1,0},{2,3},{3,2},{4,5},{5,4},{6,7},{7,6},{8,9},{9,8},{10,11... | collective-permute-start | bytes 6291464 | tf_op jit(solution)/shard_map/ppermute | solution.py:116
  112.4 1.3 copy-start.2
  113.8 9.8 %collective-permute-start.1 = (bf16[128,1024]{0,1:T(8,128)(2,1)S(1)}, bf16[128,1024]{0,1:T(8,128)(2,1)}, u32[]{:S(2)}, u32[]{:S(2)}) collective-permute-start(bf16[128,1024]{0,1:T(8,128)(2,1)S(1)} %fusion.36), channel_id=1, source_target_pairs={{0,2},{2,4},{4,6},{6,0},{1,3},{3,5},{5,7},{7,1},{8,10},{10,12},{12... | collective-permute-start | bytes 786440 | tf_op jit(solution)/shard_map/ppermute | solution.py:125
  116.2 9.0 %collective-permute-start.4 = (bf16[128,1024]{0,1:T(8,128)(2,1)}, bf16[128,1024]{0,1:T(8,128)(2,1)}, u32[]{:S(2)}, u32[]{:S(2)}) collective-permute-start(bf16[128,1024]{0,1:T(8,128)(2,1)} %fusion.37), channel_id=1, source_target_pairs={{0,6},{2,0},{4,2},{6,4},{1,7},{3,1},{5,3},{7,5},{8,14},{10,8},{12,... | collective-permute-start | bytes 786440 | tf_op jit(solution)/shard_map/ppermute | solution.py:126
  124.8 9.0 %collective-permute-start.2 = (bf16[128,1024]{0,1:T(8,128)(2,1)S(1)}, bf16[128,1024]{0,1:T(8,128)(2,1)}, u32[]{:S(2)}, u32[]{:S(2)}) collective-permute-start(bf16[128,1024]{0,1:T(8,128)(2,1)S(1)} %fusion.33), channel_id=1, source_target_pairs={{0,2},{2,4},{4,6},{6,0},{1,3},{3,5},{5,7},{7,1},{8,10},{10,12},{12... | collective-permute-start | bytes 786440 | tf_op jit(solution)/shard_map/ppermute | solution.py:125
  126.8 8.2 %collective-permute-start.5 = (bf16[128,1024]{0,1:T(8,128)(2,1)}, bf16[128,1024]{0,1:T(8,128)(2,1)}, u32[]{:S(2)}, u32[]{:S(2)}) collective-permute-start(bf16[128,1024]{0,1:T(8,128)(2,1)} %fusion.30), channel_id=1, source_target_pairs={{0,6},{2,0},{4,2},{6,4},{1,7},{3,1},{5,3},{7,5},{8,14},{10,8},{12,... | collective-permute-start | bytes 786440 | tf_op jit(solution)/shard_map/ppermute | solution.py:126
  134.9 8.1 %collective-permute-start.3 = (bf16[128,1024]{0,1:T(8,128)(2,1)S(1)}, bf16[128,1024]{0,1:T(8,128)(2,1)}, u32[]{:S(2)}, u32[]{:S(2)}) collective-permute-start(bf16[128,1024]{0,1:T(8,128)(2,1)S(1)} %fusion.34), channel_id=1, source_target_pairs={{0,2},{2,4},{4,6},{6,0},{1,3},{3,5},{5,7},{7,1},{8,10},{10,12},{12... | collective-permute-start | bytes 786440 | tf_op jit(solution)/shard_map/ppermute | solution.py:125
  136.8 7.9 %collective-permute-start.6 = (bf16[128,1024]{0,1:T(8,128)(2,1)}, bf16[128,1024]{0,1:T(8,128)(2,1)}, u32[]{:S(2)}, u32[]{:S(2)}) collective-permute-start(bf16[128,1024]{0,1:T(8,128)(2,1)} %fusion.31), channel_id=1, source_target_pairs={{0,6},{2,0},{4,2},{6,4},{1,7},{3,1},{5,3},{7,5},{8,14},{10,8},{12,... | collective-permute-start | bytes 786440 | tf_op jit(solution)/shard_map/ppermute | solution.py:126
Sparse Core Ops, SparseCore 0:
  88.5 30.2 reduce-scatter.4
  132.0 19.8 reduce-scatter.6

commit v9 on v8

--- a/solution.py
+++ b/solution.py
@@ -12,89 +12,125 @@
 UNROLL = 8
 
 
-def _summary_kernel(g_ref, gn_ref, r_ref, drive_ref, up_ref, fa_ref, fb_ref, ba_ref, bb_ref):
-    steps, segs, _ = g_ref.shape
+ROWS = 512
+
+
+def _summary_kernel(g_ref, gn_ref, r_ref, drive_ref, up_ref, fa_ref, fb_ref, ba_ref, bb_ref,
+                    fa_s, fb_s, ba_s, bb_s):
+    segs = fa_ref.shape[0]
+    per = drive_ref.shape[0] // segs
+    j = pl.program_id(0)
+    last = pl.num_programs(0) - 1
     r = r_ref[...]
-    ones = jnp.ones(fa_ref.shape, jnp.float32)
-    zeros = jnp.zeros(fb_ref.shape, jnp.float32)
+
+    @pl.when(j == 0)
+    def _():
+        fa_s[...] = jnp.ones(fa_s.shape, jnp.float32)
+        fb_s[...] = jnp.zeros(fb_s.shape, jnp.float32)
+        ba_s[...] = jnp.ones(ba_s.shape, jnp.float32)
+        bb_s[...] = jnp.zeros(bb_s.shape, jnp.float32)
 
     def fwd(i, carry):
         a, b = carry
-        d = jnp.exp(-(g_ref[i] * r))
+        d = jnp.exp(-(g_ref[j * per + i] * r))
         x = drive_ref[pl.ds(pl.multiple_of(i * segs, segs), segs), :]
         return (a * d, d * b + x)
 
-    a, b = lax.fori_loop(0, steps, fwd, (ones, zeros), unroll=UNROLL)
-    fa_ref[...] = a
-    fb_ref[...] = b
-
-    def bwd(j, carry):
+    a, b = lax.fori_loop(0, per, fwd, (fa_s[...], fb_s[...]), unroll=UNROLL)
+    fa_s[...] = a
+    fb_s[...] = b
+
+    def bwd(k, carry):
         a, b = carry
-        i = steps - 1 - j
-        e = jnp.exp(-(gn_ref[i] * r))
+        i = per - 1 - k
+        e = jnp.exp(-(gn_ref[(last - j) * per + i] * r))
         u = up_ref[pl.ds(pl.multiple_of(i * segs, segs), segs), :]
         return (a * e, e * b + u)
 
-    a, b = lax.fori_loop(0, steps, bwd, (ones, zeros), unroll=UNROLL)
-    ba_ref[...] = a
-    bb_ref[...] = b
-
-
-def _sweep_kernel(g_ref, gn_ref, r_ref, if_ref, ib_ref, drive_ref, up_ref, st_ref, adj_ref):
-    steps, segs, _ = g_ref.shape
+    a, b = lax.fori_loop(0, per, bwd, (ba_s[...], bb_s[...]), unroll=UNROLL)
+    ba_s[...] = a
+    bb_s[...] = b
+
+    @pl.when(j == last)
+    def _():
+        fa_ref[...] = fa_s[...]
+        fb_ref[...] = fb_s[...]
+        ba_ref[...] = ba_s[...]
+        bb_ref[...] = bb_s[...]
+
+
+def _sweep_kernel(g_ref, gn_ref, r_ref, if_ref, ib_ref, drive_ref, up_ref, st_ref, adj_ref,
+                  f_s, b_s):
+    segs = f_s.shape[0]
+    per = drive_ref.shape[0] // segs
+    j = pl.program_id(0)
+    last = pl.num_programs(0) - 1
     r = r_ref[...]
+
+    @pl.when(j == 0)
+    def _():
+        f_s[...] = if_ref[...]
+        b_s[...] = ib_ref[...]
 
     def fwd(i, b):
         rows = pl.ds(pl.multiple_of(i * segs, segs), segs)
-        d = jnp.exp(-(g_ref[i] * r))
+        d = jnp.exp(-(g_ref[j * per + i] * r))
         b = d * b + drive_ref[rows, :]
         st_ref[rows, :] = b
         return b
 
-    lax.fori_loop(0, steps, fwd, if_ref[...], unroll=UNROLL)
-
-    def bwd(j, b):
-        i = steps - 1 - j
+    f_s[...] = lax.fori_loop(0, per, fwd, f_s[...], unroll=UNROLL)
+
+    def bwd(k, b):
+        i = per - 1 - k
         rows = pl.ds(pl.multiple_of(i * segs, segs), segs)
-        e = jnp.exp(-(gn_ref[i] * r))
+        e = jnp.exp(-(gn_ref[(last - j) * per + i] * r))
         b = e * b + up_ref[rows, :]
         adj_ref[rows, :] = b
         return b
 
-    lax.fori_loop(0, steps, bwd, ib_ref[...], unroll=UNROLL)
+    b_s[...] = lax.fori_loop(0, per, bwd, b_s[...], unroll=UNROLL)
 
 
 def _whole(shape):
     return pl.BlockSpec(shape, lambda j: (0,) * len(shape))
+
+
+def _row_specs(total, width):
+    blocks = total // ROWS
+    ahead = pl.BlockSpec((ROWS, width), lambda j: (j, 0))
+    behind = pl.BlockSpec((ROWS, width), lambda j: (blocks - 1 - j, 0))
+    return blocks, ahead, behind
 
 
 def local_summaries(g3, gn3, rates2, drive, up):
     total, width = drive.shape
     steps, segs, _ = g3.shape
+    blocks, ahead, behind = _row_specs(total, width)
     seg_shape = jax.ShapeDtypeStruct((segs, width), jnp.float32)
     return pl.pallas_call(
         _summary_kernel,
-        grid=(1,),
-        in_specs=[_whole(g3.shape), _whole(gn3.shape), _whole(rates2.shape),
-                  _whole(drive.shape), _whole(up.shape)],
+        grid=(blocks,),
+        in_specs=[_whole(g3.shape), _whole(gn3.shape), _whole(rates2.shape), ahead, behind],
         out_specs=[_whole((segs, width))] * 4,
         out_shape=[seg_shape] * 4,
-        compiler_params=pltpu.CompilerParams(vmem_limit_bytes=48 * 1024 * 1024),
+        scratch_shapes=[pltpu.VMEM((segs, width), jnp.float32)] * 4,
     )(g3, gn3, rates2, drive, up)
 
 
 def sweeps(g3, gn3, rates2, drive, up, init_f, init_b):
     total, width = drive.shape
+    steps, segs, _ = g3.shape
+    blocks, ahead, behind = _row_specs(total, width)
     full = jax.ShapeDtypeStruct((total, width), jnp.float32)
     return pl.pallas_call(
         _sweep_kernel,
-        grid=(1,),
+        grid=(blocks,),
         in_specs=[_whole(g3.shape), _whole(gn3.shape), _whole(rates2.shape),
-                  _whole(init_f.shape), _whole(init_b.shape),
-                  _whole(drive.shape), _whole(up.shape)],
-        out_specs=[_whole(full.shape)] * 2,
+                  _whole(init_f.shape), _whole(init_b.shape), ahead, behind],
+        out_specs=[ahead, behind],
         out_shape=[full, full],
-        compiler_params=pltpu.CompilerParams(vmem_limit_bytes=48 * 1024 * 1024),
+        scratch_shapes=[pltpu.VMEM((segs, width), jnp.float32)] * 2,
     )(g3, gn3, rates2, init_f, init_b, drive, up)
 
 

time: 162 us -> 170 us (1.049)
  other arithmetic: 12.7 us -> 18 us
  local copies, waits for them, and re-layouts: 22.8 us -> 25.8 us
  Pallas kernels: 23.2 us -> 21.4 us
    pallas_call x2, Pallas kernels: 23.2 us -> 21.4 us  [the longest x1 11.4 us: sweeps(): pl.pallas_call(_sweep_kernel, grid=(blocks,), in_specs=[_whole(g3.shape),...]
    unnamed x19 -> x21, local copies, waits for them, and re-layouts: 8.59 us -> 8.53 us
  transfers between devices with their start and end apart: 9 -> 9, of which waited for: 6 -> 6; matrix products, arithmetic and copies ran while one was open for 21% -> 20% of each run, Pallas kernels for 0% -> 0%
where the time goes in v9:
time: 170 us; the launch traced here: 169 us
  matrix products  34.6 us (20%)
  local copies, waits for them, and re-layouts  25.8 us (15%)
  blocking collectives  25.8 us (15%)
  Pallas kernels  21.4 us (13%)
  waiting for transfers between devices  18.1 us (11%)
  other arithmetic  18 us (11%)
  between operations  14.8 us (9%)
  starting transfers between devices  10.6 us (6%)
    all_gather x1, blocking collectives, local(): lax.all_gather(summary, 'sz')  13.2 us
    all_gather x1, blocking collectives, local(): lax.all_gather(lax.all_gather(summary, 'sz'), 'sx').reshape(peers, 3, width)  12.5 us
    pallas_call x1, Pallas kernels, sweeps(): pl.pallas_call(_sweep_kernel, grid=(blocks,), in_specs=[_whole(g3.shape),...  11.4 us
    ppermute x3, waiting for transfers between devices, chan_reduce(): got_a = lax.ppermute(buf_a.astype(jnp.bfloat16), 'cy', up_ring)  10.3 us
    pallas_call x1, Pallas kernels, local_summaries(): pl.pallas_call(_summary_kernel, grid=(blocks,), in_specs=[_whole(g3.shape...  9.98 us
    dot_general x1, matrix products, local(): lax.dot_general(x_rows, drive_grad, (((0,), (0,)), ((), ())), preferred_e...  8.84 us
    unnamed x21, local copies, waits for them, and re-layouts  8.53 us
    another operation x2, local copies, waits for them, and re-layouts  8.36 us
  transfers between devices with their start and end apart: 9, of which 6 were waited for; matrix products, arithmetic and copies ran while one was open for 20% of the time, Pallas kernels for 0%

profile of v9, /device:TPU:0, one launch (start us, length us, event | category | flops | bytes accessed | tf_op | source)
XLA Modules:
  0.0 169.0 jit_solution(9457155105312464118)
XLA Ops:
  7.2 0.8 reshape.1244
  8.0 0.8 slice.310
  8.8 1.2 slice.327
  10.2 1.4 copy.38.g_ref
  11.7 1.3 copy.39.gn_ref
  13.0 7.6 %fusion.2.up_ref = f32[2048,512]{1,0:T(8,128)} fusion(bf16[512,1024]{1,0:T(8,128)(2,1)} %param.10, bf16[256,8,1024]{2,0,1:T(8,128)(2,1)} %bitcast.514), kind=kOutput, calls=%fused_computation.3 | convolution fusion | flops 2147483648 | bytes 9437184 | tf_op jit(solution)/shard_map/dot_general | solution.py:185
  20.7 7.2 %fusion.8.drive_ref = f32[2048,512]{1,0:T(8,128)} fusion(bf16[1024,512]{1,0:T(8,128)(2,1)S(1)} %copy-done, bf16[256,8,1024]{2,0,1:T(8,128)(2,1)S(1)} %bitcast.513, f32[512]{0:T(512)S(1)} %copy-done.2, f32[2048]{0:T(1024)S(1)} %mul.787), kind=kOutput, calls=%fused_computation.11 | convolution fusion | flops 2150629376 | bytes 9447424 | tf_op jit(solution)/shard_map/dot_general | solution.py:184
  27.9 10.0 %shard_map.85 = (f32[8,512]{1,0:T(8,128)}, f32[8,512]{1,0:T(8,128)}, f32[8,512]{1,0:T(8,128)}, f32[8,512]{1,0:T(8,128)}) custom-call(f32[256,8,1]{2,1,0:T(8,128)} %copy.38.g_ref, f32[256,8,1]{2,1,0:T(8,128)} %copy.39.gn_ref, f32[1,512]{1,0:T(1,128)} %bitcast.508, f32[2048,512]{1,0:T(8,128)} %fusion.8.drive_ref, f32[2048,512]{1,0:T(8,128)} %fusion.2.up_ref), custom_call_target="tpu_custom_call" | custom-call | tf_op jit(solution)/shard_map/pallas_call | solution.py:111
  37.9 1.0 multiply_multiply_fusion
  38.9 1.1 multiply_add_fusion.15
  40.5 1.3 multiply_add_fusion
  41.8 13.2 %all-gather.2 = f32[4,3,512]{2,1,0:T(4,128)S(1)} all-gather(f32[1,3,512]{2,1,0:T(4,128)S(1)} %maximum_bitcast_fusion.1), channel_id=2, replica_groups=mesh['sx'=4,'sz'=4,'cy'=4,'cc'=2] {'sz'}, dimensions={0}, use_global_device_ids=true | all-gather | bytes 30720 | tf_op jit(solution)/shard_map/all_gather | solution.py:206
  55.1 12.5 %all-gather.1 = f32[16,3,512]{2,1,0:T(4,128)S(1)} all-gather(f32[4,3,512]{2,1,0:T(4,128)S(1)} %all-gather.2), channel_id=3, replica_groups=mesh['sx'=4,'sz'=4,'cy'=4,'cc'=2] {'sx'}, dimensions={0}, use_global_device_ids=true | all-gather | bytes 122880 | tf_op jit(solution)/shard_map/all_gather | solution.py:206
  67.6 1.3 multiply_add_fusion.1
  68.9 0.6 stack.11.ib_ref
  69.5 1.1 multiply_add_fusion.8
  70.6 0.6 stack.10.if_ref
  71.2 11.4 %shard_map.86 = (f32[2048,512]{1,0:T(8,128)}, f32[2048,512]{1,0:T(8,128)}) custom-call(f32[256,8,1]{2,1,0:T(8,128)} %copy.38.g_ref, f32[256,8,1]{2,1,0:T(8,128)} %copy.39.gn_ref, f32[1,512]{1,0:T(1,128)} %bitcast.509, f32[8,512]{1,0:T(8,128)} %stack.10.if_ref, f32[8,512]{1,0:T(8,128)} %stack.11.ib_ref, f32[2048,512]{1,0:T(8,128)} %fusion.8.drive_ref, ...), custom_call_target="tpu_custom_call" | custom-call | tf_op jit(solution)/shard_map/pallas_call | solution.py:126
  82.6 8.8 %fusion.22 = bf16[1024,512]{0,1:T(8,128)(2,1)S(1)} fusion(bf16[256,8,1024]{2,0,1:T(8,128)(2,1)} %bitcast.512, f32[2048,512]{1,0:T(8,128)} %get-tuple-element.13, f32[512]{0:T(512)S(1)} %copy-done.4, f32[2048]{0:T(1024)S(1)} %mul.787), kind=kOutput, calls=%fused_computation.21 | convolution fusion | flops 2152726528 | bytes 9447424 | tf_op jit(solution)/shard_map/dot_general | solution.py:232
  91.5 3.0 %fusion.25 = bf16[1024,512]{0,1:T(8,128)(2,1)S(1)} fusion(bf16[256,8,1024]{2,0,1:T(8,128)(2,1)S(1)} %bitcast.515, f32[2048,512]{1,0:T(8,128)S(1)} %copy-done.7), kind=kOutput, calls=%fused_computation.22 | convolution fusion | flops 2149580800 | bytes 9437184 | tf_op jit(solution)/shard_map/dot_general | solution.py:235
  94.5 1.5 pad_maximum_fusion
  96.3 7.9 %convolution_convert_fusion = bf16[2048,1024]{0,1:T(8,128)(2,1)} fusion(bf16[1024,512]{1,0:T(8,128)(2,1)S(1)} %copy-done, f32[2048,512]{1,0:T(8,128)} %get-tuple-element.13, f32[512]{0:T(512)S(1)} %copy-done.4, f32[2048]{0:T(1024)S(1)} %mul.787), kind=kOutput, calls=%fused_computation.12 | convolution fusion | flops 2153775104 | bytes 9447424 | tf_op jit(solution)/shard_map/dot_general | solution.py:243
  104.2 4.4 %constant_dynamic-slice_fusion.1 = (bf16[4,1,128,2048]{3,2,1,0:T(8,128)(2,1)S(1)}, bf16[4,1,128,2048]{3,2,1,0:T(8,128)(2,1)}) fusion(bf16[4,2,128,2048]{3,2,1,0:T(8,128)(2,1)} %bitcast.503, s32[]{:T(128)S(6)} %select_n.777, s32[]{:T(128)S(6)} %select_n.779), kind=kLoop, calls=%fused_computation.77 | loop fusion | bytes 8388616 | tf_op jit(solution)/shard_map/dynamic-slice
  108.6 3.9 %copy.41 = bf16[4,1,128,2048]{2,3,0,1:T(8,128)(2,1)} copy(bf16[4,1,128,2048]{3,2,1,0:T(8,128)(2,1)} %get-tuple-element.46) | data formatting | bytes 4194304 | tf_op jit(solution)/shard_map/dynamic-slice.1
  112.5 2.5 %copy.47 = bf16[4,1,128,2048]{2,3,0,1:T(8,128)(2,1)} copy(bf16[4,1,128,2048]{3,2,1,0:T(8,128)(2,1)S(1)} %get-tuple-element.45) | data formatting | bytes 4194304
  115.1 2.0 %collective-permute-done = bf16[4,128,2048]{1,2,0:T(8,128)(2,1)} collective-permute-done((bf16[4,128,2048]{1,2,0:T(8,128)(2,1)}, bf16[4,128,2048]{1,2,0:T(8,128)(2,1)}, u32[]{:S(2)}, u32[]{:S(2)}) %collective-permute-start) | collective-permute-done | bytes 2097184 | tf_op jit(solution)/shard_map/ppermute | solution.py:152
  117.0 2.7 %convert_add_fusion = f32[4,128,2048]{1,2,0:T(8,128)S(1)} fusion(bf16[4,128,2048]{1,2,0:T(8,128)(2,1)} %collective-permute-done, bf16[4,1,128,2048]{2,3,0,1:T(8,128)(2,1)} %copy.47), kind=kLoop, calls=%fused_computation | loop fusion | flops 3145728 | bytes 8388608 | tf_op jit(solution)/shard_map/add | solution.py:152
  120.0 1.3 copy-done.1
  121.4 1.6 collective-permute-start.1
  123.0 0.7 fusion.37
  123.7 1.7 collective-permute-start.4
  125.4 5.8 %collective-permute-done.1 = bf16[128,1024]{0,1:T(8,128)(2,1)} collective-permute-done((bf16[128,1024]{0,1:T(8,128)(2,1)S(1)}, bf16[128,1024]{0,1:T(8,128)(2,1)}, u32[]{:S(2)}, u32[]{:S(2)}) %collective-permute-start.1) | collective-permute-done | bytes 262176 | tf_op jit(solution)/shard_map/ppermute | solution.py:161
  131.2 1.2 fusion.33
  132.7 1.7 %fusion.30 = bf16[128,1024]{0,1:T(8,128)(2,1)} fusion(bf16[128,1024]{0,1:T(8,128)(2,1)} %collective-permute-done.4, f32[4,128,1024]{1,2,0:T(8,128)S(1)} %get-tuple-element.44, s32[]{:T(128)S(6)} %select_n.793), kind=kLoop, calls=%fused_computation.25 | loop fusion | flops 393216 | bytes 1048580 | tf_op jit(solution)/shard_map/convert_element_type | solution.py:162
  134.4 2.9 %collective-permute-start.5 = (bf16[128,1024]{0,1:T(8,128)(2,1)}, bf16[128,1024]{0,1:T(8,128)(2,1)}, u32[]{:S(2)}, u32[]{:S(2)}) collective-permute-start(bf16[128,1024]{0,1:T(8,128)(2,1)} %fusion.30), channel_id=1, source_target_pairs={{0,6},{2,0},{4,2},{6,4},{1,7},{3,1},{5,3},{7,5},{8,14},{10,8},{12,... | collective-permute-start | bytes 786440 | tf_op jit(solution)/shard_map/ppermute | solution.py:162
  137.4 2.0 %copy.45 = bf16[256,1024]{1,0:T(8,128)(2,1)} copy(bf16[256,1024]{0,1:T(8,128)(2,1)} %reduce-scatter.5.cloned.1.call-done) | data formatting | bytes 1048576
  139.4 1.9 %collective-permute-done.2 = bf16[128,1024]{0,1:T(8,128)(2,1)} collective-permute-done((bf16[128,1024]{0,1:T(8,128)(2,1)S(1)}, bf16[128,1024]{0,1:T(8,128)(2,1)}, u32[]{:S(2)}, u32[]{:S(2)}) %collective-permute-start.2) | collective-permute-done | bytes 262176 | tf_op jit(solution)/shard_map/ppermute | solution.py:161
  141.3 1.2 fusion.34
  142.6 1.7 %fusion.31 = bf16[128,1024]{0,1:T(8,128)(2,1)} fusion(bf16[128,1024]{0,1:T(8,128)(2,1)} %collective-permute-done.5, f32[4,128,1024]{1,2,0:T(8,128)S(1)} %get-tuple-element.44, s32[]{:T(128)S(6)} %select_n.791), kind=kLoop, calls=%fused_computation.27 | loop fusion | flops 393216 | bytes 1048580 | tf_op jit(solution)/shard_map/convert_element_type | solution.py:162
  144.3 3.6 %collective-permute-start.6 = (bf16[128,1024]{0,1:T(8,128)(2,1)}, bf16[128,1024]{0,1:T(8,128)(2,1)}, u32[]{:S(2)}, u32[]{:S(2)}) collective-permute-start(bf16[128,1024]{0,1:T(8,128)(2,1)} %fusion.31), channel_id=1, source_target_pairs={{0,6},{2,0},{4,2},{6,4},{1,7},{3,1},{5,3},{7,5},{8,14},{10,8},{12,... | collective-permute-start | bytes 786440 | tf_op jit(solution)/shard_map/ppermute | solution.py:162
  147.9 2.7 %collective-permute-done.3 = bf16[128,1024]{0,1:T(8,128)(2,1)} collective-permute-done((bf16[128,1024]{0,1:T(8,128)(2,1)S(1)}, bf16[128,1024]{0,1:T(8,128)(2,1)}, u32[]{:S(2)}, u32[]{:S(2)}) %collective-permute-start.3) | collective-permute-done | bytes 262176 | tf_op jit(solution)/shard_map/ppermute | solution.py:161
  150.5 1.2 fusion.35
  152.1 1.0 fusion.32
  153.2 0.9 copy.42
  154.0 5.4 %reduce-scatter.7.cloned.1.call-done = bf16[64,1024]{1,0:T(8,128)(2,1)} async-done(((bf16[256,1024]{1,0:T(8,128)(2,1)}), bf16[64,1024]{1,0:T(8,128)(2,1)}) %reduce-scatter.7.cloned.1.call-update) | async-done | bytes 131088
  159.5 1.1 copy.46
  160.6 0.8 copy.44
  161.4 0.8 copy.43
  (39 shorter events, 2.0 us)
Async XLA Ops:
  7.2 13.5 %copy-start = (bf16[1024,512]{1,0:T(8,128)(2,1)S(1)}, bf16[1024,512]{1,0:T(8,128)(2,1)}, u32[]{:S(2)}) copy-start(bf16[1024,512]{1,0:T(8,128)(2,1)} %param.9) | copy-start | bytes 3145732
  7.2 130.2 %reduce-scatter.5.cloned.1.call-start = ((), (), s32[]{:S(2)}) async-start(), calls=%async_computation.2 | async-start | bytes 2621440 | tf_op jit(solution)/shard_map/reduce_scatter | solution.py:239
  13.0 7.6 %copy-start.2 = (f32[512]{0:T(512)S(1)}, f32[512]{0:T(512)}, u32[]{:S(2)}) copy-start(f32[512]{0:T(512)} %param.8) | copy-start | bytes 6148
  13.0 7.6 %copy-start.5 = (bf16[2048,1024]{1,0:T(8,128)(2,1)S(1)}, bf16[2048,1024]{1,0:T(8,128)(2,1)}, u32[]{:S(2)}) copy-start(bf16[2048,1024]{1,0:T(8,128)(2,1)} %param.6) | copy-start | bytes 12582916
  27.9 13.9 %copy-start.3 = (f32[512]{0:T(512)S(1)}, f32[512]{0:T(512)}, u32[]{:S(2)}) copy-start(f32[512]{0:T(512)} %param.8) | copy-start | bytes 6148
  71.2 11.4 %copy-start.4 = (f32[512]{0:T(512)S(1)}, f32[512]{0:T(512)}, u32[]{:S(2)}) copy-start(f32[512]{0:T(512)} %param.8) | copy-start | bytes 6148
  82.6 8.9 %copy-start.6 = (bf16[2048,1024]{1,0:T(8,128)(2,1)S(1)}, bf16[2048,1024]{1,0:T(8,128)(2,1)}, u32[]{:S(2)}) copy-start(bf16[2048,1024]{1,0:T(8,128)(2,1)} %param.11) | copy-start | bytes 12582916
  82.6 8.9 %copy-start.7 = (f32[2048,512]{1,0:T(8,128)S(1)}, f32[2048,512]{1,0:T(8,128)}, u32[]{:S(2)}) copy-start(f32[2048,512]{1,0:T(8,128)} %get-tuple-element.14) | copy-start | bytes 12582916
  96.0 63.4 %reduce-scatter.7.cloned.1.call-start = ((), (), s32[]{:S(2)}) async-start(), calls=%async_computation.3 | async-start | bytes 655360
  112.5 4.5 %collective-permute-start = (bf16[4,128,2048]{1,2,0:T(8,128)(2,1)}, bf16[4,128,2048]{1,2,0:T(8,128)(2,1)}, u32[]{:S(2)}, u32[]{:S(2)}) collective-permute-start(bf16[4,128,2048]{1,2,0:T(8,128)(2,1)} %bitcast.504), channel_id=1, source_target_pairs={{0,1},{1,0},{2,3},{3,2},{4,5},{5,4},{6,7},{7,6},{8,9},{9,8},{10,11... | collective-permute-start | bytes 6291464 | tf_op jit(solution)/shard_map/ppermute | solution.py:152
  120.0 1.3 copy-start.1
  121.4 9.8 %collective-permute-start.1 = (bf16[128,1024]{0,1:T(8,128)(2,1)S(1)}, bf16[128,1024]{0,1:T(8,128)(2,1)}, u32[]{:S(2)}, u32[]{:S(2)}) collective-permute-start(bf16[128,1024]{0,1:T(8,128)(2,1)S(1)} %fusion.36), channel_id=1, source_target_pairs={{0,2},{2,4},{4,6},{6,0},{1,3},{3,5},{5,7},{7,1},{8,10},{10,12},{12... | collective-permute-start | bytes 786440 | tf_op jit(solution)/shard_map/ppermute | solution.py:161
  123.7 9.0 %collective-permute-start.4 = (bf16[128,1024]{0,1:T(8,128)(2,1)}, bf16[128,1024]{0,1:T(8,128)(2,1)}, u32[]{:S(2)}, u32[]{:S(2)}) collective-permute-start(bf16[128,1024]{0,1:T(8,128)(2,1)} %fusion.37), channel_id=1, source_target_pairs={{0,6},{2,0},{4,2},{6,4},{1,7},{3,1},{5,3},{7,5},{8,14},{10,8},{12,... | collective-permute-start | bytes 786440 | tf_op jit(solution)/shard_map/ppermute | solution.py:162
  132.3 8.9 %collective-permute-start.2 = (bf16[128,1024]{0,1:T(8,128)(2,1)S(1)}, bf16[128,1024]{0,1:T(8,128)(2,1)}, u32[]{:S(2)}, u32[]{:S(2)}) collective-permute-start(bf16[128,1024]{0,1:T(8,128)(2,1)S(1)} %fusion.33), channel_id=1, source_target_pairs={{0,2},{2,4},{4,6},{6,0},{1,3},{3,5},{5,7},{7,1},{8,10},{10,12},{12... | collective-permute-start | bytes 786440 | tf_op jit(solution)/shard_map/ppermute | solution.py:161
  134.4 8.1 %collective-permute-start.5 = (bf16[128,1024]{0,1:T(8,128)(2,1)}, bf16[128,1024]{0,1:T(8,128)(2,1)}, u32[]{:S(2)}, u32[]{:S(2)}) collective-permute-start(bf16[128,1024]{0,1:T(8,128)(2,1)} %fusion.30), channel_id=1, source_target_pairs={{0,6},{2,0},{4,2},{6,4},{1,7},{3,1},{5,3},{7,5},{8,14},{10,8},{12,... | collective-permute-start | bytes 786440 | tf_op jit(solution)/shard_map/ppermute | solution.py:162
  142.5 8.1 %collective-permute-start.3 = (bf16[128,1024]{0,1:T(8,128)(2,1)S(1)}, bf16[128,1024]{0,1:T(8,128)(2,1)}, u32[]{:S(2)}, u32[]{:S(2)}) collective-permute-start(bf16[128,1024]{0,1:T(8,128)(2,1)S(1)} %fusion.34), channel_id=1, source_target_pairs={{0,2},{2,4},{4,6},{6,0},{1,3},{3,5},{5,7},{7,1},{8,10},{10,12},{12... | collective-permute-start | bytes 786440 | tf_op jit(solution)/shard_map/ppermute | solution.py:161
  144.3 7.8 %collective-permute-start.6 = (bf16[128,1024]{0,1:T(8,128)(2,1)}, bf16[128,1024]{0,1:T(8,128)(2,1)}, u32[]{:S(2)}, u32[]{:S(2)}) collective-permute-start(bf16[128,1024]{0,1:T(8,128)(2,1)} %fusion.31), channel_id=1, source_target_pairs={{0,6},{2,0},{4,2},{6,4},{1,7},{3,1},{5,3},{7,5},{8,14},{10,8},{12,... | collective-permute-start | bytes 786440 | tf_op jit(solution)/shard_map/ppermute | solution.py:162
Sparse Core Ops, SparseCore 0:
  96.1 30.2 reduce-scatter.4
  139.5 19.8 reduce-scatter.6

commit v10 on v8

--- a/solution.py
+++ b/solution.py
@@ -12,7 +12,8 @@
 UNROLL = 8
 
 
-def _summary_kernel(g_ref, gn_ref, r_ref, drive_ref, up_ref, fa_ref, fb_ref, ba_ref, bb_ref):
+def _summary_kernel(g_ref, gn_ref, r_ref, drive_ref, up_ref, fa_ref, fb_ref, ba_ref, bb_ref,
+                    dec_ref):
     steps, segs, _ = g_ref.shape
     r = r_ref[...]
     ones = jnp.ones(fa_ref.shape, jnp.float32)
@@ -20,18 +21,22 @@
 
     def fwd(i, carry):
         a, b = carry
+        rows = pl.ds(pl.multiple_of(i * segs, segs), segs)
         d = jnp.exp(-(g_ref[i] * r))
-        x = drive_ref[pl.ds(pl.multiple_of(i * segs, segs), segs), :]
+        dec_ref[rows, :] = d
+        x = drive_ref[rows, :]
         return (a * d, d * b + x)
 
     a, b = lax.fori_loop(0, steps, fwd, (ones, zeros), unroll=UNROLL)
     fa_ref[...] = a
     fb_ref[...] = b
 
+    dec_ref[pl.ds(steps * segs, segs), :] = jnp.exp(-(gn_ref[steps - 1] * r))
+
     def bwd(j, carry):
         a, b = carry
         i = steps - 1 - j
-        e = jnp.exp(-(gn_ref[i] * r))
+        e = dec_ref[pl.ds(pl.multiple_of((i + 1) * segs, segs), segs), :]
         u = up_ref[pl.ds(pl.multiple_of(i * segs, segs), segs), :]
         return (a * e, e * b + u)
 
@@ -40,23 +45,27 @@
     bb_ref[...] = b
 
 
-def _sweep_kernel(g_ref, gn_ref, r_ref, if_ref, ib_ref, drive_ref, up_ref, st_ref, adj_ref):
+def _sweep_kernel(g_ref, gn_ref, r_ref, if_ref, ib_ref, drive_ref, up_ref, st_ref, adj_ref,
+                  dec_ref):
     steps, segs, _ = g_ref.shape
     r = r_ref[...]
 
     def fwd(i, b):
         rows = pl.ds(pl.multiple_of(i * segs, segs), segs)
         d = jnp.exp(-(g_ref[i] * r))
+        dec_ref[rows, :] = d
         b = d * b + drive_ref[rows, :]
         st_ref[rows, :] = b
         return b
 
     lax.fori_loop(0, steps, fwd, if_ref[...], unroll=UNROLL)
 
+    dec_ref[pl.ds(steps * segs, segs), :] = jnp.exp(-(gn_ref[steps - 1] * r))
+
     def bwd(j, b):
         i = steps - 1 - j
         rows = pl.ds(pl.multiple_of(i * segs, segs), segs)
-        e = jnp.exp(-(gn_ref[i] * r))
+        e = dec_ref[pl.ds(pl.multiple_of((i + 1) * segs, segs), segs), :]
         b = e * b + up_ref[rows, :]
         adj_ref[rows, :] = b
         return b
@@ -79,12 +88,14 @@
                   _whole(drive.shape), _whole(up.shape)],
         out_specs=[_whole((segs, width))] * 4,
         out_shape=[seg_shape] * 4,
+        scratch_shapes=[pltpu.VMEM((total + segs, width), jnp.float32)],
         compiler_params=pltpu.CompilerParams(vmem_limit_bytes=48 * 1024 * 1024),
     )(g3, gn3, rates2, drive, up)
 
 
 def sweeps(g3, gn3, rates2, drive, up, init_f, init_b):
     total, width = drive.shape
+    segs = g3.shape[1]
     full = jax.ShapeDtypeStruct((total, width), jnp.float32)
     return pl.pallas_call(
         _sweep_kernel,
@@ -94,6 +105,7 @@
                   _whole(drive.shape), _whole(up.shape)],
         out_specs=[_whole(full.shape)] * 2,
         out_shape=[full, full],
+        scratch_shapes=[pltpu.VMEM((total + segs, width), jnp.float32)],
         compiler_params=pltpu.CompilerParams(vmem_limit_bytes=48 * 1024 * 1024),
     )(g3, gn3, rates2, init_f, init_b, drive, up)
 

time: 162 us -> 158 us (0.975)
  Pallas kernels: 23.2 us -> 18.9 us
    pallas_call x1, Pallas kernels: 10.1 us -> 7.76 us  [local_summaries(): pl.pallas_call(_summary_kernel, grid=(1,), in_specs=[_whole(g3.shape), _w...]
    pallas_call x1, Pallas kernels: 13.1 us -> 11.1 us  [sweeps(): pl.pallas_call(_sweep_kernel, grid=(1,), in_specs=[_whole(g3.shape), _who...]
where the time goes in v10:
time: 158 us; the launch traced here: 157 us
  matrix products  33.4 us (21%)
  blocking collectives  25.7 us (16%)
  local copies, waits for them, and re-layouts  22.8 us (14%)
  Pallas kernels  18.9 us (12%)
  waiting for transfers between devices  18.1 us (11%)
  between operations  14.9 us (9%)
  other arithmetic  12.7 us (8%)
  starting transfers between devices  10.6 us (7%)
    all_gather x1, blocking collectives, local(): lax.all_gather(summary, 'sz')  13.2 us
    all_gather x1, blocking collectives, local(): lax.all_gather(lax.all_gather(summary, 'sz'), 'sx').reshape(peers, 3, width)  12.5 us
    pallas_call x1, Pallas kernels, sweeps(): pl.pallas_call(_sweep_kernel, grid=(1,), in_specs=[_whole(g3.shape), _who...  11.1 us
    ppermute x3, waiting for transfers between devices, chan_reduce(): got_a = lax.ppermute(buf_a.astype(jnp.bfloat16), 'cy', up_ring)  10.4 us
    unnamed x19, local copies, waits for them, and re-layouts  8.59 us
    another operation x2, local copies, waits for them, and re-layouts  8.34 us
    ppermute x3, starting transfers between devices, chan_reduce(): got_b = lax.ppermute(buf_b.astype(jnp.bfloat16), 'cy', down_ring)  8.18 us
    dot_general x1, matrix products, local(): lax.dot_general(w_in, drive_grad, (((1,), (1,)), ((), ())), preferred_ele...  7.92 us
  transfers between devices with their start and end apart: 9, of which 6 were waited for; matrix products, arithmetic and copies ran while one was open for 21% of the time, Pallas kernels for 0%

profile of v10, /device:TPU:0, one launch (start us, length us, event | category | flops | bytes accessed | tf_op | source)
XLA Modules:
  0.0 157.1 jit_solution(3693486547963999174)
XLA Ops:
  7.2 0.8 reshape.1244
  8.0 0.8 slice.310
  8.8 1.2 slice.327
  10.0 0.1 copy.33
  10.1 0.1 mul.787
  10.2 0.4 copy.38.g_ref
  10.8 0.4 copy.39.gn_ref
  11.2 7.6 %fusion.2.up_ref = f32[2048,512]{1,0:T(8,128)} fusion(bf16[512,1024]{1,0:T(8,128)(2,1)} %param.10, bf16[256,8,1024]{2,0,1:T(8,128)(2,1)} %bitcast.514), kind=kOutput, calls=%fused_computation.3 | convolution fusion | flops 2147483648 | bytes 9437184 | tf_op jit(solution)/shard_map/dot_general | solution.py:161
  18.8 7.3 %fusion.8.drive_ref = f32[2048,512]{1,0:T(8,128)} fusion(bf16[1024,512]{1,0:T(8,128)(2,1)S(1)} %copy-done, bf16[256,8,1024]{2,0,1:T(8,128)(2,1)S(1)} %bitcast.512, f32[512]{0:T(512)S(1)} %copy-done.1, f32[2048]{0:T(1024)S(1)} %mul.787), kind=kOutput, calls=%fused_computation.11 | convolution fusion | flops 2150629376 | bytes 9447424 | tf_op jit(solution)/shard_map/dot_general | solution.py:160
  26.1 7.8 %shard_map.85 = (f32[8,512]{1,0:T(8,128)S(1)}, f32[8,512]{1,0:T(8,128)S(1)}, f32[8,512]{1,0:T(8,128)S(1)}, f32[8,512]{1,0:T(8,128)S(1)}) custom-call(f32[256,8,1]{2,1,0:T(8,128)S(1)} %copy.38.g_ref, f32[256,8,1]{2,1,0:T(8,128)S(1)} %copy.39.gn_ref, f32[1,512]{1,0:T(1,128)S(1)} %bitcast.503, f32[2048,512]{1,0:T(8,128)} %fusion.8.drive_ref, ...), custom_call_target="tpu_custom_call" | custom-call | tf_op jit(solution)/shard_map/pallas_call | solution.py:84
  34.7 13.2 %all-gather.2 = f32[4,3,512]{2,1,0:T(4,128)S(1)} all-gather(f32[1,3,512]{2,1,0:T(4,128)S(1)} %maximum_bitcast_fusion.1), channel_id=2, replica_groups=mesh['sx'=4,'sz'=4,'cy'=4,'cc'=2] {'sz'}, dimensions={0}, use_global_device_ids=true | all-gather | bytes 30720 | tf_op jit(solution)/shard_map/all_gather | solution.py:182
  47.9 12.5 %all-gather.1 = f32[16,3,512]{2,1,0:T(4,128)S(1)} all-gather(f32[4,3,512]{2,1,0:T(4,128)S(1)} %all-gather.2), channel_id=3, replica_groups=mesh['sx'=4,'sz'=4,'cy'=4,'cc'=2] {'sx'}, dimensions={0}, use_global_device_ids=true | all-gather | bytes 122880 | tf_op jit(solution)/shard_map/all_gather | solution.py:182
  60.6 0.1 multiply_add_fusion.8
  60.7 11.1 %shard_map.86 = (f32[2048,512]{1,0:T(8,128)}, f32[2048,512]{1,0:T(8,128)}) custom-call(f32[256,8,1]{2,1,0:T(8,128)S(1)} %copy.38.g_ref, f32[256,8,1]{2,1,0:T(8,128)S(1)} %copy.39.gn_ref, f32[1,512]{1,0:T(1,128)S(1)} %bitcast.504, f32[8,512]{1,0:T(8,128)S(1)} %stack.10.if_ref, f32[8,512]{1,0:T(8,128)S(1)} %stack.11.ib_ref, f32[2048,512]{1,0:T(8,128)} %fusion.8.drive_ref, ...), custom_call_target="tpu_custom_call" | custom-call | tf_op jit(solution)/shard_map/pallas_call | solution.py:100
  71.9 7.6 %fusion.22 = bf16[1024,512]{0,1:T(8,128)(2,1)S(1)} fusion(bf16[256,8,1024]{2,0,1:T(8,128)(2,1)S(1)} %bitcast.513, f32[2048,512]{1,0:T(8,128)} %get-tuple-element.13, f32[512]{0:T(512)S(1)} %copy-done.1, f32[2048]{0:T(1024)S(1)} %mul.787), kind=kOutput, calls=%fused_computation.21 | convolution fusion | flops 2152726528 | bytes 9447424 | tf_op jit(solution)/shard_map/dot_general | solution.py:208
  79.5 3.0 %fusion.25 = bf16[1024,512]{0,1:T(8,128)(2,1)S(1)} fusion(bf16[256,8,1024]{2,0,1:T(8,128)(2,1)S(1)} %bitcast.515, f32[2048,512]{1,0:T(8,128)S(1)} %copy-done.6), kind=kOutput, calls=%fused_computation.22 | convolution fusion | flops 2149580800 | bytes 9437184 | tf_op jit(solution)/shard_map/dot_general | solution.py:211
  82.5 1.6 pad_maximum_fusion
  84.1 0.3 reduce-scatter.7.cloned.1.call-start
  84.3 7.9 %convolution_convert_fusion = bf16[2048,1024]{0,1:T(8,128)(2,1)} fusion(bf16[1024,512]{1,0:T(8,128)(2,1)S(1)} %copy-done, f32[2048,512]{1,0:T(8,128)} %get-tuple-element.13, f32[512]{0:T(512)S(1)} %copy-done.1, f32[2048]{0:T(1024)S(1)} %mul.787), kind=kOutput, calls=%fused_computation.12 | convolution fusion | flops 2153775104 | bytes 9447424 | tf_op jit(solution)/shard_map/dot_general | solution.py:219
  92.3 4.4 %constant_dynamic-slice_fusion.1 = (bf16[4,1,128,2048]{3,2,1,0:T(8,128)(2,1)S(1)}, bf16[4,1,128,2048]{3,2,1,0:T(8,128)(2,1)}) fusion(bf16[4,2,128,2048]{3,2,1,0:T(8,128)(2,1)} %bitcast.505, s32[]{:T(128)S(6)} %select_n.777, s32[]{:T(128)S(6)} %select_n.779), kind=kLoop, calls=%fused_computation.77 | loop fusion | bytes 8388616 | tf_op jit(solution)/shard_map/dynamic-slice
  96.6 4.0 %copy.41 = bf16[4,1,128,2048]{2,3,0,1:T(8,128)(2,1)} copy(bf16[4,1,128,2048]{3,2,1,0:T(8,128)(2,1)} %get-tuple-element.46) | data formatting | bytes 4194304 | tf_op jit(solution)/shard_map/dynamic-slice.1
  100.6 2.6 %copy.47 = bf16[4,1,128,2048]{2,3,0,1:T(8,128)(2,1)} copy(bf16[4,1,128,2048]{3,2,1,0:T(8,128)(2,1)S(1)} %get-tuple-element.45) | data formatting | bytes 4194304
  103.2 1.9 %collective-permute-done = bf16[4,128,2048]{1,2,0:T(8,128)(2,1)} collective-permute-done((bf16[4,128,2048]{1,2,0:T(8,128)(2,1)}, bf16[4,128,2048]{1,2,0:T(8,128)(2,1)}, u32[]{:S(2)}, u32[]{:S(2)}) %collective-permute-start) | collective-permute-done | bytes 2097184 | tf_op jit(solution)/shard_map/ppermute | solution.py:128
  105.1 2.7 %convert_add_fusion = f32[4,128,2048]{1,2,0:T(8,128)S(1)} fusion(bf16[4,128,2048]{1,2,0:T(8,128)(2,1)} %collective-permute-done, bf16[4,1,128,2048]{2,3,0,1:T(8,128)(2,1)} %copy.47), kind=kLoop, calls=%fused_computation | loop fusion | flops 3145728 | bytes 8388608 | tf_op jit(solution)/shard_map/add | solution.py:128
  107.8 0.3 fusion.70
  108.1 1.3 copy-done.2
  109.4 1.7 %collective-permute-start.1 = (bf16[128,1024]{0,1:T(8,128)(2,1)S(1)}, bf16[128,1024]{0,1:T(8,128)(2,1)}, u32[]{:S(2)}, u32[]{:S(2)}) collective-permute-start(bf16[128,1024]{0,1:T(8,128)(2,1)S(1)} %fusion.36), channel_id=1, source_target_pairs={{0,2},{2,4},{4,6},{6,0},{1,3},{3,5},{5,7},{7,1},{8,10},{10,12},{12... | collective-permute-start | bytes 786440 | tf_op jit(solution)/shard_map/ppermute | solution.py:137
  111.1 0.7 fusion.37
  111.8 1.6 %collective-permute-start.4 = (bf16[128,1024]{0,1:T(8,128)(2,1)}, bf16[128,1024]{0,1:T(8,128)(2,1)}, u32[]{:S(2)}, u32[]{:S(2)}) collective-permute-start(bf16[128,1024]{0,1:T(8,128)(2,1)} %fusion.37), channel_id=1, source_target_pairs={{0,6},{2,0},{4,2},{6,4},{1,7},{3,1},{5,3},{7,5},{8,14},{10,8},{12,... | collective-permute-start | bytes 786440 | tf_op jit(solution)/shard_map/ppermute | solution.py:138
  113.5 5.8 %collective-permute-done.1 = bf16[128,1024]{0,1:T(8,128)(2,1)} collective-permute-done((bf16[128,1024]{0,1:T(8,128)(2,1)S(1)}, bf16[128,1024]{0,1:T(8,128)(2,1)}, u32[]{:S(2)}, u32[]{:S(2)}) %collective-permute-start.1) | collective-permute-done | bytes 262176 | tf_op jit(solution)/shard_map/ppermute | solution.py:137
  119.3 1.2 fusion.33
  120.4 0.4 collective-permute-start.2
  120.8 1.7 %fusion.30 = bf16[128,1024]{0,1:T(8,128)(2,1)} fusion(bf16[128,1024]{0,1:T(8,128)(2,1)} %collective-permute-done.4, f32[4,128,1024]{1,2,0:T(8,128)S(1)} %get-tuple-element.44, s32[]{:T(128)S(6)} %select_n.793), kind=kLoop, calls=%fused_computation.25 | loop fusion | flops 393216 | bytes 1048580 | tf_op jit(solution)/shard_map/convert_element_type | solution.py:138
  122.5 3.0 %collective-permute-start.5 = (bf16[128,1024]{0,1:T(8,128)(2,1)}, bf16[128,1024]{0,1:T(8,128)(2,1)}, u32[]{:S(2)}, u32[]{:S(2)}) collective-permute-start(bf16[128,1024]{0,1:T(8,128)(2,1)} %fusion.30), channel_id=1, source_target_pairs={{0,6},{2,0},{4,2},{6,4},{1,7},{3,1},{5,3},{7,5},{8,14},{10,8},{12,... | collective-permute-start | bytes 786440 | tf_op jit(solution)/shard_map/ppermute | solution.py:138
  125.5 2.0 %copy.45 = bf16[256,1024]{1,0:T(8,128)(2,1)} copy(bf16[256,1024]{0,1:T(8,128)(2,1)} %reduce-scatter.5.cloned.1.call-done) | data formatting | bytes 1048576
  127.5 1.9 %collective-permute-done.2 = bf16[128,1024]{0,1:T(8,128)(2,1)} collective-permute-done((bf16[128,1024]{0,1:T(8,128)(2,1)S(1)}, bf16[128,1024]{0,1:T(8,128)(2,1)}, u32[]{:S(2)}, u32[]{:S(2)}) %collective-permute-start.2) | collective-permute-done | bytes 262176 | tf_op jit(solution)/shard_map/ppermute | solution.py:137
  129.4 1.2 fusion.34
  130.7 1.7 %fusion.31 = bf16[128,1024]{0,1:T(8,128)(2,1)} fusion(bf16[128,1024]{0,1:T(8,128)(2,1)} %collective-permute-done.5, f32[4,128,1024]{1,2,0:T(8,128)S(1)} %get-tuple-element.44, s32[]{:T(128)S(6)} %select_n.791), kind=kLoop, calls=%fused_computation.27 | loop fusion | flops 393216 | bytes 1048580 | tf_op jit(solution)/shard_map/convert_element_type | solution.py:138
  132.4 3.6 %collective-permute-start.6 = (bf16[128,1024]{0,1:T(8,128)(2,1)}, bf16[128,1024]{0,1:T(8,128)(2,1)}, u32[]{:S(2)}, u32[]{:S(2)}) collective-permute-start(bf16[128,1024]{0,1:T(8,128)(2,1)} %fusion.31), channel_id=1, source_target_pairs={{0,6},{2,0},{4,2},{6,4},{1,7},{3,1},{5,3},{7,5},{8,14},{10,8},{12,... | collective-permute-start | bytes 786440 | tf_op jit(solution)/shard_map/ppermute | solution.py:138
  136.0 2.7 %collective-permute-done.3 = bf16[128,1024]{0,1:T(8,128)(2,1)} collective-permute-done((bf16[128,1024]{0,1:T(8,128)(2,1)S(1)}, bf16[128,1024]{0,1:T(8,128)(2,1)}, u32[]{:S(2)}, u32[]{:S(2)}) %collective-permute-start.3) | collective-permute-done | bytes 262176 | tf_op jit(solution)/shard_map/ppermute | solution.py:137
  138.7 1.2 fusion.35
  139.9 0.4 collective-permute-done.6
  140.3 1.0 fusion.32
  141.3 0.9 copy.42
  142.2 5.3 %reduce-scatter.7.cloned.1.call-done = bf16[64,1024]{1,0:T(8,128)(2,1)} async-done(((bf16[256,1024]{1,0:T(8,128)(2,1)}), bf16[64,1024]{1,0:T(8,128)(2,1)}) %reduce-scatter.7.cloned.1.call-update) | async-done | bytes 131088
  147.5 1.1 copy.46
  148.7 0.8 copy.44
  149.5 0.8 copy.43
  (37 shorter events, 0.7 us)
Async XLA Ops:
  7.2 11.7 %copy-start = (bf16[1024,512]{1,0:T(8,128)(2,1)S(1)}, bf16[1024,512]{1,0:T(8,128)(2,1)}, u32[]{:S(2)}) copy-start(bf16[1024,512]{1,0:T(8,128)(2,1)} %param.9) | copy-start | bytes 3145732
  7.2 118.3 %reduce-scatter.5.cloned.1.call-start = ((), (), s32[]{:S(2)}) async-start(), calls=%async_computation.2 | async-start | bytes 2621440 | tf_op jit(solution)/shard_map/reduce_scatter | solution.py:215
  11.2 7.6 %copy-start.1 = (f32[512]{0:T(512)S(1)}, f32[512]{0:T(512)}, u32[]{:S(2)}) copy-start(f32[512]{0:T(512)} %param.8) | copy-start | bytes 6148
  11.2 7.6 %copy-start.3 = (bf16[2048,1024]{1,0:T(8,128)(2,1)S(1)}, bf16[2048,1024]{1,0:T(8,128)(2,1)}, u32[]{:S(2)}) copy-start(bf16[2048,1024]{1,0:T(8,128)(2,1)} %param.6) | copy-start | bytes 12582916
  60.7 11.1 %copy-start.4 = (bf16[2048,1024]{1,0:T(8,128)(2,1)S(1)}, bf16[2048,1024]{1,0:T(8,128)(2,1)}, u32[]{:S(2)}) copy-start(bf16[2048,1024]{1,0:T(8,128)(2,1)} %param.6) | copy-start | bytes 12582916
  71.8 7.6 %copy-start.5 = (bf16[2048,1024]{1,0:T(8,128)(2,1)S(1)}, bf16[2048,1024]{1,0:T(8,128)(2,1)}, u32[]{:S(2)}) copy-start(bf16[2048,1024]{1,0:T(8,128)(2,1)} %param.11) | copy-start | bytes 12582916
  71.8 7.6 %copy-start.6 = (f32[2048,512]{1,0:T(8,128)S(1)}, f32[2048,512]{1,0:T(8,128)}, u32[]{:S(2)}) copy-start(f32[2048,512]{1,0:T(8,128)} %get-tuple-element.14) | copy-start | bytes 12582916
  84.1 63.5 %reduce-scatter.7.cloned.1.call-start = ((), (), s32[]{:S(2)}) async-start(), calls=%async_computation.3 | async-start | bytes 655360
  100.6 4.5 %collective-permute-start = (bf16[4,128,2048]{1,2,0:T(8,128)(2,1)}, bf16[4,128,2048]{1,2,0:T(8,128)(2,1)}, u32[]{:S(2)}, u32[]{:S(2)}) collective-permute-start(bf16[4,128,2048]{1,2,0:T(8,128)(2,1)} %bitcast.506), channel_id=1, source_target_pairs={{0,1},{1,0},{2,3},{3,2},{4,5},{5,4},{6,7},{7,6},{8,9},{9,8},{10,11... | collective-permute-start | bytes 6291464 | tf_op jit(solution)/shard_map/ppermute | solution.py:128
  108.1 1.3 copy-start.2
  109.4 9.8 %collective-permute-start.1 = (bf16[128,1024]{0,1:T(8,128)(2,1)S(1)}, bf16[128,1024]{0,1:T(8,128)(2,1)}, u32[]{:S(2)}, u32[]{:S(2)}) collective-permute-start(bf16[128,1024]{0,1:T(8,128)(2,1)S(1)} %fusion.36), channel_id=1, source_target_pairs={{0,2},{2,4},{4,6},{6,0},{1,3},{3,5},{5,7},{7,1},{8,10},{10,12},{12... | collective-permute-start | bytes 786440 | tf_op jit(solution)/shard_map/ppermute | solution.py:137
  111.8 9.0 %collective-permute-start.4 = (bf16[128,1024]{0,1:T(8,128)(2,1)}, bf16[128,1024]{0,1:T(8,128)(2,1)}, u32[]{:S(2)}, u32[]{:S(2)}) collective-permute-start(bf16[128,1024]{0,1:T(8,128)(2,1)} %fusion.37), channel_id=1, source_target_pairs={{0,6},{2,0},{4,2},{6,4},{1,7},{3,1},{5,3},{7,5},{8,14},{10,8},{12,... | collective-permute-start | bytes 786440 | tf_op jit(solution)/shard_map/ppermute | solution.py:138
  120.4 9.0 %collective-permute-start.2 = (bf16[128,1024]{0,1:T(8,128)(2,1)S(1)}, bf16[128,1024]{0,1:T(8,128)(2,1)}, u32[]{:S(2)}, u32[]{:S(2)}) collective-permute-start(bf16[128,1024]{0,1:T(8,128)(2,1)S(1)} %fusion.33), channel_id=1, source_target_pairs={{0,2},{2,4},{4,6},{6,0},{1,3},{3,5},{5,7},{7,1},{8,10},{10,12},{12... | collective-permute-start | bytes 786440 | tf_op jit(solution)/shard_map/ppermute | solution.py:137
  122.5 8.2 %collective-permute-start.5 = (bf16[128,1024]{0,1:T(8,128)(2,1)}, bf16[128,1024]{0,1:T(8,128)(2,1)}, u32[]{:S(2)}, u32[]{:S(2)}) collective-permute-start(bf16[128,1024]{0,1:T(8,128)(2,1)} %fusion.30), channel_id=1, source_target_pairs={{0,6},{2,0},{4,2},{6,4},{1,7},{3,1},{5,3},{7,5},{8,14},{10,8},{12,... | collective-permute-start | bytes 786440 | tf_op jit(solution)/shard_map/ppermute | solution.py:138
  130.6 8.1 %collective-permute-start.3 = (bf16[128,1024]{0,1:T(8,128)(2,1)S(1)}, bf16[128,1024]{0,1:T(8,128)(2,1)}, u32[]{:S(2)}, u32[]{:S(2)}) collective-permute-start(bf16[128,1024]{0,1:T(8,128)(2,1)S(1)} %fusion.34), channel_id=1, source_target_pairs={{0,2},{2,4},{4,6},{6,0},{1,3},{3,5},{5,7},{7,1},{8,10},{10,12},{12... | collective-permute-start | bytes 786440 | tf_op jit(solution)/shard_map/ppermute | solution.py:137
  132.4 7.9 %collective-permute-start.6 = (bf16[128,1024]{0,1:T(8,128)(2,1)}, bf16[128,1024]{0,1:T(8,128)(2,1)}, u32[]{:S(2)}, u32[]{:S(2)}) collective-permute-start(bf16[128,1024]{0,1:T(8,128)(2,1)} %fusion.31), channel_id=1, source_target_pairs={{0,6},{2,0},{4,2},{6,4},{1,7},{3,1},{5,3},{7,5},{8,14},{10,8},{12,... | collective-permute-start | bytes 786440 | tf_op jit(solution)/shard_map/ppermute | solution.py:138
Sparse Core Ops, SparseCore 0:
  84.2 30.2 reduce-scatter.4
  127.7 19.8 reduce-scatter.6
